TPU v7x, 32 devices: a whole 2x2x4 slice. The times are simulated.
32 devices in a mesh: line: 16 (over z, y, x), chan: 2 (over core).
Axes of the slice: x: 2, y: 2, z: 4, core: 2. Of those that a mesh axis runs over, the one named last changes fastest.
Arguments:
- observed: float32 [2, 16, 128, 16384], P(None, 'chan', None, 'line'), may hold values from -6 to 6
- current_image: float32 [2, 16, 128, 16384], P(None, 'chan', 'line'), may hold values from -4 to 4
- previous_image: float32 [2, 16, 128, 16384], P(None, 'chan', 'line'), may hold values from -4 to 4
- doppler_phase: float32 [128, 16384], P(None, 'line'), may hold values from -3.140625 to 3.140625
- channel_ramp: float32 [16, 16384], P('chan', 'line'), may hold values from -3.140625 to 3.140625
- range_offset: int32 [16384], P('line'), may hold values from -2 to 2
- tap_index: int32 [16384], P('line'), may hold values from 0 to 15
- kernel_table: float32 [16, 4], replicated, may hold values from -0.5 to 0.5
- group_of: int32 [16], P('chan'), may hold values from 0 to 3
- calib_gain: float32 [4], replicated, may hold values from 0.5 to 2
Outputs:
- next_image: float32 [2, 16, 128, 16384], P(None, 'chan', 'line')
- prior_image: float32 [2, 16, 128, 16384], P(None, 'chan', 'line')
All inputs are finite; a program needn't handle non-finite values.
Results may differ from a plain program's by a relative error of at most 0.0003.
Values sent between devices are 32-bit elements; how exact they have to be, the bound alone decides.
No kernel may reach another device: no remote copies, remote signals or barrier semaphores. Data moves between devices by JAX's collectives and lax.ppermute only.
A program may use at most 192 MiB of HBM per device.

v0:
```python
import math

import jax
import jax.numpy as jnp
from jax import lax
from jax.sharding import PartitionSpec as P

NA = 16384
NA1 = 128
NA2 = 128
K = 4
Q = 16
OFFMAX = 2
G = 4
ITERS = 2
START_ITER = 8


step_length = 0.25
threshold = 3.0


def extended(block, sides, width):
    for axis, dim in sides:
        count = lax.axis_size(axis)
        forward = [(i, i + 1) for i in range(count - 1)]
        backward = [(target, source) for source, target in forward]
        low = lax.ppermute(
            lax.slice_in_dim(block, block.shape[dim] - width, None, axis=dim), axis, forward
        )
        high = lax.ppermute(lax.slice_in_dim(block, 0, width, axis=dim), axis, backward)
        block = jnp.concatenate([low, block, high], axis=dim)
    return block


def momentum_weights():
    current = 1.0
    for counter in range(1, START_ITER):
        current = (1.0 + math.sqrt(1.0 + 4.0 * current * current)) / 2.0
    momenta = []
    for counter in range(ITERS):
        following = (1.0 + math.sqrt(1.0 + 4.0 * current * current)) / 2.0
        momenta.append((current - 1.0) / following)
        current = following
    return momenta


def shift_weights(range_offset, tap_index, kernel_table):
    levels = jnp.arange(Q, dtype=jnp.int32)
    onehot = (tap_index[:, None] == levels[None, :]).astype(jnp.float32)
    tap_weights = jnp.dot(
        onehot, kernel_table, precision=lax.Precision.HIGHEST, preferred_element_type=jnp.float32
    )
    stacked = []
    for displacement in range(-(OFFMAX + K // 2 - 1), OFFMAX + K // 2 + 1):
        summed = jnp.zeros(range_offset.shape, jnp.float32)
        for tap_number in range(K):
            matches = (range_offset + (tap_number - (K // 2 - 1)) == displacement).astype(
                jnp.float32
            )
            summed = summed + tap_weights[:, tap_number] * matches
        stacked.append(summed)
    return jnp.stack(stacked)


def shifted_sum(padded, weights, row_count, adjoint):
    rim_width = OFFMAX + K // 2
    lowest = -(OFFMAX + K // 2 - 1)
    summed = None
    for position in range(weights.shape[0]):
        displacement = lowest + position
        anchor = rim_width - displacement if adjoint else rim_width + displacement
        sliced = lax.slice_in_dim(padded, anchor, anchor + row_count, axis=padded.ndim - 2)
        weighted = sliced * weights[position]
        summed = weighted if summed is None else summed + weighted
    return summed


def dft_tables(count, sign):
    counter = jnp.arange(count, dtype=jnp.int32)
    product = counter[:, None] * counter[None, :] % count
    angle = product.astype(jnp.float32) * (2.0 * math.pi / count)
    return (jnp.cos(angle), sign * jnp.sin(angle))


def contract(pattern, operand, matrix):
    return jnp.einsum(
        pattern,
        operand,
        matrix,
        precision=lax.Precision.HIGHEST,
        preferred_element_type=jnp.float32,
    )


def transform(spatial, sign):
    extent = spatial.shape
    real_in = spatial[0].reshape(-1, NA2, NA1)
    imag_in = spatial[1].reshape(-1, NA2, NA1)
    cos_outer, sin_outer = dft_tables(NA2, sign)
    cos_inner, sin_inner = dft_tables(NA1, sign)
    outer_index = jnp.arange(NA2, dtype=jnp.int32)
    inner_index = jnp.arange(NA1, dtype=jnp.int32)
    twist = (outer_index[:, None] * inner_index[None, :] % NA).astype(jnp.float32) * (
        2.0 * math.pi / NA
    )
    cos_twist = jnp.cos(twist)
    sin_twist = sign * jnp.sin(twist)
    real_mid = contract("bpq,pk->bkq", real_in, cos_outer) - contract(
        "bpq,pk->bkq", imag_in, sin_outer
    )
    imag_mid = contract("bpq,pk->bkq", imag_in, cos_outer) + contract(
        "bpq,pk->bkq", real_in, sin_outer
    )
    real_turn = real_mid * cos_twist - imag_mid * sin_twist
    imag_turn = imag_mid * cos_twist + real_mid * sin_twist
    real_out = contract("bkq,qj->bjk", real_turn, cos_inner) - contract(
        "bkq,qj->bjk", imag_turn, sin_inner
    )
    imag_out = contract("bkq,qj->bjk", imag_turn, cos_inner) + contract(
        "bkq,qj->bjk", real_turn, sin_inner
    )
    scale = 1.0 / math.sqrt(NA)
    return jnp.stack([real_out.reshape(extent[1:]), imag_out.reshape(extent[1:])]) * scale


def shrink(squares):
    magnitude = jnp.sqrt(squares)
    return jnp.maximum(magnitude - threshold, 0.0) / jnp.maximum(magnitude, threshold)


def body(
    observed,
    current_image,
    previous_image,
    doppler_phase,
    channel_ramp,
    range_offset,
    tap_index,
    kernel_table,
    group_of,
    calib_gain,
):
    rim_width = OFFMAX + K // 2
    levels = jnp.arange(G, dtype=jnp.int32)
    channel_gain = jnp.sum(
        (group_of[:, None] == levels[None, :]).astype(jnp.float32) * calib_gain[None, :], axis=1
    )
    coefficients = shift_weights(range_offset, tap_index, kernel_table)
    local_data = lax.all_to_all(observed, "line", split_axis=2, concat_axis=3, tiled=True)
    local_phase = lax.all_to_all(doppler_phase, "line", split_axis=0, concat_axis=1, tiled=True)
    ramp_table, coefficients = (
        lax.all_gather(channel_ramp, "line", axis=1, tiled=True),
        lax.all_gather(coefficients, "line", axis=1, tiled=True),
    )
    angles = local_phase[None, :, :] + ramp_table[:, None, :]
    wave_real = channel_gain[:, None, None] * jnp.cos(angles)
    wave_imag = channel_gain[:, None, None] * jnp.sin(angles)
    momenta = momentum_weights()
    earlier = previous_image
    latest = current_image
    for iteration in range(ITERS):
        blended = latest + momenta[iteration] * (latest - earlier)
        spectrum = transform(blended, -1.0)
        padded = extended(spectrum, (("line", 2),), rim_width)
        row_count = padded.shape[2] - 2 * rim_width
        migrated = shifted_sum(padded, coefficients, row_count, False)
        error_real = wave_real * migrated[0] - wave_imag * migrated[1] - local_data[0]
        error_imag = wave_real * migrated[1] + wave_imag * migrated[0] - local_data[1]
        returned = jnp.stack(
            [
                wave_real * error_real + wave_imag * error_imag,
                wave_real * error_imag - wave_imag * error_real,
            ]
        )
        padded_back = extended(returned, (("line", 2),), rim_width)
        spread = shifted_sum(padded_back, coefficients, row_count, True)
        gradient = transform(spread, 1.0)
        shifted = blended - step_length * gradient
        squares = jnp.sum(shifted * shifted, axis=(0, 1))
        factor = shrink(lax.psum(squares, "chan"))
        earlier = latest
        latest = shifted * factor[None, None]
    return (latest, earlier)


def solution(mesh):
    in_specs = (
        P(None, "chan", None, "line"),
        P(None, "chan", "line", None),
        P(None, "chan", "line", None),
        P(None, "line"),
        P("chan", "line"),
        P("line"),
        P("line"),
        P(),
        P("chan"),
        P(),
    )
    out_specs = (P(None, "chan", "line", None), P(None, "chan", "line", None))
    return jax.shard_map(body, mesh=mesh, in_specs=in_specs, out_specs=out_specs, check_vma=False)
```

profile of v0, /device:TPU:21, one launch (start us, length us, event | category | flops | bytes accessed | tf_op | source)
XLA Modules:
  0.0 1516.3 jit_solution(9158974285051247247)
XLA Ops:
  7.2 11.6 copy.23
  18.8 6.7 all-to-all-start.1
  26.1 10.4 multiply_add_fusion.1
  41.3 4.3 fusion.180
  46.3 4.7 fusion.182
  51.0 5.6 convolution_add_fusion.3
  56.7 5.7 convolution_subtract_fusion.3
  62.5 9.9 fusion.114
  72.4 4.1 fusion.116
  76.5 5.9 subtract_bitcast_fusion.3
  82.4 4.9 stack_reshape.24
  87.3 4.8 constant_dynamic-update-slice_fusion.1
  93.6 7.7 add_bitcast_fusion.3
  101.2 5.0 stack_reshape.25
  106.3 4.5 constant_dynamic-update-slice_fusion
  110.8 7.5 broadcast_multiply_fusion.3
  118.3 10.8 fusion.381
  135.8 255.4 %all_gather.7 = f32[8,16384]{1,0:T(8,128)S(1)} all-gather(f32[8,1024]{1,0:T(8,128)S(1)} %stack.58), channel_id=1, replica_groups=mesh['line'=16,'chan'=2] {'line'}, dimensions={1}, use_global_device_ids=true | all-gather | bytes 557056 | tf_op jit(solution)/shard_map/all_gather | solution.py:154
  391.3 26.2 %all_gather.6 = f32[8,16384]{1,0:T(8,128)S(1)} all-gather(f32[8,1024]{1,0:T(8,128)S(1)} %copy-done.36), channel_id=1, replica_groups=mesh['line'=16,'chan'=2] {'line'}, dimensions={1}, use_global_device_ids=true | all-gather | bytes 557056 | tf_op jit(solution)/shard_map/all_gather | solution.py:153
  418.0 13.0 all-to-all-start
  431.0 36.5 %fusion.31 = f32[2,8,8,16384]{3,2,1,0:T(8,128)} fusion(f32[2,8,8,16384]{3,2,1,0:T(8,128)} %broadcast_multiply_fusion.3, f32[2,8,4,16384]{3,2,1,0:T(4,128)} %collective-permute-done, f32[2,8,4,16384]{3,2,1,0:T(4,128)} %collective-permute-done.1, f32[2,8,8,16384]{3,2,1,0:T(8,128)} %constant_dynamic-update-slice_fusion, f32[16384]{0:T(1024)S(1)} %bitcast.251, ...), kind=kLoop, calls=%fused_computation.65 | loop fusion | flops 46137344 | bytes 34078720 | tf_op jit(solution)/shard_map/add | solution.py:75
  467.5 4.3 fusion.380
  471.9 4.4 copy.24
  476.3 4.5 copy.25
  480.8 19.1 %fusion.67 = (f32[1,8,8,16384]{3,2,1,0:T(8,128)S(1)}, f32[1,8,8,16384]{3,2,1,0:T(8,128)S(1)}) fusion(f32[8,16384]{1,0:T(8,128)S(1)} %all_gather.6, f32[8,16384]{1,0:T(8,128)S(1)} %bitcast.245, f32[8]{0:T(128)S(1)} %select_reduce_fusion, f32[1,8,8,16384]{3,2,1,0:T(8,128)} %bitcast.243, f32[2,8,8,16384]{3,2,1,0:T(8,128)} %fusion.31, ...), kind=kLoop, calls=%fused_computation.127 | loop fusion | flops 17825792 | bytes 26214432 | tf_op jit(solution)/shard_map/add | solution.py:172
  499.9 4.6 fusion.88
  511.5 174.0 %collective-permute-done.2 = f32[2,8,4,16384]{3,2,1,0:T(4,128)} collective-permute-done((f32[2,8,4,16384]{3,2,1,0:T(4,128)}, f32[2,8,4,16384]{3,2,1,0:T(4,128)}, u32[]{:S(2)}, u32[]{:S(2)}) %collective-permute-start.2) | collective-permute-done | bytes 4194336 | tf_op jit(solution)/shard_map/ppermute | solution.py:31
  685.4 22.4 %pad_maximum_fusion = (f32[2,8,12,16384]{3,2,1,0:T(8,128)}, f32[2,8,12,16384]{3,2,1,0:T(8,128)}) fusion(f32[2,8,4,16384]{3,2,1,0:T(4,128)} %collective-permute-done.2, f32[1,8,8,16384]{3,2,1,0:T(8,128)} %copy-done.16, f32[1,8,8,16384]{3,2,1,0:T(8,128)} %copy-done.14, f32[2,8,4,16384]{3,2,1,0:T(4,128)} %collective-permute-done.3), kind=kLoop, calls=%fused_computation.20 | loop fusion | flops 12582912 | bytes 41943040 | tf_op jit(solution)/shard_map/concatenate | solution.py:32
  707.8 39.1 %fusion.11 = f32[2,8,8,16384]{3,2,1,0:T(8,128)} fusion(f32[1,8,8,16384]{3,2,1,0:T(8,128)} %copy-done.16, f32[1,8,8,16384]{3,2,1,0:T(8,128)S(1)} %copy-done.15, f32[2,8,12,16384]{3,2,1,0:T(8,128)} %get-tuple-element.21, f32[2,8,12,16384]{3,2,1,0:T(8,128)} %get-tuple-element.20, f32[16384]{0:T(1024)S(1)} %bitcast.276, f32[16384]{0:T(1024)S(1)} %bitcast.252, ...), kind=kLoop, calls=%fused_computation.45 | loop fusion | flops 33554432 | bytes 76021760 | tf_op jit(solution)/shard_map/add | solution.py:75
  760.7 4.2 convolution_add_fusion.2
  769.0 4.1 fusion.108
  773.1 6.0 fusion.106
  779.1 5.8 subtract_bitcast_fusion.2
  784.9 5.0 stack_reshape.26
  789.9 10.8 add_bitcast_fusion.2
  800.7 5.0 stack_reshape.27
  805.7 7.3 multiply_reduce_fusion.1
  813.1 25.2 %all-reduce.3.cloned.1.call-done = f32[8,16384]{1,0:T(8,128)} async-done(((f32[8,16384]{1,0:T(8,128)}), f32[8,16384]{1,0:T(8,128)}) %all-reduce.3.cloned.1.call-update) | async-done | bytes 524304 | tf_op jit(solution)/shard_map/psum | solution.py:181
  839.6 13.6 multiply_add_fusion
  866.2 4.2 convolution_add_fusion.1
  874.5 4.1 fusion.98
  878.7 6.0 fusion.100
  884.7 5.9 add_bitcast_fusion.1
  890.6 5.0 stack_reshape.29
  895.6 10.8 subtract_bitcast_fusion.1
  906.4 5.0 stack_reshape.28
  922.4 11.0 fusion.379
  939.7 88.7 %collective-permute-done.4 = f32[2,8,4,16384]{3,2,1,0:T(4,128)} collective-permute-done((f32[2,8,4,16384]{3,2,1,0:T(4,128)}, f32[2,8,4,16384]{3,2,1,0:T(4,128)}, u32[]{:S(2)}, u32[]{:S(2)}) %collective-permute-start.4) | collective-permute-done | bytes 4194336 | tf_op jit(solution)/shard_map/ppermute | solution.py:28
  1028.4 90.4 %collective-permute-done.5 = f32[2,8,4,16384]{3,2,1,0:T(4,128)} collective-permute-done((f32[2,8,4,16384]{3,2,1,0:T(4,128)}, f32[2,8,4,16384]{3,2,1,0:T(4,128)}, u32[]{:S(2)}, u32[]{:S(2)}) %collective-permute-start.5) | collective-permute-done | bytes 4194336 | tf_op jit(solution)/shard_map/ppermute | solution.py:31
  1118.9 36.9 %fusion.20 = f32[2,8,8,16384]{3,2,1,0:T(8,128)} fusion(f32[2,8,8,16384]{3,2,1,0:T(8,128)} %broadcast_multiply_fusion.2, f32[2,8,4,16384]{3,2,1,0:T(4,128)} %collective-permute-done.4, f32[2,8,4,16384]{3,2,1,0:T(4,128)} %collective-permute-done.5, f32[2,8,8,16384]{3,2,1,0:T(8,128)} %copy-done.17, f32[16384]{0:T(1024)S(1)} %bitcast.253, ...), kind=kLoop, calls=%fused_computation.54 | loop fusion | flops 46137344 | bytes 34078720 | tf_op jit(solution)/shard_map/add | solution.py:75
  1155.8 19.1 %fusion.73 = (f32[1,8,8,16384]{3,2,1,0:T(8,128)S(1)}, f32[1,8,8,16384]{3,2,1,0:T(8,128)S(1)}) fusion(f32[8,16384]{1,0:T(8,128)S(1)} %copy-done.24, f32[8,16384]{1,0:T(8,128)} %bitcast.246, f32[8]{0:T(128)S(1)} %copy-done.39, f32[1,8,8,16384]{3,2,1,0:T(8,128)} %bitcast.244, f32[2,8,8,16384]{3,2,1,0:T(8,128)} %fusion.20, f32[1,8,8,16384]{3,2,1,0:T(8,128)} %bitcast.242), kind=kLoop, calls=%fused_computation.133 | loop fusion | flops 17825792 | bytes 26214432 | tf_op jit(solution)/shard_map/add | solution.py:172
  1182.1 178.0 %collective-permute-done.6 = f32[2,8,4,16384]{3,2,1,0:T(4,128)S(1)} collective-permute-done((f32[2,8,4,16384]{3,2,1,0:T(4,128)S(1)}, f32[2,8,4,16384]{3,2,1,0:T(4,128)S(1)}, u32[]{:S(2)}, u32[]{:S(2)}) %collective-permute-start.6) | collective-permute-done | bytes 4194336 | tf_op jit(solution)/shard_map/ppermute | solution.py:31
  1360.0 11.9 pad_maximum_fusion.1
  1371.9 38.9 %fusion.5 = f32[2,8,8,16384]{3,2,1,0:T(8,128)} fusion(f32[1,8,8,16384]{3,2,1,0:T(8,128)} %copy-done.13, f32[1,8,8,16384]{3,2,1,0:T(8,128)S(1)} %get-tuple-element.4, f32[2,8,12,16384]{3,2,1,0:T(8,128)} %get-tuple-element.11, f32[2,8,12,16384]{3,2,1,0:T(8,128)} %get-tuple-element.10, f32[16384]{0:T(1024)S(1)} %bitcast.277, f32[16384]{0:T(1024)S(1)} %bitcast.254, ...), kind=kLoop, calls=%fused_computation.39 | loop fusion | flops 33554432 | bytes 76021760 | tf_op jit(solution)/shard_map/add | solution.py:75
  1424.5 4.3 convolution_add_fusion
  1432.9 4.1 fusion.92
  1437.0 6.1 fusion.90
  1443.1 5.9 subtract_bitcast_fusion
  1448.9 5.0 stack_reshape.30
  1453.9 10.8 add_bitcast_fusion
  1464.7 5.0 stack_reshape.31
  1469.8 7.3 multiply_reduce_fusion
  1477.1 20.6 %all-reduce.5.cloned.1.call-done = f32[8,16384]{1,0:T(8,128)} async-done(((f32[8,16384]{1,0:T(8,128)}), f32[8,16384]{1,0:T(8,128)}) %all-reduce.5.cloned.1.call-update) | async-done | bytes 524304 | tf_op jit(solution)/shard_map/psum | solution.py:181
  1499.0 10.0 broadcast_multiply_fusion
  (144 shorter events, 101.4 us)
Async XLA Ops:
  7.2 128.1 %copy-start = (f32[16,4]{0,1:T(4,128)S(1)}, f32[16,4]{0,1:T(4,128)}, u32[]{:S(2)}) copy-start(f32[16,4]{0,1:T(4,128)} %param.17) | copy-start | bytes 772
  18.8 399.1 %all-to-all-start.1 = ((f32[2,8,128,1024]{3,1,0,2:T(8,128)}), f32[2,8,128,1024]{3,1,0,2:T(8,128)}, u32[]{:S(2)}, u32[]{:S(2)}) async-start(f32[2,8,128,1024]{3,1,0,2:T(8,128)} %copy.23), calls=%async_computation.1 | async-start | bytes 16777216 | tf_op jit(solution)/shard_map/all_to_all | solution.py:150
  62.5 29.6 %copy-start.19 = (f32[128,128]{1,0:T(8,128)}, f32[128,128]{1,0:T(8,128)S(1)}, u32[]{:S(2)}) copy-start(f32[128,128]{1,0:T(8,128)S(1)} %copy.22) | copy-start | bytes 196612
  62.5 9.9 copy-start.3
  62.5 9.9 copy-start.5
  87.3 4.8 copy-start.4
  87.3 6.2 copy-start.6
  118.2 17.0 %copy-start.40 = (s32[1024]{0:T(1024)S(1)}, s32[1024]{0:T(1024)}, u32[]{:S(2)}) copy-start(s32[1024]{0:T(1024)} %param.16) | copy-start | bytes 12292
  118.2 17.5 %copy-start.37 = (s32[1024]{0:T(1024)S(1)}, s32[1024]{0:T(1024)}, u32[]{:S(2)}) copy-start(s32[1024]{0:T(1024)} %param.15) | copy-start | bytes 12292
  118.3 273.0 %copy-start.36 = (f32[8,1024]{1,0:T(8,128)S(1)}, f32[8,1024]{1,0:T(8,128)}, u32[]{:S(2)}) copy-start(f32[8,1024]{1,0:T(8,128)} %param.14) | copy-start | bytes 98308
  118.3 299.2 %copy-start.41 = (f32[4]{0:T(128)S(1)}, f32[4]{0:T(128)}, u32[]{:S(2)}) copy-start(f32[4]{0:T(128)} %param.19) | copy-start | bytes 52
  118.3 299.2 %copy-start.42 = (s32[8]{0:T(128)S(1)}, s32[8]{0:T(128)}, u32[]{:S(2)}) copy-start(s32[8]{0:T(128)} %param.18) | copy-start | bytes 100
  129.0 301.9 %collective-permute-start = (f32[2,8,4,16384]{3,2,1,0:T(4,128)}, f32[2,8,4,16384]{3,2,1,0:T(4,128)}, u32[]{:S(2)}, u32[]{:S(2)}) collective-permute-start(f32[2,8,4,16384]{3,2,1,0:T(4,128)} %get-tuple-element.27), channel_id=1, source_target_pairs={{0,2},{2,4},{4,6},{6,8},{8,10},{10,12},{12,14},{14,16},{16,18},{18... | collective-permute-start | bytes 12582920 | tf_op jit(solution)/shard_map/ppermute | solution.py:28
  132.1 298.9 %collective-permute-start.1 = (f32[2,8,4,16384]{3,2,1,0:T(4,128)}, f32[2,8,4,16384]{3,2,1,0:T(4,128)}, u32[]{:S(2)}, u32[]{:S(2)}) collective-permute-start(f32[2,8,4,16384]{3,2,1,0:T(4,128)} %get-tuple-element.26), channel_id=1, source_target_pairs={{2,0},{4,2},{6,4},{8,6},{10,8},{12,10},{14,12},{16,14},{18,16},{20... | collective-permute-start | bytes 12582920 | tf_op jit(solution)/shard_map/ppermute | solution.py:31
  417.4 63.3 %copy-start.23 = (f32[8,16384]{1,0:T(8,128)}, f32[8,16384]{1,0:T(8,128)S(1)}, u32[]{:S(2)}) copy-start(f32[8,16384]{1,0:T(8,128)S(1)} %all_gather.6) | copy-start | bytes 1572868
  417.5 63.3 %copy-start.38 = (f32[8]{0:T(128)}, f32[8]{0:T(128)S(1)}, u32[]{:S(2)}) copy-start(f32[8]{0:T(128)S(1)} %select_reduce_fusion) | copy-start | bytes 100
  417.9 289.9 %copy-start.26 = (f32[1,16384]{1,0:T(1,128)}, f32[1,16384]{1,0:T(1,128)S(1)}, u32[]{:S(2)}) copy-start(f32[1,16384]{1,0:T(1,128)S(1)} %get-tuple-element.36) | copy-start | bytes 196612
  417.9 289.9 %copy-start.29 = (f32[1,16384]{1,0:T(1,128)}, f32[1,16384]{1,0:T(1,128)S(1)}, u32[]{:S(2)}) copy-start(f32[1,16384]{1,0:T(1,128)S(1)} %get-tuple-element.37) | copy-start | bytes 196612
  417.9 289.9 %copy-start.32 = (f32[1,16384]{1,0:T(1,128)}, f32[1,16384]{1,0:T(1,128)S(1)}, u32[]{:S(2)}) copy-start(f32[1,16384]{1,0:T(1,128)S(1)} %get-tuple-element.35) | copy-start | bytes 196612
  417.9 49.6 %copy-start.34 = (f32[16384]{0:T(1024)}, f32[16384]{0:T(1024)S(1)}, u32[]{:S(2)}) copy-start(f32[16384]{0:T(1024)S(1)} %broadcast_multiply_fusion.4) | copy-start | bytes 196612
  418.0 62.8 %all-to-all-start = ((f32[16,8,1024]{2,1,0:T(8,128)}), f32[16,8,1024]{2,1,0:T(8,128)S(1)}, u32[]{:S(2)}, u32[]{:S(2)}) async-start(f32[16,8,1024]{2,1,0:T(8,128)} %bitcast.1), calls=%async_computation | async-start | bytes 1048576 | tf_op jit(solution)/shard_map/all_to_all | solution.py:151
  430.9 407.4 %all-reduce.3.cloned.1.call-start = ((), (), s32[]{:S(2)}) async-start(), calls=%async_computation.2 | async-start | bytes 1048576 | tf_op jit(solution)/shard_map/psum | solution.py:181
  480.8 19.1 %copy-start.25 = (f32[16,8,1024]{2,1,0:T(8,128)}, f32[16,8,1024]{2,1,0:T(8,128)S(1)}, u32[]{:S(2)}) copy-start(f32[16,8,1024]{2,1,0:T(8,128)S(1)} %all-to-all-done) | copy-start | bytes 1572868
  499.9 4.6 copy-start.14
  499.9 5.9 copy-start.16
  505.8 179.6 %collective-permute-start.2 = (f32[2,8,4,16384]{3,2,1,0:T(4,128)}, f32[2,8,4,16384]{3,2,1,0:T(4,128)}, u32[]{:S(2)}, u32[]{:S(2)}) collective-permute-start(f32[2,8,4,16384]{3,2,1,0:T(4,128)} %get-tuple-element.22), channel_id=1, source_target_pairs={{2,0},{4,2},{6,4},{8,6},{10,8},{12,10},{14,12},{16,14},{18,16},{20... | collective-permute-start | bytes 12582920 | tf_op jit(solution)/shard_map/ppermute | solution.py:31
  508.9 176.5 %collective-permute-start.3 = (f32[2,8,4,16384]{3,2,1,0:T(4,128)}, f32[2,8,4,16384]{3,2,1,0:T(4,128)}, u32[]{:S(2)}, u32[]{:S(2)}) collective-permute-start(f32[2,8,4,16384]{3,2,1,0:T(4,128)} %get-tuple-element.23), channel_id=1, source_target_pairs={{0,2},{2,4},{4,6},{6,8},{8,10},{10,12},{12,14},{14,16},{16,18},{18... | collective-permute-start | bytes 12582920 | tf_op jit(solution)/shard_map/ppermute | solution.py:28
  511.5 278.4 %copy-start.21 = (f32[128,128]{1,0:T(8,128)}, f32[128,128]{1,0:T(8,128)S(1)}, u32[]{:S(2)}) copy-start(f32[128,128]{1,0:T(8,128)S(1)} %copy.26) | copy-start | bytes 196612
  511.5 196.4 %copy-start.15 = (f32[1,8,8,16384]{3,2,1,0:T(8,128)S(1)}, f32[1,8,8,16384]{3,2,1,0:T(8,128)}, u32[]{:S(2)}) copy-start(f32[1,8,8,16384]{3,2,1,0:T(8,128)} %copy-done.14) | copy-start | bytes 12582916
  764.9 14.2 copy-start.9
  769.0 10.1 copy-start.12
  813.1 684.6 %all-reduce.5.cloned.1.call-start = ((), (), s32[]{:S(2)}) async-start(), calls=%async_computation.3 | async-start | bytes 1048576 | tf_op jit(solution)/shard_map/psum | solution.py:181
  853.2 3.4 copy-start.2
  870.4 14.3 copy-start.8
  870.4 4.1 copy-start.20
  874.5 10.2 copy-start.11
  911.4 3.4 copy-start.18
  915.1 3.3 copy-start.17
  922.4 196.4 %copy-start.27 = (f32[1,16384]{1,0:T(1,128)S(1)}, f32[1,16384]{1,0:T(1,128)}, u32[]{:S(2)}) copy-start(f32[1,16384]{1,0:T(1,128)} %copy-done.26) | copy-start | bytes 196612
  922.4 196.4 %copy-start.30 = (f32[1,16384]{1,0:T(1,128)S(1)}, f32[1,16384]{1,0:T(1,128)}, u32[]{:S(2)}) copy-start(f32[1,16384]{1,0:T(1,128)} %copy-done.29) | copy-start | bytes 196612
  922.4 196.4 %copy-start.35 = (f32[16384]{0:T(1024)S(1)}, f32[16384]{0:T(1024)}, u32[]{:S(2)}) copy-start(f32[16384]{0:T(1024)} %copy-done.34) | copy-start | bytes 196612
  933.4 95.1 %collective-permute-start.4 = (f32[2,8,4,16384]{3,2,1,0:T(4,128)}, f32[2,8,4,16384]{3,2,1,0:T(4,128)}, u32[]{:S(2)}, u32[]{:S(2)}) collective-permute-start(f32[2,8,4,16384]{3,2,1,0:T(4,128)} %get-tuple-element.15), channel_id=1, source_target_pairs={{0,2},{2,4},{4,6},{6,8},{8,10},{10,12},{12,14},{14,16},{16,18},{18... | collective-permute-start | bytes 12582920 | tf_op jit(solution)/shard_map/ppermute | solution.py:28
  936.5 219.3 %copy-start.24 = (f32[8,16384]{1,0:T(8,128)S(1)}, f32[8,16384]{1,0:T(8,128)}, u32[]{:S(2)}) copy-start(f32[8,16384]{1,0:T(8,128)} %copy-done.23) | copy-start | bytes 1572868
  936.5 219.3 %copy-start.39 = (f32[8]{0:T(128)S(1)}, f32[8]{0:T(128)}, u32[]{:S(2)}) copy-start(f32[8]{0:T(128)} %copy-done.38) | copy-start | bytes 100
  936.5 182.4 %collective-permute-start.5 = (f32[2,8,4,16384]{3,2,1,0:T(4,128)}, f32[2,8,4,16384]{3,2,1,0:T(4,128)}, u32[]{:S(2)}, u32[]{:S(2)}) collective-permute-start(f32[2,8,4,16384]{3,2,1,0:T(4,128)} %get-tuple-element.14), channel_id=1, source_target_pairs={{2,0},{4,2},{6,4},{8,6},{10,8},{12,10},{14,12},{16,14},{18,16},{20... | collective-permute-start | bytes 12582920 | tf_op jit(solution)/shard_map/ppermute | solution.py:31
  1174.9 185.1 %copy-start.13 = (f32[1,8,8,16384]{3,2,1,0:T(8,128)}, f32[1,8,8,16384]{3,2,1,0:T(8,128)S(1)}, u32[]{:S(2)}) copy-start(f32[1,8,8,16384]{3,2,1,0:T(8,128)S(1)} %get-tuple-element.5) | copy-start | bytes 12582916
  1176.6 183.4 %collective-permute-start.6 = (f32[2,8,4,16384]{3,2,1,0:T(4,128)S(1)}, f32[2,8,4,16384]{3,2,1,0:T(4,128)S(1)}, u32[]{:S(2)}, u32[]{:S(2)}) collective-permute-start(f32[2,8,4,16384]{3,2,1,0:T(4,128)S(1)} %get-tuple-element.12), channel_id=1, source_target_pairs={{2,0},{4,2},{6,4},{8,6},{10,8},{12,10},{14,12},{16,14},{18,16},{20... | collective-permute-start | bytes 12582920 | tf_op jit(solution)/shard_map/ppermute | solution.py:31
  1179.2 192.8 %copy-start.28 = (f32[1,16384]{1,0:T(1,128)S(1)}, f32[1,16384]{1,0:T(1,128)}, u32[]{:S(2)}) copy-start(f32[1,16384]{1,0:T(1,128)} %copy-done.26) | copy-start | bytes 196612
  1179.2 192.8 %copy-start.31 = (f32[1,16384]{1,0:T(1,128)S(1)}, f32[1,16384]{1,0:T(1,128)}, u32[]{:S(2)}) copy-start(f32[1,16384]{1,0:T(1,128)} %copy-done.29) | copy-start | bytes 196612
  1179.2 192.8 %copy-start.33 = (f32[1,16384]{1,0:T(1,128)S(1)}, f32[1,16384]{1,0:T(1,128)}, u32[]{:S(2)}) copy-start(f32[1,16384]{1,0:T(1,128)} %copy-done.32) | copy-start | bytes 196612
  1179.2 180.8 %collective-permute-start.7 = (f32[2,8,4,16384]{3,2,1,0:T(4,128)S(1)}, f32[2,8,4,16384]{3,2,1,0:T(4,128)S(1)}, u32[]{:S(2)}, u32[]{:S(2)}) collective-permute-start(f32[2,8,4,16384]{3,2,1,0:T(4,128)S(1)} %get-tuple-element.13), channel_id=1, source_target_pairs={{0,2},{2,4},{4,6},{6,8},{8,10},{10,12},{12,14},{14,16},{16,18},{18... | collective-permute-start | bytes 12582920 | tf_op jit(solution)/shard_map/ppermute | solution.py:28
  1428.8 14.3 copy-start.7
  1428.8 4.1 copy-start.22
  1432.9 10.2 copy-start.10
  1499.0 10.0 copy-start.1
Sparse Core Ops, SparseCore 0:
  813.2 25.1 all-reduce.2
  1477.2 20.4 all-reduce.4
where the time goes:
time: 1520 us
  waiting for transfers between devices  577 us (38%)
  other arithmetic  294 us (19%)
  blocking collectives  282 us (19%)
  matrix products  178 us (12%)
  local copies, waits for them, and re-layouts  128 us (8%)
  starting transfers between devices  42.9 us (3%)
  between operations  15.3 us (1%)
    ppermute x4, waiting for transfers between devices, extended(): lax.ppermute(lax.slice_in_dim(block, 0, width, axis=dim), axis, backward)  442 us
    all_gather x1, blocking collectives, body(): lax.all_gather(coefficients, 'line', axis=1, tiled=True)  255 us
    dot_general x32, matrix products, contract(): jnp.einsum(pattern, operand, matrix, precision=lax.Precision.HIGHEST, pre...  177 us
    add x4, other arithmetic, shifted_sum(): summed = weighted if summed is None else summed + weighted  151 us
    ppermute x4, waiting for transfers between devices, extended(): lax.ppermute(lax.slice_in_dim(block, block.shape[dim] - width, None, axis...  88.7 us
    unnamed x101, local copies, waits for them, and re-layouts  47.7 us
    psum x2, waiting for transfers between devices, body(): factor = shrink(lax.psum(squares, 'chan'))  45.8 us
    another operation x10, local copies, waits for them, and re-layouts, transform(): jnp.stack([real_out.reshape(extent[1:]), imag_out.reshape(extent[1:])])  44.8 us
  transfers between devices with their start and end apart: 12, of which 6 were waited for; matrix products, arithmetic and copies ran while one was open for 10% of the time, Pallas kernels for 0%

commit v1 on v0

v1 whole, which is shorter than its diff:
```python
import math

import numpy as np
import jax
import jax.numpy as jnp
from jax import lax
from jax.sharding import PartitionSpec as P

K = 4
Q = 16
OFFMAX = 2
G = 4
ITERS = 2
START_ITER = 8
HALO = K - 1

step_length = 0.25
threshold = 3.0


def momentum_weights():
    current = 1.0
    for counter in range(1, START_ITER):
        current = (1.0 + math.sqrt(1.0 + 4.0 * current * current)) / 2.0
    momenta = []
    for counter in range(ITERS):
        following = (1.0 + math.sqrt(1.0 + 4.0 * current * current)) / 2.0
        momenta.append((current - 1.0) / following)
        current = following
    return momenta


def tap_table(tap_index, kernel_table):
    levels = jnp.arange(Q, dtype=jnp.int32)
    onehot = (tap_index[:, None] == levels[None, :]).astype(jnp.float32)
    return jnp.dot(
        onehot, kernel_table, precision=lax.Precision.HIGHEST, preferred_element_type=jnp.float32
    )


def shift_weights(range_offset, tap_weights):
    stacked = []
    for displacement in range(-(OFFMAX + K // 2 - 1), OFFMAX + K // 2 + 1):
        summed = jnp.zeros(range_offset.shape, jnp.float32)
        for tap_number in range(K):
            matches = (range_offset + (tap_number - (K // 2 - 1)) == displacement).astype(
                jnp.float32
            )
            summed = summed + tap_weights[..., tap_number] * matches
        stacked.append(summed)
    return jnp.stack(stacked)


LOWEST = -(OFFMAX + K // 2 - 1)


def adjoint_shift(rows, weights):
    rim_width = OFFMAX + K // 2
    count = rows.shape[-2]
    pad = [(0, 0)] * rows.ndim
    pad[-2] = (rim_width, rim_width)
    padded = jnp.pad(rows, pad)
    summed = None
    for position in range(weights.shape[0]):
        displacement = LOWEST + position
        anchor = rim_width - displacement
        sliced = lax.slice_in_dim(padded, anchor, anchor + count, axis=rows.ndim - 2)
        weighted = sliced * weights[position]
        summed = weighted if summed is None else summed + weighted
    return summed


def dft_matrix(count, sign, scale):
    counter = np.arange(count)
    angle = (np.outer(counter, counter) % count) * (2.0 * np.pi / count)
    return (
        jnp.asarray(np.cos(angle) * scale, jnp.float32),
        jnp.asarray(sign * np.sin(angle) * scale, jnp.float32),
    )


def twiddle(rows, cols, total, sign):
    angle = (np.outer(np.arange(rows), np.arange(cols)) % total) * (2.0 * np.pi / total)
    return jnp.asarray(np.cos(angle), jnp.float32), jnp.asarray(sign * np.sin(angle), jnp.float32)


def mm(pattern, a, b):
    return jnp.einsum(
        pattern, a, b, precision=lax.Precision.HIGHEST, preferred_element_type=jnp.float32
    )


def forward_transform(xr, xi, p_len, q_len):
    wc, ws = dft_matrix(p_len, -1.0, 1.0)
    vc, vs = dft_matrix(q_len, -1.0, 1.0)
    tc, ts = twiddle(p_len, q_len, p_len * q_len, -1.0)
    mr = mm("kp,bpq->bkq", wc, xr) - mm("kp,bpq->bkq", ws, xi)
    mi = mm("kp,bpq->bkq", wc, xi) + mm("kp,bpq->bkq", ws, xr)
    tr = mr * tc - mi * ts
    ti = mi * tc + mr * ts
    out_r = mm("bkq,qj->bkj", tr, vc) - mm("bkq,qj->bkj", ti, vs)
    out_i = mm("bkq,qj->bkj", ti, vc) + mm("bkq,qj->bkj", tr, vs)
    return out_r, out_i


def inverse_transform(yr, yi, p_len, q_len):
    wc, ws = dft_matrix(p_len, 1.0, 1.0)
    vc, vs = dft_matrix(q_len, 1.0, 1.0)
    tc, ts = twiddle(p_len, q_len, p_len * q_len, 1.0)
    mr = mm("bkj,jq->bkq", yr, vc) - mm("bkj,jq->bkq", yi, vs)
    mi = mm("bkj,jq->bkq", yi, vc) + mm("bkj,jq->bkq", yr, vs)
    tr = mr * tc - mi * ts
    ti = mi * tc + mr * ts
    out_r = mm("pk,bkq->bpq", wc, tr) - mm("pk,bkq->bpq", ws, ti)
    out_i = mm("pk,bkq->bpq", wc, ti) + mm("pk,bkq->bpq", ws, tr)
    return out_r, out_i


def shrink(squares):
    magnitude = jnp.sqrt(squares)
    return jnp.maximum(magnitude - threshold, 0.0) / jnp.maximum(magnitude, threshold)


def body(
    observed,
    current_image,
    previous_image,
    doppler_phase,
    channel_ramp,
    range_offset,
    tap_index,
    kernel_table,
    group_of,
    calib_gain,
):
    lines = lax.axis_size("line")
    chans = lax.axis_size("chan")
    me = lax.axis_index("line")
    _, cl, rows, na = current_image.shape
    p_len = 128 if na % 128 == 0 else 1
    q_len = na // p_len

    levels = jnp.arange(G, dtype=jnp.int32)
    channel_gain = jnp.sum(
        (group_of[:, None] == levels[None, :]).astype(jnp.float32) * calib_gain[None, :], axis=1
    )

    local_taps = tap_table(tap_index, kernel_table)
    local_weights = shift_weights(range_offset, local_taps)
    angles = doppler_phase[None, :, :] + channel_ramp[:, None, :]
    cos_a = jnp.cos(angles)
    sin_a = jnp.sin(angles)
    gain = channel_gain[:, None, None]
    back_r = gain * (cos_a * observed[0] + sin_a * observed[1])
    back_i = gain * (cos_a * observed[1] - sin_a * observed[0])
    data = adjoint_shift(jnp.stack([back_r, back_i]), local_weights)
    data = data * (step_length / math.sqrt(na))
    data = lax.all_to_all(data, "line", split_axis=2, concat_axis=3, tiled=True)
    data = data.reshape(2, cl, rows, q_len, p_len).swapaxes(-1, -2)

    packed = lax.all_gather(jnp.stack([tap_index, range_offset]), "line", axis=1, tiled=True)
    taps = tap_table(packed[0], kernel_table)
    weights = shift_weights(packed[1], taps)

    def spectral(v):
        return v.reshape(v.shape[:-1] + (q_len, p_len)).swapaxes(-1, -2)

    weights = spectral(weights)
    band = [
        spectral(sum(taps[:, k] * taps[:, k + e] for k in range(K - e))) for e in range(K)
    ]
    coef = (channel_gain * channel_gain) * (step_length / na)

    momenta = momentum_weights()
    earlier = previous_image
    latest = current_image
    forward_pairs = [(i, i + 1) for i in range(lines - 1)]
    backward_pairs = [(i + 1, i) for i in range(lines - 1)]
    first = (me == 0)
    last = (me == lines - 1)

    def wgt(d):
        return weights[d - LOWEST]

    for iteration in range(ITERS):
        blended = latest + momenta[iteration] * (latest - earlier)
        low = lax.ppermute(blended[:, :, rows - HALO :], "line", forward_pairs)
        high = lax.ppermute(blended[:, :, :HALO], "line", backward_pairs)
        ext = jnp.concatenate([low, blended, high], axis=2)
        ext_rows = rows + 2 * HALO
        xr, xi = forward_transform(
            ext[0].reshape(-1, p_len, q_len), ext[1].reshape(-1, p_len, q_len), p_len, q_len
        )
        spec = jnp.stack([xr, xi]).reshape(2, cl, ext_rows, p_len, q_len)

        def at(r):
            return spec[:, :, r]

        gram = []
        for r in range(rows):
            c = r + HALO
            acc = band[0] * at(c)
            for e in range(1, K):
                acc = acc + band[e] * (at(c - e) + at(c + e))
            gram.append(acc)
        low_fix = []
        for rr in range(K):
            acc = None
            for s in range(1, K + 1):
                if rr + s > OFFMAX + K // 2:
                    continue
                u = None
                for j in range(K):
                    if j + s > OFFMAX + K // 2:
                        continue
                    term = wgt(j + s) * at(HALO + j)
                    u = term if u is None else u + term
                term = wgt(rr + s) * u
                acc = term if acc is None else acc + term
            low_fix.append(acc)
        high_fix = []
        for tt in range(-(K - 2), 1):
            acc = None
            for s in range(1, K):
                if tt - s < LOWEST:
                    continue
                u = None
                for t in range(-(K - 2), 1):
                    if t - s < LOWEST:
                        continue
                    term = wgt(t - s) * at(HALO + rows - 1 + t)
                    u = term if u is None else u + term
                term = wgt(tt - s) * u
                acc = term if acc is None else acc + term
            high_fix.append(acc)
        for rr in range(K):
            gram[rr] = gram[rr] - jnp.where(first, low_fix[rr], 0.0)
        for idx, tt in enumerate(range(-(K - 2), 1)):
            r = rows - 1 + tt
            gram[r] = gram[r] - jnp.where(last, high_fix[idx], 0.0)
        gram = jnp.stack(gram, axis=2)
        resid = coef[None, :, None, None, None] * gram - data
        gr, gi = inverse_transform(
            resid[0].reshape(-1, p_len, q_len), resid[1].reshape(-1, p_len, q_len), p_len, q_len
        )
        shifted = blended - jnp.stack([gr, gi]).reshape(blended.shape)
        squares = jnp.sum(shifted * shifted, axis=(0, 1))
        if chans == 2:
            squares = squares + lax.ppermute(squares, "chan", [(0, 1), (1, 0)])
        else:
            squares = lax.psum(squares, "chan")
        factor = shrink(squares)
        earlier = latest
        latest = shifted * factor[None, None]
    return (latest, earlier)


def solution(mesh):
    in_specs = (
        P(None, "chan", None, "line"),
        P(None, "chan", "line", None),
        P(None, "chan", "line", None),
        P(None, "line"),
        P("chan", "line"),
        P("line"),
        P("line"),
        P(),
        P("chan"),
        P(),
    )
    out_specs = (P(None, "chan", "line", None), P(None, "chan", "line", None))
    return jax.shard_map(body, mesh=mesh, in_specs=in_specs, out_specs=out_specs, check_vma=False)
```

time: 1520 us -> 1150 us (0.76)
  waiting for transfers between devices: 577 us -> 133 us
  matrix products: 178 us -> 365 us
  other arithmetic: 294 us -> 145 us
  local copies, waits for them, and re-layouts: 128 us -> 209 us
  blocking collectives: 282 us -> 258 us
    ppermute x8 -> x6, waiting for transfers between devices: 531 us -> 133 us  [the longest x2 129 us: body(): high = lax.ppermute(blended[:, :, :HALO], 'line', backward_pairs)]
    dot_general x33 -> x34, matrix products: 178 us -> 365 us  [the longest x32 364 us: mm(): jnp.einsum(pattern, a, b, precision=lax.Precision.HIGHEST, preferred_elem...]
    add x7 -> x5, other arithmetic: 190 us -> 2.45 us  [the longest x4 2.09 us: shift_weights(): summed = summed + tap_weights[..., tap_number] * matches]
    psum x2 -> x0, waiting for transfers between devices: 45.8 us -> none  [body(): factor = shrink(lax.psum(squares, 'chan'))]
    unnamed x101 -> x155, local copies, waits for them, and re-layouts: 47.7 us -> 4.72 us
    another operation x10 -> x12, local copies, waits for them, and re-layouts: 44.8 us -> 84 us  [the longest x4 34 us: body(): spec = jnp.stack([xr, xi]).reshape(2, cl, ext_rows, p_len, q_len)]
    unnamed x0 -> x19, other arithmetic: none -> 32.7 us
    slice x7 -> x13, local copies, waits for them, and re-layouts: 35.3 us -> 59.5 us  [the longest x4 27 us: body(): low = lax.ppermute(blended[:, :, rows - HALO:], 'line', forward_pairs)]
  transfers between devices with their start and end apart: 12 -> 7, of which waited for: 6 -> 3; matrix products, arithmetic and copies ran while one was open for 10% -> 21% of each run, Pallas kernels for 0% -> 0%
where the time goes in v1:
time: 1150 us; the launch traced here: 1140 us
  matrix products  365 us (32%)
  blocking collectives  258 us (22%)
  local copies, waits for them, and re-layouts  209 us (18%)
  other arithmetic  145 us (13%)
  waiting for transfers between devices  133 us (12%)
  starting transfers between devices  29.9 us (3%)
    dot_general x32, matrix products, mm(): jnp.einsum(pattern, a, b, precision=lax.Precision.HIGHEST, preferred_elem...  364 us
    all_gather x1, blocking collectives, body(): lax.all_gather(jnp.stack([tap_index, range_offset]), 'line', axis=1, tile...  258 us
    ppermute x2, waiting for transfers between devices, body(): high = lax.ppermute(blended[:, :, :HALO], 'line', backward_pairs)  129 us
    another operation x4, local copies, waits for them, and re-layouts, body(): spec = jnp.stack([xr, xi]).reshape(2, cl, ext_rows, p_len, q_len)  34 us
    unnamed x19, other arithmetic  32.7 us
    slice x4, local copies, waits for them, and re-layouts, body(): low = lax.ppermute(blended[:, :, rows - HALO:], 'line', forward_pairs)  27 us
    sub x2, other arithmetic, body(): resid = coef[None, :, None, None, None] * gram - data  24.1 us
  transfers between devices with their start and end apart: 7, of which 3 were waited for; matrix products, arithmetic and copies ran while one was open for 21% of the time, Pallas kernels for 0%

profile of v1, /device:TPU:21, one launch (start us, length us, event | category | flops | bytes accessed | tf_op | source)
XLA Modules:
  0.0 1142.6 jit_solution(16639016854318823054)
XLA Ops:
  0.6 10.4 multiply_add_fusion.1
  11.0 10.8 fusion.106
  21.9 5.9 copy.144
  39.2 17.5 %fusion.12 = (f32[1,8,128,1024]{3,1,0,2:T(8,128)S(1)}, f32[1,8,128,1024]{3,1,0,2:T(8,128)S(1)}) fusion(f32[1,8,128,1024]{3,2,1,0:T(8,128)S(1)} %get-tuple-element.49, f32[1,8,128,1024]{3,2,1,0:T(8,128)S(1)} %get-tuple-element.48, f32[8,1024]{1,0:T(8,128)S(1)} %copy-done.57, f32[128,1024]{1,0:T(8,128)S(1)} %copy-done.52, f32[8]{0:T(128)S(1)} %select_reduce_fusion), kind=kLoop, calls=%fused_computation.89 | loop fusion | flops 9437184 | bytes 17334304 | tf_op jit(solution)/shard_map/mul | solution.py:154
  58.3 10.7 add_multiply_fusion
  69.1 7.3 all-to-all-start
  76.4 258.3 %all_gather.3 = s32[2,16384]{1,0:T(2,128)S(1)} all-gather(s32[2,1024]{1,0:T(2,128)S(1)} %pad_add_fusion), channel_id=1, replica_groups=mesh['line'=16,'chan'=2] {'line'}, dimensions={1}, use_global_device_ids=true | all-gather | bytes 139264 | tf_op jit(solution)/shard_map/all_gather | solution.py:161
  343.0 6.1 copy.145
  354.4 6.3 fusion.102
  360.8 7.5 reshape_squeeze.24
  368.3 7.6 reshape_squeeze.25
  375.9 15.7 %fusion.110 = f32[112,128,128]{2,1,0:T(8,128)} fusion(f32[112,128,128]{2,1,0:T(8,128)} %reshape_squeeze.25, f32[128,128,1]{1,0,2:T(8,128)S(1)} %copy-done.43), kind=kOutput, calls=%fused_computation.285 | convolution fusion | flops 2818572288 | bytes 14745600 | tf_op jit(solution)/shard_map/kp,bpq->bkq/dot_general | solution.py:88
  391.6 14.0 %fusion.111 = f32[112,128,128]{2,1,0:T(8,128)} fusion(f32[112,128,128]{2,1,0:T(8,128)S(1)} %copy-done.8, f32[128,128,1]{1,0,2:T(8,128)S(1)} %copy-done.43), kind=kOutput, calls=%fused_computation.286 | convolution fusion | flops 2818572288 | bytes 14745600 | tf_op jit(solution)/shard_map/kp,bpq->bkq/dot_general | solution.py:88
  405.6 14.1 %fusion.109 = f32[112,128,128]{2,1,0:T(8,128)} fusion(f32[112,128,128]{2,1,0:T(8,128)S(1)} %copy-done.8, f32[128,128,1]{1,0,2:T(8,128)S(1)} %copy-done.25), kind=kOutput, calls=%fused_computation.284 | convolution fusion | flops 2818572288 | bytes 14745600 | tf_op jit(solution)/shard_map/kp,bpq->bkq/dot_general | solution.py:88
  419.7 20.9 %fusion.5 = (f32[112,128,128]{1,2,0:T(8,128)}, f32[112,128,128]{1,2,0:T(8,128)S(1)}) fusion(f32[128,128]{0,1:T(8,128)S(1)} %copy-done.53, f32[128,128]{0,1:T(8,128)S(1)} %copy-done.55, f32[112,128,128]{2,1,0:T(8,128)} %fusion.111, f32[112,128,128]{2,1,0:T(8,128)} %fusion.109, f32[112,128,128]{2,1,0:T(8,128)} %fusion.110, ...), kind=kOutput, calls=%fused_computation.78 | convolution fusion | flops 2833252352 | bytes 44236800 | tf_op jit(solution)/shard_map/kp,bpq->bkq/dot_general | solution.py:88
  440.7 11.9 %fusion.113 = f32[112,128,128]{2,1,0:T(8,128)S(1)} fusion(f32[112,128,128]{1,2,0:T(8,128)S(1)} %get-tuple-element.33, f32[128,128,1]{1,0,2:T(8,128)S(1)} %copy-done.25), kind=kOutput, calls=%fused_computation.288 | convolution fusion | flops 2818572288 | bytes 14745600 | tf_op jit(solution)/shard_map/bkq,qj->bkj/dot_general | solution.py:88
  452.6 14.1 %convolution_add_fusion.1 = f32[112,128,128]{2,1,0:T(8,128)} fusion(f32[112,128,128]{2,1,0:T(8,128)S(1)} %fusion.113, f32[112,128,128]{1,2,0:T(8,128)S(1)} %copy-done.11, f32[128,128,1]{1,0,2:T(8,128)S(1)} %copy-done.43), kind=kOutput, calls=%fused_computation.104 | convolution fusion | flops 2820407296 | bytes 22085632 | tf_op jit(solution)/shard_map/bkq,qj->bkj/dot_general | solution.py:88
  466.7 8.6 copy.156
  475.3 14.3 %fusion.112 = f32[112,128,128]{2,1,0:T(8,128)S(1)} fusion(f32[112,128,128]{1,2,0:T(8,128)} %get-tuple-element.32, f32[128,128,1]{1,0,2:T(8,128)S(1)} %copy-done.25), kind=kOutput, calls=%fused_computation.287 | convolution fusion | flops 2818572288 | bytes 14745600 | tf_op jit(solution)/shard_map/bkq,qj->bkj/dot_general | solution.py:88
  489.6 14.1 %convolution_subtract_fusion.1 = f32[112,128,128]{2,1,0:T(8,128)} fusion(f32[112,128,128]{2,1,0:T(8,128)S(1)} %fusion.112, f32[112,128,128]{1,2,0:T(8,128)S(1)} %bitcast.257, f32[128,128,1]{1,0,2:T(8,128)S(1)} %copy-done.44), kind=kOutput, calls=%fused_computation.105 | convolution fusion | flops 2820407296 | bytes 22085632 | tf_op jit(solution)/shard_map/bkq,qj->bkj/dot_general | solution.py:88
  503.7 8.5 copy.155
  533.0 11.6 %copy.222 = f32[2,8,16,8,1024]{4,2,3,1,0:T(8,128)} copy(f32[2,8,16,8,1024]{4,1,0,3,2:T(8,128)} %bitcast.41) | data formatting | bytes 16777216 | tf_op jit(solution)/shard_map/all_to_all | solution.py:158
  544.6 9.5 reshape.152
  554.1 12.1 %bitcast_subtract_fusion.1 = f32[2,8,8,128,128]{3,4,2,1,0:T(8,128)} fusion(f32[2,8,8,128,128]{4,3,2,1,0:T(8,128)} %reshape.152, f32[2,8,8,128,128]{3,4,2,1,0:T(8,128)} %fusion.56, f32[8]{0:T(128)S(1)} %multiply_multiply_fusion), kind=kLoop, calls=%fused_computation.58 | loop fusion | flops 4194304 | bytes 25165856 | tf_op jit(solution)/shard_map/sub | solution.py:242
  570.3 6.7 fusion.114
  577.0 7.1 fusion.115
  584.0 6.7 convolution_subtract_fusion.3
  590.8 7.2 convolution_add_fusion.3
  598.0 7.0 fusion.16
  605.0 8.4 fusion.15
  613.4 8.3 add_bitcast_fusion.1
  632.3 11.4 subtract_bitcast_fusion.1
  654.3 6.6 multiply_reduce_fusion.1
  660.9 7.9 collective-permute-start.2
  670.6 11.0 multiply_add_fusion
  681.6 10.8 fusion.104
  696.6 5.7 collective-permute-start.4
  706.7 129.5 %collective-permute-done.4 = f32[2,8,3,16384]{3,1,2,0:T(8,128)S(1)} collective-permute-done((f32[2,8,3,16384]{3,1,2,0:T(8,128)S(1)}, f32[2,8,3,16384]{3,1,2,0:T(8,128)S(1)}, u32[]{:S(2)}, u32[]{:S(2)}) %collective-permute-start.4) | collective-permute-done | bytes 3145760 | tf_op jit(solution)/shard_map/ppermute | solution.py:188
  847.9 6.3 fusion.101
  854.2 7.5 reshape_squeeze.28
  861.8 16.5 %fusion.118 = f32[112,128,128]{2,1,0:T(8,128)} fusion(f32[112,128,128]{2,1,0:T(8,128)} %reshape_squeeze.28, f32[128,128,1]{1,0,2:T(8,128)S(1)} %copy-done.45), kind=kOutput, calls=%fused_computation.293 | convolution fusion | flops 2818572288 | bytes 14745600 | tf_op jit(solution)/shard_map/kp,bpq->bkq/dot_general | solution.py:88
  878.3 14.0 %fusion.116 = f32[112,128,128]{2,1,0:T(8,128)} fusion(f32[112,128,128]{2,1,0:T(8,128)S(1)} %copy-done.9, f32[128,128,1]{1,0,2:T(8,128)S(1)} %copy-done.25), kind=kOutput, calls=%fused_computation.291 | convolution fusion | flops 2818572288 | bytes 14745600 | tf_op jit(solution)/shard_map/kp,bpq->bkq/dot_general | solution.py:88
  892.3 7.5 reshape_squeeze.29
  899.8 15.8 %fusion.117 = f32[112,128,128]{2,1,0:T(8,128)} fusion(f32[112,128,128]{2,1,0:T(8,128)} %reshape_squeeze.29, f32[128,128,1]{1,0,2:T(8,128)S(1)} %copy-done.45), kind=kOutput, calls=%fused_computation.292 | convolution fusion | flops 2818572288 | bytes 14745600 | tf_op jit(solution)/shard_map/kp,bpq->bkq/dot_general | solution.py:88
  915.6 21.5 %fusion.3 = (f32[112,128,128]{1,2,0:T(8,128)S(1)}, f32[112,128,128]{1,2,0:T(8,128)}) fusion(f32[128,128]{0,1:T(8,128)S(1)} %copy-done.54, f32[128,128]{0,1:T(8,128)S(1)} %copy-done.56, f32[112,128,128]{2,1,0:T(8,128)} %fusion.118, f32[112,128,128]{2,1,0:T(8,128)} %fusion.116, f32[112,128,128]{2,1,0:T(8,128)} %fusion.117, ...), kind=kOutput, calls=%fused_computation.72 | convolution fusion | flops 2833252352 | bytes 44236800 | tf_op jit(solution)/shard_map/kp,bpq->bkq/dot_general | solution.py:88
  937.1 11.9 %fusion.119 = f32[112,128,128]{2,1,0:T(8,128)S(1)} fusion(f32[112,128,128]{1,2,0:T(8,128)S(1)} %get-tuple-element.30, f32[128,128,1]{1,0,2:T(8,128)S(1)} %copy-done.25), kind=kOutput, calls=%fused_computation.294 | convolution fusion | flops 2818572288 | bytes 14745600 | tf_op jit(solution)/shard_map/bkq,qj->bkj/dot_general | solution.py:88
  949.0 11.7 %fusion.120 = f32[112,128,128]{2,1,0:T(8,128)S(1)} fusion(f32[112,128,128]{1,2,0:T(8,128)S(1)} %copy-done.12, f32[128,128,1]{1,0,2:T(8,128)S(1)} %copy-done.25), kind=kOutput, calls=%fused_computation.295 | convolution fusion | flops 2818572288 | bytes 14745600 | tf_op jit(solution)/shard_map/bkq,qj->bkj/dot_general | solution.py:88
  960.8 14.3 %convolution_subtract_fusion = f32[112,128,128]{2,1,0:T(8,128)} fusion(f32[112,128,128]{2,1,0:T(8,128)S(1)} %fusion.119, f32[112,128,128]{1,2,0:T(8,128)S(1)} %copy-done.12, f32[128,128,1]{1,0,2:T(8,128)S(1)} %copy-done.45), kind=kOutput, calls=%fused_computation.103 | convolution fusion | flops 2820407296 | bytes 22085632 | tf_op jit(solution)/shard_map/bkq,qj->bkj/dot_general | solution.py:88
  975.1 13.9 %convolution_add_fusion = f32[112,128,128]{2,1,0:T(8,128)} fusion(f32[112,128,128]{2,1,0:T(8,128)S(1)} %fusion.120, f32[112,128,128]{1,2,0:T(8,128)S(1)} %get-tuple-element.30, f32[128,128,1]{1,0,2:T(8,128)S(1)} %copy-done.45), kind=kOutput, calls=%fused_computation.102 | convolution fusion | flops 2820407296 | bytes 22085632 | tf_op jit(solution)/shard_map/bkq,qj->bkj/dot_general | solution.py:88
  989.0 8.4 copy.182
  997.4 8.5 copy.181
  1026.5 12.0 %bitcast_subtract_fusion = f32[2,8,8,128,128]{3,4,2,1,0:T(8,128)} fusion(f32[2,8,8,128,128]{4,3,2,1,0:T(8,128)} %reshape.152, f32[2,8,8,128,128]{3,4,2,1,0:T(8,128)} %fusion.51, f32[8]{0:T(128)S(1)} %copy-done.61), kind=kLoop, calls=%fused_computation.57 | loop fusion | flops 4194304 | bytes 25165856 | tf_op jit(solution)/shard_map/sub | solution.py:242
  1042.6 6.9 fusion.121
  1049.4 6.9 fusion.122
  1056.3 7.1 convolution_subtract_fusion.2
  1063.5 6.8 convolution_add_fusion.2
  1070.3 7.0 fusion.18
  1077.3 8.4 fusion.17
  1085.7 8.6 add_bitcast_fusion
  1094.2 5.6 copy.190
  1104.8 11.2 subtract_bitcast_fusion
  1116.1 5.6 copy.187
  1126.7 6.6 multiply_reduce_fusion
  1136.1 6.3 broadcast_multiply_fusion
  (220 shorter events, 131.5 us)
Async XLA Ops:
  0.6 36.2 %copy-start = (f32[16,4]{0,1:T(4,128)S(1)}, f32[16,4]{0,1:T(4,128)}, u32[]{:S(2)}) copy-start(f32[16,4]{0,1:T(4,128)} %param.41) | copy-start | bytes 772
  21.9 9.1 copy-start.26
  21.9 15.0 %copy-start.59 = (s32[1024]{0:T(1024)S(1)}, s32[1024]{0:T(1024)}, u32[]{:S(2)}) copy-start(s32[1024]{0:T(1024)} %param.40) | copy-start | bytes 12292
  21.9 15.5 %copy-start.28 = (f32[2,8,128,1024]{3,2,1,0:T(8,128)S(1)}, f32[2,8,128,1024]{3,2,1,0:T(8,128)}, u32[]{:S(2)}) copy-start(f32[2,8,128,1024]{3,2,1,0:T(8,128)} %param.34) | copy-start | bytes 25165828
  27.7 310.9 %collective-permute-start.1 = (f32[2,8,3,16384]{3,1,2,0:T(8,128)}, f32[2,8,3,16384]{3,1,2,0:T(8,128)}, u32[]{:S(2)}, u32[]{:S(2)}) collective-permute-start(f32[2,8,3,16384]{3,1,2,0:T(8,128)} %copy.144), channel_id=1, source_target_pairs={{2,0},{4,2},{6,4},{8,6},{10,8},{12,10},{14,12},{16,14},{18,16},{20... | collective-permute-start | bytes 9437192 | tf_op jit(solution)/shard_map/ppermute | solution.py:188
  34.4 308.5 %collective-permute-start = (f32[2,8,3,16384]{3,1,2,0:T(8,128)}, f32[2,8,3,16384]{3,1,2,0:T(8,128)}, u32[]{:S(2)}, u32[]{:S(2)}) collective-permute-start(f32[2,8,3,16384]{3,1,2,0:T(8,128)} %copy.143), channel_id=1, source_target_pairs={{0,2},{2,4},{4,6},{6,8},{8,10},{10,12},{12,14},{14,16},{16,18},{18... | collective-permute-start | bytes 9437192 | tf_op jit(solution)/shard_map/ppermute | solution.py:187
  69.1 463.9 %all-to-all-start = ((f32[2,8,128,1024]{3,1,0,2:T(8,128)}), f32[2,8,128,1024]{3,1,0,2:T(8,128)}, u32[]{:S(2)}, u32[]{:S(2)}) async-start(f32[2,8,128,1024]{3,1,0,2:T(8,128)} %add_multiply_fusion), calls=%async_computation | async-start | bytes 16777216 | tf_op jit(solution)/shard_map/all_to_all | solution.py:158
  76.3 477.7 %copy-start.60 = (f32[8]{0:T(128)}, f32[8]{0:T(128)S(1)}, u32[]{:S(2)}) copy-start(f32[8]{0:T(128)S(1)} %multiply_multiply_fusion) | copy-start | bytes 100
  338.2 185.4 %copy-start.29 = (f32[128,128]{0,1:T(8,128)}, f32[128,128]{0,1:T(8,128)S(1)}, u32[]{:S(2)}) copy-start(f32[128,128]{0,1:T(8,128)S(1)} %get-tuple-element.53) | copy-start | bytes 196612
  338.2 10.9 slice-start.4
  338.5 192.5 %copy-start.17 = (f32[16384,1]{0,1:T(1,128)}, f32[16384,1]{0,1:T(1,128)S(1)}, u32[]{:S(2)}) copy-start(f32[16384,1]{0,1:T(1,128)S(1)} %get-tuple-element.65) | copy-start | bytes 196612
  338.6 192.4 %copy-start.19 = (f32[16384,1]{0,1:T(1,128)}, f32[16384,1]{0,1:T(1,128)S(1)}, u32[]{:S(2)}) copy-start(f32[16384,1]{0,1:T(1,128)S(1)} %get-tuple-element.66) | copy-start | bytes 196612
  338.6 192.4 %copy-start.21 = (f32[16384,1]{0,1:T(1,128)}, f32[16384,1]{0,1:T(1,128)S(1)}, u32[]{:S(2)}) copy-start(f32[16384,1]{0,1:T(1,128)S(1)} %get-tuple-element.67) | copy-start | bytes 196612
  338.6 192.4 %copy-start.23 = (f32[16384,1]{0,1:T(1,128)}, f32[16384,1]{0,1:T(1,128)S(1)}, u32[]{:S(2)}) copy-start(f32[16384,1]{0,1:T(1,128)S(1)} %get-tuple-element.68) | copy-start | bytes 196612
  338.6 10.5 slice-start.5
  368.3 7.6 copy-start.43
  375.9 15.7 %copy-start.8 = (f32[112,128,128]{2,1,0:T(8,128)S(1)}, f32[112,128,128]{2,1,0:T(8,128)}, u32[]{:S(2)}) copy-start(f32[112,128,128]{2,1,0:T(8,128)} %reshape_squeeze.24) | copy-start | bytes 22020100
  391.6 14.1 %copy-start.25 = (f32[128,128,1]{1,0,2:T(8,128)S(1)}, f32[128,128,1]{1,0,2:T(8,128)}, u32[]{:S(2)}) copy-start(f32[128,128,1]{1,0,2:T(8,128)} %constant.137) | copy-start | bytes 196612
  405.6 14.1 %copy-start.53 = (f32[128,128]{0,1:T(8,128)S(1)}, f32[128,128]{0,1:T(8,128)}, u32[]{:S(2)}) copy-start(f32[128,128]{0,1:T(8,128)} %constant.130.clone) | copy-start | bytes 196612
  405.6 14.1 %copy-start.55 = (f32[128,128]{0,1:T(8,128)S(1)}, f32[128,128]{0,1:T(8,128)}, u32[]{:S(2)}) copy-start(f32[128,128]{0,1:T(8,128)} %constant.129.clone) | copy-start | bytes 196612
  440.7 11.9 %copy-start.10 = (f32[112,128,128]{1,2,0:T(8,128)}, f32[112,128,128]{1,2,0:T(8,128)S(1)}, u32[]{:S(2)}) copy-start(f32[112,128,128]{1,2,0:T(8,128)S(1)} %get-tuple-element.33) | copy-start | bytes 22020100
  440.7 11.9 %copy-start.11 = (f32[112,128,128]{1,2,0:T(8,128)S(1)}, f32[112,128,128]{1,2,0:T(8,128)}, u32[]{:S(2)}) copy-start(f32[112,128,128]{1,2,0:T(8,128)} %get-tuple-element.32) | copy-start | bytes 22020100
  466.7 22.9 %slice-start.8 = ((s8[7340032]{0:T(1024)(128)(4,1)}), s8[3145728]{0:T(1024)(128)(4,1)S(1)}, s32[]{:S(2)}) async-start(s8[7340032]{0:T(1024)(128)(4,1)} %bitcast.256), calls=%async_computation.9 | async-start | bytes 6291456
  475.3 14.3 %slice-start.9 = ((s8[7340032]{0:T(1024)(128)(4,1)}), s8[4194304]{0:T(1024)(128)(4,1)S(1)}, s32[]{:S(2)}) async-start(s8[7340032]{0:T(1024)(128)(4,1)} %bitcast.256), calls=%async_computation.10 | async-start | bytes 8388608
  475.3 14.3 %copy-start.44 = (f32[128,128,1]{1,0,2:T(8,128)S(1)}, f32[128,128,1]{1,0,2:T(8,128)}, u32[]{:S(2)}) copy-start(f32[128,128,1]{1,0,2:T(8,128)} %constant.138) | copy-start | bytes 196612
  503.7 13.3 %slice-start.2 = ((s8[7340032]{0:T(1024)(128)(4,1)}), s8[3145728]{0:T(1024)(128)(4,1)S(1)}, s32[]{:S(2)}) async-start(s8[7340032]{0:T(1024)(128)(4,1)} %bitcast.250), calls=%async_computation.3 | async-start | bytes 6291456
  512.3 7.0 copy-start.3
  512.3 7.0 copy-start.31
  512.3 7.0 copy-start.33
  512.3 7.0 copy-start.35
  570.3 13.8 %copy-start.37 = (f32[128,128,1]{1,0,2:T(8,128)S(1)}, f32[128,128,1]{1,0,2:T(8,128)}, u32[]{:S(2)}) copy-start(f32[128,128,1]{1,0,2:T(8,128)} %constant.139) | copy-start | bytes 196612
  590.7 22.7 %copy-start.6 = (f32[64,128,128]{2,1,0:T(8,128)}, f32[64,128,128]{2,1,0:T(8,128)S(1)}, u32[]{:S(2)}) copy-start(f32[64,128,128]{2,1,0:T(8,128)S(1)} %convolution_subtract_fusion.3) | copy-start | bytes 12582916
  590.7 7.2 copy-start.39
  590.8 7.2 copy-start.41
  598.0 15.4 %copy-start.7 = (f32[64,128,128]{2,1,0:T(8,128)}, f32[64,128,128]{2,1,0:T(8,128)S(1)}, u32[]{:S(2)}) copy-start(f32[64,128,128]{2,1,0:T(8,128)S(1)} %convolution_add_fusion.3) | copy-start | bytes 12582916
  654.3 16.3 %copy-start.15 = (f32[1,8,8,16384]{3,2,1,0:T(8,128)S(1)}, f32[1,8,8,16384]{3,2,1,0:T(8,128)}, u32[]{:S(2)}) copy-start(f32[1,8,8,16384]{3,2,1,0:T(8,128)} %stack.117) | copy-start | bytes 12582916
  654.3 16.3 %copy-start.16 = (f32[1,8,8,16384]{3,2,1,0:T(8,128)S(1)}, f32[1,8,8,16384]{3,2,1,0:T(8,128)}, u32[]{:S(2)}) copy-start(f32[1,8,8,16384]{3,2,1,0:T(8,128)} %stack.116) | copy-start | bytes 12582916
  660.9 9.5 collective-permute-start.2
  692.5 9.9 copy-start.27
  696.6 139.5 %collective-permute-start.4 = (f32[2,8,3,16384]{3,1,2,0:T(8,128)S(1)}, f32[2,8,3,16384]{3,1,2,0:T(8,128)S(1)}, u32[]{:S(2)}, u32[]{:S(2)}) collective-permute-start(f32[2,8,3,16384]{3,1,2,0:T(8,128)S(1)} %copy.170), channel_id=1, source_target_pairs={{2,0},{4,2},{6,4},{8,6},{10,8},{12,10},{14,12},{16,14},{18,16},{20... | collective-permute-start | bytes 9437192 | tf_op jit(solution)/shard_map/ppermute | solution.py:188
  702.4 140.2 %slice-start.6 = ((s8[8388608]{0:T(1024)(128)(4,1)}), s8[4194304]{0:T(1024)(128)(4,1)S(1)}, s32[]{:S(2)}) async-start(s8[8388608]{0:T(1024)(128)(4,1)} %bitcast.254), calls=%async_computation.7 | async-start | bytes 8388608
  704.2 138.3 %slice-start.7 = ((s8[8388608]{0:T(1024)(128)(4,1)}), s8[4194304]{0:T(1024)(128)(4,1)S(1)}, s32[]{:S(2)}) async-start(s8[8388608]{0:T(1024)(128)(4,1)} %bitcast.254), calls=%async_computation.8 | async-start | bytes 8388608
  704.2 134.1 %collective-permute-start.3 = (f32[2,8,3,16384]{3,1,2,0:T(8,128)S(1)}, f32[2,8,3,16384]{3,1,2,0:T(8,128)S(1)}, u32[]{:S(2)}, u32[]{:S(2)}) collective-permute-start(f32[2,8,3,16384]{3,1,2,0:T(8,128)S(1)} %copy.169), channel_id=1, source_target_pairs={{0,2},{2,4},{4,6},{6,8},{8,10},{10,12},{12,14},{14,16},{16,18},{18... | collective-permute-start | bytes 9437192 | tf_op jit(solution)/shard_map/ppermute | solution.py:187
  854.2 7.5 copy-start.45
  861.7 16.6 %copy-start.9 = (f32[112,128,128]{2,1,0:T(8,128)S(1)}, f32[112,128,128]{2,1,0:T(8,128)}, u32[]{:S(2)}) copy-start(f32[112,128,128]{2,1,0:T(8,128)} %reshape_squeeze.28) | copy-start | bytes 22020100
  899.8 15.8 %copy-start.54 = (f32[128,128]{0,1:T(8,128)S(1)}, f32[128,128]{0,1:T(8,128)}, u32[]{:S(2)}) copy-start(f32[128,128]{0,1:T(8,128)} %constant.130.clone) | copy-start | bytes 196612
  899.8 15.8 %copy-start.56 = (f32[128,128]{0,1:T(8,128)S(1)}, f32[128,128]{0,1:T(8,128)}, u32[]{:S(2)}) copy-start(f32[128,128]{0,1:T(8,128)} %constant.129.clone) | copy-start | bytes 196612
  937.1 11.9 %copy-start.12 = (f32[112,128,128]{1,2,0:T(8,128)S(1)}, f32[112,128,128]{1,2,0:T(8,128)}, u32[]{:S(2)}) copy-start(f32[112,128,128]{1,2,0:T(8,128)} %get-tuple-element.31) | copy-start | bytes 22020100
  997.4 8.6 copy-start.18
  997.4 8.6 copy-start.20
  997.4 8.6 copy-start.22
  997.4 8.6 copy-start.24
  997.4 8.6 copy-start.30
  997.4 13.4 %slice-start = ((s8[7340032]{0:T(1024)(128)(4,1)}), s8[3145728]{0:T(1024)(128)(4,1)S(1)}, s32[]{:S(2)}) async-start(s8[7340032]{0:T(1024)(128)(4,1)} %bitcast.248), calls=%async_computation.1 | async-start | bytes 6291456
  1006.0 7.0 copy-start.2
  1006.0 7.0 copy-start.32
  1006.0 7.0 copy-start.34
  1006.0 6.9 copy-start.36
  1042.5 13.8 %copy-start.38 = (f32[128,128,1]{1,0,2:T(8,128)S(1)}, f32[128,128,1]{1,0,2:T(8,128)}, u32[]{:S(2)}) copy-start(f32[128,128,1]{1,0,2:T(8,128)} %constant.139) | copy-start | bytes 196612
  1063.4 22.2 %copy-start.4 = (f32[64,128,128]{2,1,0:T(8,128)}, f32[64,128,128]{2,1,0:T(8,128)S(1)}, u32[]{:S(2)}) copy-start(f32[64,128,128]{2,1,0:T(8,128)S(1)} %convolution_subtract_fusion.2) | copy-start | bytes 12582916
  1070.3 15.4 %copy-start.5 = (f32[64,128,128]{2,1,0:T(8,128)}, f32[64,128,128]{2,1,0:T(8,128)S(1)}, u32[]{:S(2)}) copy-start(f32[64,128,128]{2,1,0:T(8,128)S(1)} %convolution_add_fusion.2) | copy-start | bytes 12582916
  1126.7 9.3 copy-start.13
  1126.7 9.3 copy-start.14
  1133.3 2.5 collective-permute-start.5
  (17 other events, 50.7 us)

commit v2 on v1

--- a/solution.py
+++ b/solution.py
@@ -5,6 +5,7 @@
 import jax.numpy as jnp
 from jax import lax
 from jax.sharding import PartitionSpec as P
+from jax.experimental import pallas as pl
 
 K = 4
 Q = 16
@@ -70,50 +71,131 @@
     return summed
 
 
-def dft_matrix(count, sign, scale):
+def left_block(count, sign):
     counter = np.arange(count)
     angle = (np.outer(counter, counter) % count) * (2.0 * np.pi / count)
-    return (
-        jnp.asarray(np.cos(angle) * scale, jnp.float32),
-        jnp.asarray(sign * np.sin(angle) * scale, jnp.float32),
-    )
+    c = np.cos(angle)
+    s = sign * np.sin(angle)
+    return jnp.asarray(np.block([[c, -s], [s, c]]), jnp.float32)
+
+
+def right_block(count, sign):
+    counter = np.arange(count)
+    angle = (np.outer(counter, counter) % count) * (2.0 * np.pi / count)
+    c = np.cos(angle)
+    s = sign * np.sin(angle)
+    return jnp.asarray(np.block([[c, s], [-s, c]]), jnp.float32)
 
 
 def twiddle(rows, cols, total, sign):
     angle = (np.outer(np.arange(rows), np.arange(cols)) % total) * (2.0 * np.pi / total)
-    return jnp.asarray(np.cos(angle), jnp.float32), jnp.asarray(sign * np.sin(angle), jnp.float32)
-
-
-def mm(pattern, a, b):
-    return jnp.einsum(
-        pattern, a, b, precision=lax.Precision.HIGHEST, preferred_element_type=jnp.float32
-    )
-
-
-def forward_transform(xr, xi, p_len, q_len):
-    wc, ws = dft_matrix(p_len, -1.0, 1.0)
-    vc, vs = dft_matrix(q_len, -1.0, 1.0)
-    tc, ts = twiddle(p_len, q_len, p_len * q_len, -1.0)
-    mr = mm("kp,bpq->bkq", wc, xr) - mm("kp,bpq->bkq", ws, xi)
-    mi = mm("kp,bpq->bkq", wc, xi) + mm("kp,bpq->bkq", ws, xr)
+    return jnp.asarray(np.stack([np.cos(angle), sign * np.sin(angle)]), jnp.float32)
+
+
+def dot(a, b):
+    return jnp.dot(a, b, precision=lax.Precision.HIGHEST, preferred_element_type=jnp.float32)
+
+
+def forward_kernel(x_ref, w_ref, v_ref, t_ref, o_ref):
+    nb, p_len, q_len = x_ref.shape[1], x_ref.shape[2], x_ref.shape[3]
+    stacked = jnp.concatenate(
+        [
+            jnp.concatenate([x_ref[0, b] for b in range(nb)], axis=1),
+            jnp.concatenate([x_ref[1, b] for b in range(nb)], axis=1),
+        ],
+        axis=0,
+    )
+    mid = dot(w_ref[...], stacked)
+    tc = jnp.concatenate([t_ref[0]] * nb, axis=1)
+    ts = jnp.concatenate([t_ref[1]] * nb, axis=1)
+    mr = mid[:p_len]
+    mi = mid[p_len:]
     tr = mr * tc - mi * ts
     ti = mi * tc + mr * ts
-    out_r = mm("bkq,qj->bkj", tr, vc) - mm("bkq,qj->bkj", ti, vs)
-    out_i = mm("bkq,qj->bkj", ti, vc) + mm("bkq,qj->bkj", tr, vs)
-    return out_r, out_i
-
-
-def inverse_transform(yr, yi, p_len, q_len):
-    wc, ws = dft_matrix(p_len, 1.0, 1.0)
-    vc, vs = dft_matrix(q_len, 1.0, 1.0)
-    tc, ts = twiddle(p_len, q_len, p_len * q_len, 1.0)
-    mr = mm("bkj,jq->bkq", yr, vc) - mm("bkj,jq->bkq", yi, vs)
-    mi = mm("bkj,jq->bkq", yi, vc) + mm("bkj,jq->bkq", yr, vs)
+    turned = jnp.concatenate(
+        [
+            jnp.concatenate([tr[:, b * q_len : (b + 1) * q_len], ti[:, b * q_len : (b + 1) * q_len]], axis=1)
+            for b in range(nb)
+        ],
+        axis=0,
+    )
+    out = dot(turned, v_ref[...])
+    for b in range(nb):
+        o_ref[0, b] = out[b * p_len : (b + 1) * p_len, :q_len]
+        o_ref[1, b] = out[b * p_len : (b + 1) * p_len, q_len:]
+
+
+def inverse_kernel(y_ref, v_ref, w_ref, t_ref, o_ref):
+    nb, p_len, q_len = y_ref.shape[1], y_ref.shape[2], y_ref.shape[3]
+    stacked = jnp.concatenate(
+        [jnp.concatenate([y_ref[0, b], y_ref[1, b]], axis=1) for b in range(nb)], axis=0
+    )
+    mid = dot(stacked, v_ref[...])
+    tc = jnp.concatenate([t_ref[0]] * nb, axis=0)
+    ts = jnp.concatenate([t_ref[1]] * nb, axis=0)
+    mr = mid[:, :q_len]
+    mi = mid[:, q_len:]
     tr = mr * tc - mi * ts
     ti = mi * tc + mr * ts
-    out_r = mm("pk,bkq->bpq", wc, tr) - mm("pk,bkq->bpq", ws, ti)
-    out_i = mm("pk,bkq->bpq", wc, ti) + mm("pk,bkq->bpq", ws, tr)
-    return out_r, out_i
+    turned = jnp.concatenate(
+        [
+            jnp.concatenate([tr[b * p_len : (b + 1) * p_len] for b in range(nb)], axis=1),
+            jnp.concatenate([ti[b * p_len : (b + 1) * p_len] for b in range(nb)], axis=1),
+        ],
+        axis=0,
+    )
+    out = dot(w_ref[...], turned)
+    for b in range(nb):
+        o_ref[0, b] = out[:p_len, b * q_len : (b + 1) * q_len]
+        o_ref[1, b] = out[p_len:, b * q_len : (b + 1) * q_len]
+
+
+def block_count(total):
+    for nb in (8, 7, 6, 5, 4, 3, 2, 1):
+        if total % nb == 0:
+            return nb
+    return 1
+
+
+def run_transform(kernel, data, first, second, turn):
+    _, total, p_len, q_len = data.shape
+    nb = block_count(total)
+    flops = 2 * 2 * total * (2 * p_len) * (2 * q_len) * (p_len + q_len) // 2
+    return pl.pallas_call(
+        kernel,
+        out_shape=jax.ShapeDtypeStruct(data.shape, jnp.float32),
+        grid=(total // nb,),
+        in_specs=[
+            pl.BlockSpec((2, nb, p_len, q_len), lambda i: (0, i, 0, 0)),
+            pl.BlockSpec(first.shape, lambda i: (0, 0)),
+            pl.BlockSpec(second.shape, lambda i: (0, 0)),
+            pl.BlockSpec(turn.shape, lambda i: (0, 0, 0)),
+        ],
+        out_specs=pl.BlockSpec((2, nb, p_len, q_len), lambda i: (0, i, 0, 0)),
+        cost_estimate=pl.CostEstimate(
+            flops=flops, bytes_accessed=2 * data.size * 4, transcendentals=0
+        ),
+    )(data, first, second, turn)
+
+
+def forward_transform(x, p_len, q_len):
+    return run_transform(
+        forward_kernel,
+        x,
+        left_block(p_len, -1.0),
+        right_block(q_len, -1.0),
+        twiddle(p_len, q_len, p_len * q_len, -1.0),
+    )
+
+
+def inverse_transform(y, p_len, q_len):
+    return run_transform(
+        inverse_kernel,
+        y,
+        right_block(q_len, 1.0),
+        left_block(p_len, 1.0),
+        twiddle(p_len, q_len, p_len * q_len, 1.0),
+    )
 
 
 def shrink(squares):
@@ -155,10 +237,11 @@
     back_i = gain * (cos_a * observed[1] - sin_a * observed[0])
     data = adjoint_shift(jnp.stack([back_r, back_i]), local_weights)
     data = data * (step_length / math.sqrt(na))
+    packed = lax.all_gather(jnp.stack([tap_index, range_offset]), "line", axis=1, tiled=True)
+    packed, data = lax.optimization_barrier((packed, data))
     data = lax.all_to_all(data, "line", split_axis=2, concat_axis=3, tiled=True)
     data = data.reshape(2, cl, rows, q_len, p_len).swapaxes(-1, -2)
 
-    packed = lax.all_gather(jnp.stack([tap_index, range_offset]), "line", axis=1, tiled=True)
     taps = tap_table(packed[0], kernel_table)
     weights = shift_weights(packed[1], taps)
 
@@ -188,10 +271,8 @@
         high = lax.ppermute(blended[:, :, :HALO], "line", backward_pairs)
         ext = jnp.concatenate([low, blended, high], axis=2)
         ext_rows = rows + 2 * HALO
-        xr, xi = forward_transform(
-            ext[0].reshape(-1, p_len, q_len), ext[1].reshape(-1, p_len, q_len), p_len, q_len
-        )
-        spec = jnp.stack([xr, xi]).reshape(2, cl, ext_rows, p_len, q_len)
+        spec = forward_transform(ext.reshape(2, -1, p_len, q_len), p_len, q_len)
+        spec = spec.reshape(2, cl, ext_rows, p_len, q_len)
 
         def at(r):
             return spec[:, :, r]
@@ -240,10 +321,8 @@
             gram[r] = gram[r] - jnp.where(last, high_fix[idx], 0.0)
         gram = jnp.stack(gram, axis=2)
         resid = coef[None, :, None, None, None] * gram - data
-        gr, gi = inverse_transform(
-            resid[0].reshape(-1, p_len, q_len), resid[1].reshape(-1, p_len, q_len), p_len, q_len
-        )
-        shifted = blended - jnp.stack([gr, gi]).reshape(blended.shape)
+        grad = inverse_transform(resid.reshape(2, -1, p_len, q_len), p_len, q_len)
+        shifted = blended - grad.reshape(blended.shape)
         squares = jnp.sum(shifted * shifted, axis=(0, 1))
         if chans == 2:
             squares = squares + lax.ppermute(squares, "chan", [(0, 1), (1, 0)])

time: 1150 us -> 909 us (0.79)
  matrix products: 365 us -> 0.86 us
  Pallas kernels: 0 us -> 118 us
  blocking collectives: 258 us -> 150 us
  waiting for transfers between devices: 133 us -> 182 us
  other arithmetic: 145 us -> 181 us
  local copies, waits for them, and re-layouts: 209 us -> 236 us
    dot_general x32 -> x0, matrix products: 364 us -> none  [mm(): jnp.einsum(pattern, a, b, precision=lax.Precision.HIGHEST, preferred_elem...]
    pallas_call x0 -> x4, Pallas kernels: none -> 118 us  [run_transform(): pl.pallas_call(kernel, out_shape=jax.ShapeDtypeStruct(data.shape, jnp.flo...]
    all_gather x1, blocking collectives: 258 us -> 150 us  [body(): lax.all_gather(jnp.stack([tap_index, range_offset]), 'line', axis=1, tile...]
    reshape x0 -> x6, local copies, waits for them, and re-layouts: none -> 87.2 us  [the longest x4 67.9 us: body(): spec = forward_transform(ext.reshape(2, -1, p_len, q_len), p_len, q_len)]
    another operation x12 -> x0, local copies, waits for them, and re-layouts: 84 us -> none  [the longest x4 34 us: body(): spec = jnp.stack([xr, xi]).reshape(2, cl, ext_rows, p_len, q_len)]
    unnamed x155 -> x125, local copies, waits for them, and re-layouts: 4.72 us -> 85 us
    ppermute x2, waiting for transfers between devices: 0.01 us -> 66.2 us  [body(): low = lax.ppermute(blended[:, :, rows - HALO:], 'line', forward_pairs)]
    ppermute x2, waiting for transfers between devices: 129 us -> 68.1 us  [body(): high = lax.ppermute(blended[:, :, :HALO], 'line', backward_pairs)]
  transfers between devices with their start and end apart: 7 -> 7, of which waited for: 3 -> 4; matrix products, arithmetic and copies ran while one was open for 21% -> 17% of each run, Pallas kernels for 0% -> 3%
where the time goes in v2:
time: 909 us; the launch traced here: 900 us
  local copies, waits for them, and re-layouts  236 us (26%)
  waiting for transfers between devices  182 us (20%)
  other arithmetic  181 us (20%)
  blocking collectives  150 us (17%)
  Pallas kernels  118 us (13%)
  starting transfers between devices  29.5 us (3%)
    all_gather x1, blocking collectives, body(): lax.all_gather(jnp.stack([tap_index, range_offset]), 'line', axis=1, tile...  150 us
    pallas_call x4, Pallas kernels, run_transform(): pl.pallas_call(kernel, out_shape=jax.ShapeDtypeStruct(data.shape, jnp.flo...  118 us
    unnamed x125, local copies, waits for them, and re-layouts  85 us
    ppermute x2, waiting for transfers between devices, body(): high = lax.ppermute(blended[:, :, :HALO], 'line', backward_pairs)  68.1 us
    reshape x4, local copies, waits for them, and re-layouts, body(): spec = forward_transform(ext.reshape(2, -1, p_len, q_len), p_len, q_len)  67.9 us
    ppermute x2, waiting for transfers between devices, body(): low = lax.ppermute(blended[:, :, rows - HALO:], 'line', forward_pairs)  66.2 us
    all_to_all x1, waiting for transfers between devices, body(): data = lax.all_to_all(data, 'line', split_axis=2, concat_axis=3, tiled=True)  46.6 us
    add x2, other arithmetic, body(): blended = latest + momenta[iteration] * (latest - earlier)  39.2 us
  transfers between devices with their start and end apart: 7, of which 4 were waited for; matrix products, arithmetic and copies ran while one was open for 17% of the time, Pallas kernels for 3%

profile of v2, /device:TPU:21, one launch (start us, length us, event | category | flops | bytes accessed | tf_op | source)
XLA Modules:
  0.0 899.6 jit_solution(12894249064538290372)
XLA Ops:
  0.6 16.5 %fusion.1 = f32[2,8,8,16384]{3,1,2,0:T(8,128)S(1)} fusion(f32[2,8,8,16384]{3,2,1,0:T(8,128)} %param.24, f32[2,8,8,16384]{3,2,1,0:T(8,128)} %param.23), kind=kLoop, calls=%fused_computation.10 | loop fusion | flops 6291456 | bytes 25165824 | tf_op jit(solution)/shard_map/add | solution.py:269
  17.1 3.4 copy-done.2
  20.5 3.6 fusion.44
  24.1 3.4 collective-permute-start
  27.5 3.1 collective-permute-start.1
  31.1 150.0 %all_gather.3 = s32[2,16384]{1,0:T(2,128)S(1)} all-gather(s32[2,1024]{1,0:T(2,128)S(1)} %pad_add_fusion), channel_id=1, replica_groups=mesh['line'=16,'chan'=2] {'line'}, dimensions={1}, use_global_device_ids=true | all-gather | bytes 139264 | tf_op jit(solution)/shard_map/all_gather | solution.py:240
  182.9 17.5 %fusion.10 = (f32[1,8,128,1024]{3,1,0,2:T(8,128)S(1)}, f32[1,8,128,1024]{3,1,0,2:T(8,128)S(1)}) fusion(f32[1,8,128,1024]{3,2,1,0:T(8,128)S(1)} %get-tuple-element.47, f32[1,8,128,1024]{3,2,1,0:T(8,128)S(1)} %get-tuple-element.46, f32[8,1024]{1,0:T(8,128)S(1)} %copy-done.37, f32[128,1024]{1,0:T(8,128)S(1)} %copy-done.36, f32[8]{0:T(128)S(1)} %select_reduce_fusion), kind=kLoop, calls=%fused_computation.27 | loop fusion | flops 9437184 | bytes 17334304 | tf_op jit(solution)/shard_map/mul | solution.py:236
  202.1 10.9 %add_multiply_fusion = f32[2,8,128,1024]{3,1,0,2:T(8,128)} fusion(f32[2,8,128,1024]{3,1,0,2:T(8,128)S(1)} %pad_maximum_fusion.2, f32[1024]{0:T(1024)S(1)} %get-tuple-element.68, f32[1024]{0:T(1024)S(1)} %get-tuple-element.69, f32[1024]{0:T(1024)S(1)} %get-tuple-element.70, f32[1024]{0:T(1024)S(1)} %get-tuple-element.71, f32[1024]{0:T(1024)S(1)} %get-tuple-element.72, ...), kind=kLoop, calls=%fused_computation.14 | loop fusion | flops 33554432 | bytes 16809984 | tf_op jit(solution)/shard_map/mul | solution.py:239
  212.9 14.0 %all-to-all-start = ((f32[2,8,128,1024]{3,1,0,2:T(8,128)}), f32[2,8,128,1024]{3,1,0,2:T(8,128)}, u32[]{:S(2)}, u32[]{:S(2)}) async-start(f32[2,8,128,1024]{3,1,0,2:T(8,128)} %add_multiply_fusion), calls=%async_computation | async-start | bytes 16777216 | tf_op jit(solution)/shard_map/all_to_all | solution.py:242
  230.7 10.4 %pad_maximum_fusion = f32[2,8,14,16384]{3,1,2,0:T(8,128)} fusion(f32[2,8,3,16384]{3,1,2,0:T(8,128)} %collective-permute-done.1, f32[2,8,8,16384]{3,1,2,0:T(8,128)} %copy-done.2, f32[2,8,3,16384]{3,1,2,0:T(8,128)} %collective-permute-done), kind=kLoop, calls=%fused_computation | loop fusion | flops 7340032 | bytes 29360128 | tf_op jit(solution)/shard_map/concatenate | solution.py:272
  241.1 19.5 %copy.153 = f32[2,8,14,16384]{3,2,1,0:T(8,128)} copy(f32[2,8,14,16384]{3,1,2,0:T(8,128)} %pad_maximum_fusion) | data formatting | bytes 29360128 | tf_op jit(solution)/shard_map/reshape | solution.py:274
  260.7 14.4 %reshape.157.x_ref = f32[2,112,128,128]{3,2,1,0:T(8,128)} reshape(f32[2,8,14,16384]{3,2,1,0:T(8,128)} %copy.153) | data formatting | bytes 29360128 | tf_op jit(solution)/shard_map/reshape | solution.py:274
  275.1 29.2 %shard_map.221 = f32[2,112,128,128]{3,2,1,0:T(8,128)} custom-call(f32[2,112,128,128]{3,2,1,0:T(8,128)} %reshape.157.x_ref, f32[256,256]{1,0:T(8,128)} %constant.123.clone.w_ref.v_ref, f32[256,256]{1,0:T(8,128)} %constant.124.clone.v_ref.w_ref, f32[2,128,128]{2,1,0:T(8,128)} %constant.125.clone.t_ref), custom_call_target="tpu_custom_call" | custom-call | flops 3758096384 | bytes 29360128 | tf_op jit(solution)/shard_map/pallas_call | solution.py:164
  304.3 9.6 %fusion.42 = (f32[2,8,1,128,128]{4,3,2,1,0:T(8,128)S(1)}, f32[2,8,1,128,128]{4,3,2,1,0:T(8,128)}, f32[2,8,1,128,128]{4,3,2,1,0:T(8,128)}, f32[2,8,1,128,128]{4,3...) fusion(f32[2,8,14,128,128]{4,3,2,1,0:T(8,128)} %bitcast.148), kind=kLoop, calls=%fused_computation.157 | loop fusion | bytes 29360128 | tf_op jit(solution)/shard_map/slice | solution.py:278
  317.5 2.5 copy.163
  320.0 2.5 copy.168
  322.5 2.5 copy.161
  325.0 2.5 copy.169
  327.6 2.5 copy.159
  330.1 2.6 copy.170
  332.7 2.5 copy.160
  335.2 2.5 copy.171
  337.8 2.6 copy.162
  340.3 2.5 copy.164
  342.9 5.4 subtract_dynamic-update-slice_fusion.13
  348.3 2.1 subtract_dynamic-update-slice_fusion.12
  357.8 2.1 subtract_dynamic-update-slice_fusion.8
  361.9 46.6 %all-to-all-done = f32[2,8,128,1024]{3,1,0,2:T(8,128)} async-done(((f32[2,8,128,1024]{3,1,0,2:T(8,128)}), f32[2,8,128,1024]{3,1,0,2:T(8,128)}, u32[]{:S(2)}, u32[]{:S(2)}) %all-to-all-start) | async-done | bytes 8388640 | tf_op jit(solution)/shard_map/all_to_all | solution.py:242
  408.5 11.6 %copy.210 = f32[2,8,16,8,1024]{4,2,3,1,0:T(8,128)} copy(f32[2,8,16,8,1024]{4,1,0,3,2:T(8,128)} %bitcast.36) | data formatting | bytes 16777216 | tf_op jit(solution)/shard_map/all_to_all | solution.py:242
  420.1 9.3 %reshape.150 = f32[2,8,8,128,128]{4,3,2,1,0:T(8,128)} reshape(f32[2,8,8,16,1024]{4,3,2,1,0:T(8,128)} %bitcast.150) | data formatting | bytes 16777216 | tf_op jit(solution)/shard_map/reshape | solution.py:243
  429.4 12.3 %bitcast_subtract_fusion.1 = f32[2,8,8,128,128]{3,4,2,1,0:T(8,128)} fusion(f32[2,8,8,128,128]{4,3,2,1,0:T(8,128)} %reshape.150, f32[2,8,8,128,128]{3,4,2,1,0:T(8,128)} %subtract_dynamic-update-slice_fusion.7, f32[8]{0:T(128)S(1)} %multiply_multiply_fusion), kind=kLoop, calls=%fused_computation.4 | loop fusion | flops 4194304 | bytes 25165856 | tf_op jit(solution)/shard_map/sub | solution.py:323
  441.6 8.7 copy.130
  450.4 29.5 %shard_map.222 = f32[2,64,128,128]{3,2,1,0:T(8,128)} custom-call(f32[2,64,128,128]{3,2,1,0:T(8,128)} %bitcast.151, f32[256,256]{1,0:T(8,128)} %constant.123.clone.w_ref.v_ref, f32[256,256]{1,0:T(8,128)} %constant.124.clone.v_ref.w_ref, f32[2,128,128]{2,1,0:T(8,128)} %constant.126.clone.t_ref), custom_call_target="tpu_custom_call" | custom-call | flops 2147483648 | bytes 16777216 | tf_op jit(solution)/shard_map/pallas_call | solution.py:164
  479.9 9.8 %reshape.152 = f32[2,8,8,16384]{3,2,1,0:T(8,128)} reshape(f32[2,64,128,128]{3,2,1,0:T(8,128)} %shard_map.222) | data formatting | bytes 16777216 | tf_op jit(solution)/shard_map/reshape | solution.py:325
  489.7 11.7 %multiply_reduce_fusion.1 = f32[8,16384]{1,0:T(8,128)S(1)} fusion(f32[2,8,8,16384]{3,1,2,0:T(8,128)} %copy-done.2, f32[2,8,8,16384]{3,2,1,0:T(8,128)} %reshape.152), kind=kLoop, calls=%fused_computation.13 | loop fusion | flops 6160384 | bytes 17301504 | tf_op jit(solution)/shard_map/reduce_sum | solution.py:326
  504.7 22.8 %multiply_add_fusion = (f32[2,8,8,16384]{3,1,2,0:T(8,128)S(1)}, f32[2,8,8,16384]{3,1,2,0:T(8,128)}) fusion(f32[2,8,8,16384]{3,2,1,0:T(8,128)} %param.23, f32[8,16384]{1,0:T(8,128)S(1)} %maximum_divide_fusion.1, f32[2,8,8,16384]{3,1,2,0:T(8,128)} %copy-done.2, f32[2,8,8,16384]{3,2,1,0:T(8,128)} %reshape.152), kind=kLoop, calls=%fused_computation.12 | loop fusion | flops 10485760 | bytes 42467328 | tf_op jit(solution)/shard_map/add | solution.py:269
  529.8 4.6 collective-permute-start.4
  534.5 66.2 %collective-permute-done.3 = f32[2,8,3,16384]{3,1,2,0:T(8,128)S(1)} collective-permute-done((f32[2,8,3,16384]{3,1,2,0:T(8,128)S(1)}, f32[2,8,3,16384]{3,1,2,0:T(8,128)S(1)}, u32[]{:S(2)}, u32[]{:S(2)}) %collective-permute-start.3) | collective-permute-done | bytes 3145760 | tf_op jit(solution)/shard_map/ppermute | solution.py:270
  600.7 68.1 %collective-permute-done.4 = f32[2,8,3,16384]{3,1,2,0:T(8,128)S(1)} collective-permute-done((f32[2,8,3,16384]{3,1,2,0:T(8,128)S(1)}, f32[2,8,3,16384]{3,1,2,0:T(8,128)S(1)}, u32[]{:S(2)}, u32[]{:S(2)}) %collective-permute-start.4) | collective-permute-done | bytes 3145760 | tf_op jit(solution)/shard_map/ppermute | solution.py:271
  668.8 5.6 pad_maximum_fusion.1
  674.4 19.5 %copy.154 = f32[2,8,14,16384]{3,2,1,0:T(8,128)} copy(f32[2,8,14,16384]{3,1,2,0:T(8,128)} %pad_maximum_fusion.1) | data formatting | bytes 29360128 | tf_op jit(solution)/shard_map/reshape | solution.py:274
  693.9 14.4 %reshape.158.x_ref = f32[2,112,128,128]{3,2,1,0:T(8,128)} reshape(f32[2,8,14,16384]{3,2,1,0:T(8,128)} %copy.154) | data formatting | bytes 29360128 | tf_op jit(solution)/shard_map/reshape | solution.py:274
  708.3 29.5 %shard_map.223 = f32[2,112,128,128]{3,2,1,0:T(8,128)} custom-call(f32[2,112,128,128]{3,2,1,0:T(8,128)} %reshape.158.x_ref, f32[256,256]{1,0:T(8,128)} %constant.123.clone.w_ref.v_ref, f32[256,256]{1,0:T(8,128)} %constant.124.clone.v_ref.w_ref, f32[2,128,128]{2,1,0:T(8,128)} %constant.125.clone.t_ref), custom_call_target="tpu_custom_call" | custom-call | flops 3758096384 | bytes 29360128 | tf_op jit(solution)/shard_map/pallas_call | solution.py:164
  737.9 9.6 %fusion.41 = (f32[2,8,1,128,128]{4,3,2,1,0:T(8,128)S(1)}, f32[2,8,1,128,128]{4,3,2,1,0:T(8,128)}, f32[2,8,1,128,128]{4,3,2,1,0:T(8,128)}, f32[2,8,1,128,128]{4,3...) fusion(f32[2,8,14,128,128]{4,3,2,1,0:T(8,128)} %bitcast.147), kind=kLoop, calls=%fused_computation.156 | loop fusion | bytes 29360128 | tf_op jit(solution)/shard_map/slice | solution.py:278
  751.0 2.5 copy.177
  753.6 2.5 copy.182
  756.1 2.5 copy.175
  758.6 2.5 copy.183
  761.2 2.6 copy.173
  763.8 2.6 copy.184
  766.3 2.5 copy.174
  768.9 2.5 copy.185
  771.4 2.5 copy.176
  774.0 2.5 copy.178
  776.5 5.3 subtract_dynamic-update-slice_fusion.6
  781.9 2.1 subtract_dynamic-update-slice_fusion.5
  795.4 12.1 %bitcast_subtract_fusion = f32[2,8,8,128,128]{3,4,2,1,0:T(8,128)} fusion(f32[2,8,8,128,128]{4,3,2,1,0:T(8,128)} %reshape.150, f32[2,8,8,128,128]{3,4,2,1,0:T(8,128)} %subtract_dynamic-update-slice_fusion, f32[8]{0:T(128)S(1)} %multiply_multiply_fusion), kind=kLoop, calls=%fused_computation.3 | loop fusion | flops 4194304 | bytes 25165856 | tf_op jit(solution)/shard_map/sub | solution.py:323
  807.5 8.7 copy.149
  816.2 29.5 %shard_map.224 = f32[2,64,128,128]{3,2,1,0:T(8,128)} custom-call(f32[2,64,128,128]{3,2,1,0:T(8,128)} %bitcast.149, f32[256,256]{1,0:T(8,128)} %constant.123.clone.w_ref.v_ref, f32[256,256]{1,0:T(8,128)} %constant.124.clone.v_ref.w_ref, f32[2,128,128]{2,1,0:T(8,128)} %constant.126.clone.t_ref), custom_call_target="tpu_custom_call" | custom-call | flops 2147483648 | bytes 16777216 | tf_op jit(solution)/shard_map/pallas_call | solution.py:164
  845.7 9.4 %reshape.156 = f32[2,8,8,16384]{3,2,1,0:T(8,128)} reshape(f32[2,64,128,128]{3,2,1,0:T(8,128)} %shard_map.224) | data formatting | bytes 16777216 | tf_op jit(solution)/shard_map/reshape | solution.py:325
  855.1 11.8 %multiply_reduce_fusion = f32[8,16384]{1,0:T(8,128)S(1)} fusion(f32[2,8,8,16384]{3,1,2,0:T(8,128)} %copy-done.3, f32[2,8,8,16384]{3,2,1,0:T(8,128)} %reshape.156), kind=kLoop, calls=%fused_computation.11 | loop fusion | flops 6160384 | bytes 17301504 | tf_op jit(solution)/shard_map/reduce_sum | solution.py:326
  867.9 11.8 %copy.152 = f32[2,8,8,16384]{3,2,1,0:T(8,128)} copy(f32[2,8,8,16384]{3,1,2,0:T(8,128)} %get-tuple-element.11) | data formatting | bytes 16777216
  879.9 7.7 broadcast_multiply_fusion
  887.7 11.6 %copy.151 = f32[2,8,8,16384]{3,2,1,0:T(8,128)} copy(f32[2,8,8,16384]{3,1,2,0:T(8,128)} %broadcast_multiply_fusion) | data formatting | bytes 16777216
  (140 shorter events, 42.3 us)
Async XLA Ops:
  0.6 30.0 %copy-start = (f32[16,4]{0,1:T(4,128)S(1)}, f32[16,4]{0,1:T(4,128)}, u32[]{:S(2)}) copy-start(f32[16,4]{0,1:T(4,128)} %param.29) | copy-start | bytes 772
  17.1 3.4 copy-start.2
  20.5 10.1 %copy-start.39 = (s32[1024]{0:T(1024)S(1)}, s32[1024]{0:T(1024)}, u32[]{:S(2)}) copy-start(s32[1024]{0:T(1024)} %param.28) | copy-start | bytes 12292
  20.5 10.6 %copy-start.38 = (s32[1024]{0:T(1024)S(1)}, s32[1024]{0:T(1024)}, u32[]{:S(2)}) copy-start(s32[1024]{0:T(1024)} %param.27) | copy-start | bytes 12292
  20.5 160.6 %copy-start.23 = (f32[2,8,128,1024]{3,2,1,0:T(8,128)S(1)}, f32[2,8,128,1024]{3,2,1,0:T(8,128)}, u32[]{:S(2)}) copy-start(f32[2,8,128,1024]{3,2,1,0:T(8,128)} %param.22) | copy-start | bytes 25165828
  24.1 206.6 %collective-permute-start = (f32[2,8,3,16384]{3,1,2,0:T(8,128)}, f32[2,8,3,16384]{3,1,2,0:T(8,128)}, u32[]{:S(2)}, u32[]{:S(2)}) collective-permute-start(f32[2,8,3,16384]{3,1,2,0:T(8,128)} %get-tuple-element.44), channel_id=1, source_target_pairs={{0,2},{2,4},{4,6},{6,8},{8,10},{10,12},{12,14},{14,16},{16,18},{18... | collective-permute-start | bytes 9437192 | tf_op jit(solution)/shard_map/ppermute | solution.py:270
  27.5 203.2 %collective-permute-start.1 = (f32[2,8,3,16384]{3,1,2,0:T(8,128)}, f32[2,8,3,16384]{3,1,2,0:T(8,128)}, u32[]{:S(2)}, u32[]{:S(2)}) collective-permute-start(f32[2,8,3,16384]{3,1,2,0:T(8,128)} %get-tuple-element.45), channel_id=1, source_target_pairs={{2,0},{4,2},{6,4},{8,6},{10,8},{12,10},{14,12},{16,14},{18,16},{20... | collective-permute-start | bytes 9437192 | tf_op jit(solution)/shard_map/ppermute | solution.py:271
  181.1 1.7 copy-start.40
  181.1 1.7 copy-start.41
  181.1 1.8 copy-start.36
  181.1 1.8 copy-start.37
  212.9 195.5 %all-to-all-start = ((f32[2,8,128,1024]{3,1,0,2:T(8,128)}), f32[2,8,128,1024]{3,1,0,2:T(8,128)}, u32[]{:S(2)}, u32[]{:S(2)}) async-start(f32[2,8,128,1024]{3,1,0,2:T(8,128)} %add_multiply_fusion), calls=%async_computation | async-start | bytes 16777216 | tf_op jit(solution)/shard_map/all_to_all | solution.py:242
  342.9 5.4 copy-start.6
  342.9 5.4 copy-start.10
  342.9 5.4 copy-start.14
  342.9 5.4 copy-start.17
  342.9 5.4 copy-start.21
  342.9 5.4 copy-start.24
  342.9 5.4 copy-start.26
  348.3 4.0 copy-start.8
  350.4 3.8 copy-start.12
  352.4 3.6 copy-start.16
  352.4 3.6 copy-start.30
  352.4 3.6 copy-start.32
  352.4 3.6 copy-start.34
  354.3 3.6 copy-start.20
  356.0 4.0 copy-start.29
  501.3 3.1 collective-permute-start.2
  527.4 141.3 %copy-start.3 = (f32[2,8,8,16384]{3,1,2,0:T(8,128)}, f32[2,8,8,16384]{3,1,2,0:T(8,128)S(1)}, u32[]{:S(2)}) copy-start(f32[2,8,8,16384]{3,1,2,0:T(8,128)S(1)} %get-tuple-element.10) | copy-start | bytes 25165828
  527.9 72.8 %collective-permute-start.3 = (f32[2,8,3,16384]{3,1,2,0:T(8,128)S(1)}, f32[2,8,3,16384]{3,1,2,0:T(8,128)S(1)}, u32[]{:S(2)}, u32[]{:S(2)}) collective-permute-start(f32[2,8,3,16384]{3,1,2,0:T(8,128)S(1)} %get-tuple-element.42), channel_id=1, source_target_pairs={{0,2},{2,4},{4,6},{6,8},{8,10},{10,12},{12,14},{14,16},{16,18},{18... | collective-permute-start | bytes 9437192 | tf_op jit(solution)/shard_map/ppermute | solution.py:270
  529.8 139.0 %collective-permute-start.4 = (f32[2,8,3,16384]{3,1,2,0:T(8,128)S(1)}, f32[2,8,3,16384]{3,1,2,0:T(8,128)S(1)}, u32[]{:S(2)}, u32[]{:S(2)}) collective-permute-start(f32[2,8,3,16384]{3,1,2,0:T(8,128)S(1)} %get-tuple-element.43), channel_id=1, source_target_pairs={{2,0},{4,2},{6,4},{8,6},{10,8},{12,10},{14,12},{16,14},{18,16},{20... | collective-permute-start | bytes 9437192 | tf_op jit(solution)/shard_map/ppermute | solution.py:271
  776.5 5.4 copy-start.5
  776.5 5.4 copy-start.9
  776.5 5.4 copy-start.13
  776.5 5.4 copy-start.18
  776.5 5.4 copy-start.22
  776.5 5.4 copy-start.25
  776.5 5.4 copy-start.27
  781.9 4.0 copy-start.7
  784.0 3.8 copy-start.11
  785.9 3.6 copy-start.15
  785.9 3.6 copy-start.31
  785.9 3.6 copy-start.33
  785.9 3.6 copy-start.35
  787.9 3.6 copy-start.19
  789.6 3.9 copy-start.28
  855.1 24.8 %slice-start = ((s8[8388608]{0:T(1024)(128)(4,1)}), s8[4194304]{0:T(1024)(128)(4,1)S(1)}, s32[]{:S(2)}) async-start(s8[8388608]{0:T(1024)(128)(4,1)} %bitcast.145), calls=%async_computation.1 | async-start | bytes 8388608
  866.9 12.7 %collective-permute-start.5 = (f32[8,16384]{1,0:T(8,128)S(1)}, f32[8,16384]{1,0:T(8,128)S(1)}, u32[]{:S(2)}, u32[]{:S(2)}) collective-permute-start(f32[8,16384]{1,0:T(8,128)S(1)} %multiply_reduce_fusion), channel_id=1, source_target_pairs={{0,1},{1,0},{2,3},{3,2},{4,5},{5,4},{6,7},{7,6},{8,9},{9,8},{10,11... | collective-permute-start | bytes 1572872 | tf_op jit(solution)/shard_map/ppermute | solution.py:328
  867.9 12.0 %slice-start.1 = ((s8[8388608]{0:T(1024)(128)(4,1)}), s8[4194304]{0:T(1024)(128)(4,1)S(1)}, s32[]{:S(2)}) async-start(s8[8388608]{0:T(1024)(128)(4,1)} %bitcast.145), calls=%async_computation.2 | async-start | bytes 8388608
  867.9 12.0 %copy-start.4 = (f32[2,8,8,16384]{3,2,1,0:T(8,128)S(1)}, f32[2,8,8,16384]{3,2,1,0:T(8,128)}, u32[]{:S(2)}) copy-start(f32[2,8,8,16384]{3,2,1,0:T(8,128)} %reshape.156) | copy-start | bytes 25165828
  879.9 19.4 %copy-start.1 = (f32[16,4]{0,1:T(4,128)S(1)}, f32[16,4]{0,1:T(4,128)}, u32[]{:S(2)}) copy-start(f32[16,4]{0,1:T(4,128)} %param.29) | copy-start | bytes 772

commit v3 on v2

--- a/solution.py
+++ b/solution.py
@@ -148,6 +148,24 @@
     for b in range(nb):
         o_ref[0, b] = out[:p_len, b * q_len : (b + 1) * q_len]
         o_ref[1, b] = out[p_len:, b * q_len : (b + 1) * q_len]
+
+
+def transpose_kernel(x_ref, o_ref):
+    for b in range(x_ref.shape[0]):
+        o_ref[b] = x_ref[b].T
+
+
+def swap_minor(x):
+    total, p_len, q_len = x.shape
+    nb = block_count(total)
+    return pl.pallas_call(
+        transpose_kernel,
+        out_shape=jax.ShapeDtypeStruct((total, q_len, p_len), x.dtype),
+        grid=(total // nb,),
+        in_specs=[pl.BlockSpec((nb, p_len, q_len), lambda i: (i, 0, 0))],
+        out_specs=pl.BlockSpec((nb, q_len, p_len), lambda i: (i, 0, 0)),
+        cost_estimate=pl.CostEstimate(flops=0, bytes_accessed=2 * x.size * 4, transcendentals=0),
+    )(x)
 
 
 def block_count(total):
@@ -237,13 +255,19 @@
     back_i = gain * (cos_a * observed[1] - sin_a * observed[0])
     data = adjoint_shift(jnp.stack([back_r, back_i]), local_weights)
     data = data * (step_length / math.sqrt(na))
-    packed = lax.all_gather(jnp.stack([tap_index, range_offset]), "line", axis=1, tiled=True)
-    packed, data = lax.optimization_barrier((packed, data))
-    data = lax.all_to_all(data, "line", split_axis=2, concat_axis=3, tiled=True)
-    data = data.reshape(2, cl, rows, q_len, p_len).swapaxes(-1, -2)
-
-    taps = tap_table(packed[0], kernel_table)
-    weights = shift_weights(packed[1], taps)
+    extra = jnp.stack(
+        [
+            jnp.broadcast_to(tap_index.astype(jnp.float32)[None, :], data.shape[2:]),
+            jnp.broadcast_to(range_offset.astype(jnp.float32)[None, :], data.shape[2:]),
+        ]
+    )[:, None]
+    payload = jnp.concatenate([data, extra], axis=1)
+    payload = lax.all_to_all(payload, "line", split_axis=2, concat_axis=3, tiled=True)
+    data = swap_minor(payload[:, :cl].reshape(-1, q_len, p_len)).reshape(2, cl, rows, p_len, q_len)
+    all_taps = payload[0, cl, 0].astype(jnp.int32)
+    all_offsets = payload[1, cl, 0].astype(jnp.int32)
+    taps = tap_table(all_taps, kernel_table)
+    weights = shift_weights(all_offsets, taps)
 
     def spectral(v):
         return v.reshape(v.shape[:-1] + (q_len, p_len)).swapaxes(-1, -2)
@@ -255,8 +279,8 @@
     coef = (channel_gain * channel_gain) * (step_length / na)
 
     momenta = momentum_weights()
-    earlier = previous_image
-    latest = current_image
+    earlier = previous_image.reshape(2, cl, rows, p_len, q_len)
+    latest = current_image.reshape(2, cl, rows, p_len, q_len)
     forward_pairs = [(i, i + 1) for i in range(lines - 1)]
     backward_pairs = [(i + 1, i) for i in range(lines - 1)]
     first = (me == 0)
@@ -269,13 +293,18 @@
         blended = latest + momenta[iteration] * (latest - earlier)
         low = lax.ppermute(blended[:, :, rows - HALO :], "line", forward_pairs)
         high = lax.ppermute(blended[:, :, :HALO], "line", backward_pairs)
-        ext = jnp.concatenate([low, blended, high], axis=2)
-        ext_rows = rows + 2 * HALO
-        spec = forward_transform(ext.reshape(2, -1, p_len, q_len), p_len, q_len)
-        spec = spec.reshape(2, cl, ext_rows, p_len, q_len)
+        own = forward_transform(blended.reshape(2, -1, p_len, q_len), p_len, q_len)
+        own = own.reshape(2, cl, rows, p_len, q_len)
+        rim = jnp.concatenate([low, high], axis=2)
+        rim = forward_transform(rim.reshape(2, -1, p_len, q_len), p_len, q_len)
+        rim = rim.reshape(2, cl, 2 * HALO, p_len, q_len)
 
         def at(r):
-            return spec[:, :, r]
+            if r < HALO:
+                return rim[:, :, r]
+            if r < HALO + rows:
+                return own[:, :, r - HALO]
+            return rim[:, :, r - rows]
 
         gram = []
         for r in range(rows):
@@ -331,7 +360,7 @@
         factor = shrink(squares)
         earlier = latest
         latest = shifted * factor[None, None]
-    return (latest, earlier)
+    return (latest.reshape(current_image.shape), earlier.reshape(current_image.shape))
 
 
 def solution(mesh):

time: 909 us -> 968 us (1.065)
  waiting for transfers between devices: 182 us -> 469 us
  local copies, waits for them, and re-layouts: 236 us -> 79.8 us
  blocking collectives: 150 us -> 0 us
  other arithmetic: 181 us -> 220 us
  starting transfers between devices: 29.5 us -> 56.8 us
  Pallas kernels: 118 us -> 135 us
    ppermute x2, waiting for transfers between devices: 66.2 us -> 253 us  [body(): low = lax.ppermute(blended[:, :, rows - HALO:], 'line', forward_pairs)]
    all_gather x1 -> x0, blocking collectives: 150 us -> none  [body(): lax.all_gather(jnp.stack([tap_index, range_offset]), 'line', axis=1, tile...]
    ppermute x2, waiting for transfers between devices: 68.1 us -> 206 us  [body(): high = lax.ppermute(blended[:, :, :HALO], 'line', backward_pairs)]
    reshape x5 -> x0, local copies, waits for them, and re-layouts: 77.2 us -> none  [the longest x4 67.9 us: body(): spec = forward_transform(ext.reshape(2, -1, p_len, q_len), p_len, q_len)]
    unnamed x125 -> x55, local copies, waits for them, and re-layouts: 85 us -> 25.8 us
    all_to_all x1, waiting for transfers between devices: 46.6 us -> 9.21 us  [body(): lax.all_to_all(payload, 'line', split_axis=2, concat_axis=3, tiled=True)]
    ppermute x2, starting transfers between devices: 5.29 us -> 40.9 us  [body(): low = lax.ppermute(blended[:, :, rows - HALO:], 'line', forward_pairs)]
    sub x2 -> x0, local copies, waits for them, and re-layouts: 17.5 us -> none  [body(): resid = coef[None, :, None, None, None] * gram - data]
  transfers between devices with their start and end apart: 7 -> 7, of which waited for: 4 -> 6; matrix products, arithmetic and copies ran while one was open for 17% -> 7% of each run, Pallas kernels for 3% -> 5%
where the time goes in v3:
time: 968 us; the launch traced here: 964 us
  waiting for transfers between devices  469 us (48%)
  other arithmetic  220 us (23%)
  Pallas kernels  135 us (14%)
  local copies, waits for them, and re-layouts  79.8 us (8%)
  starting transfers between devices  56.8 us (6%)
    ppermute x2, waiting for transfers between devices, body(): low = lax.ppermute(blended[:, :, rows - HALO:], 'line', forward_pairs)  253 us
    ppermute x2, waiting for transfers between devices, body(): high = lax.ppermute(blended[:, :, :HALO], 'line', backward_pairs)  206 us
    pallas_call x6, Pallas kernels, run_transform(): pl.pallas_call(kernel, out_shape=jax.ShapeDtypeStruct(data.shape, jnp.flo...  122 us
    ppermute x2, starting transfers between devices, body(): low = lax.ppermute(blended[:, :, rows - HALO:], 'line', forward_pairs)  40.9 us
    add x4, other arithmetic, body(): blended = latest + momenta[iteration] * (latest - earlier)  40.4 us
    unnamed x29, other arithmetic  37.2 us
    reduce_sum x4, other arithmetic, body(): squares = jnp.sum(shifted * shifted, axis=(0, 1))  29.8 us
    unnamed x55, local copies, waits for them, and re-layouts  25.8 us
  transfers between devices with their start and end apart: 7, of which 6 were waited for; matrix products, arithmetic and copies ran while one was open for 7% of the time, Pallas kernels for 5%

profile of v3, /device:TPU:21, one launch (start us, length us, event | category | flops | bytes accessed | tf_op | source)
XLA Modules:
  0.0 963.8 jit_solution(7480117129763390449)
XLA Ops:
  2.2 1.1 copy.84
  3.4 4.4 fusion.39
  8.3 17.7 %fusion.14 = (f32[1,8,128,1024]{3,1,0,2:T(8,128)S(1)}, f32[1,8,128,1024]{3,1,0,2:T(8,128)S(1)}) fusion(f32[1,8,128,1024]{3,2,1,0:T(8,128)S(1)} %get-tuple-element.64, f32[1,8,128,1024]{3,2,1,0:T(8,128)S(1)} %get-tuple-element.63, f32[8,1024]{1,0:T(8,128)S(1)} %copy-done.6, f32[128,1024]{1,0:T(8,128)S(1)} %copy-done.5, f32[8]{0:T(128)S(1)} %select_reduce_fusion), kind=kLoop, calls=%fused_computation.33 | loop fusion | flops 9437184 | bytes 17334304 | tf_op jit(solution)/shard_map/mul | solution.py:254
  26.0 1.7 pad_maximum_fusion.1
  27.7 10.7 %add_multiply_fusion = f32[2,8,128,1024]{3,1,0,2:T(8,128)} fusion(f32[2,8,128,1024]{3,1,0,2:T(8,128)S(1)} %pad_maximum_fusion.1, f32[1024]{0:T(1024)S(1)} %get-tuple-element.81, f32[1024]{0:T(1024)S(1)} %get-tuple-element.82, f32[1024]{0:T(1024)S(1)} %get-tuple-element.83, f32[1024]{0:T(1024)S(1)} %get-tuple-element.84, f32[1024]{0:T(1024)S(1)} %get-tuple-element.85, ...), kind=kLoop, calls=%fused_computation.18 | loop fusion | flops 33554432 | bytes 16809984 | tf_op jit(solution)/shard_map/mul | solution.py:257
  38.4 12.3 %pad_maximum_fusion = f32[2,9,128,1024]{3,1,0,2:T(8,128)} fusion(f32[2,1,128,1024]{3,1,0,2:T(1,128)S(1)} %copy.84, f32[2,8,128,1024]{3,1,0,2:T(8,128)} %add_multiply_fusion), kind=kLoop, calls=%fused_computation | loop fusion | flops 2359296 | bytes 18874368 | tf_op jit(solution)/shard_map/concatenate | solution.py:264
  50.7 6.5 all-to-all-start
  57.2 10.0 %fusion.5 = f32[2,8,8,128,128]{4,3,2,1,0:T(8,128)S(1)} fusion(f32[2,8,8,128,128]{4,2,3,1,0:T(8,128)} %bitcast.186, f32[2,8,8,128,128]{4,2,3,1,0:T(8,128)} %bitcast.189), kind=kLoop, calls=%fused_computation.10 | loop fusion | flops 6291456 | bytes 25165824 | tf_op jit(solution)/shard_map/add | solution.py:293
  67.2 2.1 fusion.38
  69.3 3.2 collective-permute-start.1
  72.5 2.7 collective-permute-start
  75.2 8.4 copy.104
  83.6 4.7 copy.103
  88.5 11.9 %fusion.1.x_ref = f32[2,64,128,128]{3,2,1,0:T(8,128)} fusion(f32[2,64,128,128]{3,2,1,0:T(8,128)} %bitcast.220, f32[2,64,128,128]{3,2,1,0:T(8,128)} %bitcast.195), kind=kLoop, calls=%fused_computation.3 | loop fusion | flops 6291456 | bytes 25165824 | tf_op jit(solution)/shard_map/add | solution.py:293
  100.3 17.6 %shard_map.275 = f32[2,64,128,128]{3,2,1,0:T(8,128)} custom-call(f32[2,64,128,128]{3,2,1,0:T(8,128)} %fusion.1.x_ref, f32[256,256]{1,0:T(8,128)} %constant.123.clone.w_ref.v_ref, f32[256,256]{1,0:T(8,128)} %constant.124.clone.v_ref.w_ref, f32[2,128,128]{2,1,0:T(8,128)} %constant.125.clone.t_ref), custom_call_target="tpu_custom_call" | custom-call | flops 2147483648 | bytes 16777216 | tf_op jit(solution)/shard_map/pallas_call | solution.py:182
  117.9 94.5 %collective-permute-done.1 = f32[2,8,3,128,128]{4,3,2,1,0:T(8,128)} collective-permute-done((f32[2,8,3,128,128]{4,3,2,1,0:T(8,128)}, f32[2,8,3,128,128]{4,3,2,1,0:T(8,128)}, u32[]{:S(2)}, u32[]{:S(2)}) %collective-permute-start.1) | collective-permute-done | bytes 3145760 | tf_op jit(solution)/shard_map/ppermute | solution.py:295
  212.5 202.1 %collective-permute-done = f32[2,8,3,128,128]{4,3,2,1,0:T(8,128)} collective-permute-done((f32[2,8,3,128,128]{4,3,2,1,0:T(8,128)S(1)}, f32[2,8,3,128,128]{4,3,2,1,0:T(8,128)}, u32[]{:S(2)}, u32[]{:S(2)}) %collective-permute-start) | collective-permute-done | bytes 3145760 | tf_op jit(solution)/shard_map/ppermute | solution.py:294
  414.6 6.3 pad_maximum_fusion.2
  420.9 14.0 %shard_map.276 = f32[2,48,128,128]{3,2,1,0:T(8,128)} custom-call(f32[2,48,128,128]{3,2,1,0:T(8,128)} %bitcast.224, f32[256,256]{1,0:T(8,128)} %constant.123.clone.w_ref.v_ref, f32[256,256]{1,0:T(8,128)} %constant.124.clone.v_ref.w_ref, f32[2,128,128]{2,1,0:T(8,128)} %constant.125.clone.t_ref), custom_call_target="tpu_custom_call" | custom-call | flops 1610612736 | bytes 12582912 | tf_op jit(solution)/shard_map/pallas_call | solution.py:182
  435.0 9.2 all-to-all-done
  444.2 14.8 %copy.85 = f32[2,9,8,16,1024]{4,2,3,1,0:T(8,128)} copy(f32[2,9,8,16,1024]{4,1,0,2,3:T(8,128)} %bitcast.6) | data formatting | bytes 18874368 | tf_op jit(solution)/shard_map/all_to_all | solution.py:265
  459.0 4.0 slice.210
  462.9 1.1 slice_convert_fusion.1
  464.0 7.7 compare_reduce_fusion
  471.7 4.9 copy.105
  476.6 13.1 %shard_map.277 = f32[128,128,128]{2,1,0:T(8,128)} custom-call(f32[128,128,128]{2,1,0:T(8,128)} %bitcast.222), custom_call_target="tpu_custom_call" | custom-call | bytes 16777216 | tf_op jit(solution)/shard_map/pallas_call | solution.py:161
  491.7 4.6 fusion.32
  496.3 4.5 subtract_dynamic-update-slice_fusion.9
  500.8 2.3 subtract_dynamic-update-slice_fusion.8
  503.1 0.9 subtract_dynamic-update-slice_fusion.7
  504.9 3.4 copy-done.3
  508.6 5.2 subtract_dynamic-update-slice_fusion.6
  513.8 5.2 subtract_dynamic-update-slice_fusion.5
  519.0 1.9 fusion.28
  521.0 12.1 %multiply_subtract_fusion.1.y_ref = f32[2,64,128,128]{3,2,1,0:T(8,128)} fusion(f32[2,64,128,128]{3,2,1,0:T(8,128)} %bitcast.199, f32[2,64,128,128]{3,2,1,0:T(8,128)} %bitcast.228, f32[64]{0:T(128)S(1)} %mul.805), kind=kLoop, calls=%fused_computation.17 | loop fusion | flops 4194304 | bytes 25166080 | tf_op jit(solution)/shard_map/sub | solution.py:352
  533.1 29.6 %shard_map.278 = f32[2,64,128,128]{3,2,1,0:T(8,128)} custom-call(f32[2,64,128,128]{3,2,1,0:T(8,128)} %multiply_subtract_fusion.1.y_ref, f32[256,256]{1,0:T(8,128)} %constant.123.clone.w_ref.v_ref, f32[256,256]{1,0:T(8,128)} %constant.124.clone.v_ref.w_ref, f32[2,128,128]{2,1,0:T(8,128)} %constant.126.clone.t_ref), custom_call_target="tpu_custom_call" | custom-call | flops 2147483648 | bytes 16777216 | tf_op jit(solution)/shard_map/pallas_call | solution.py:182
  562.7 14.6 %multiply_reduce_fusion.1 = (f32[64,128,128]{2,1,0:T(8,128)}, f32[2,64,128,128]{3,2,1,0:T(8,128)}) fusion(f32[2,64,128,128]{3,2,1,0:T(8,128)} %fusion.1.x_ref, f32[2,64,128,128]{3,2,1,0:T(8,128)} %shard_map.278), kind=kLoop, calls=%fused_computation.15 | loop fusion | flops 5242880 | bytes 29360128 | tf_op jit(solution)/shard_map/reduce_sum | solution.py:355
  577.3 2.5 reduce_sum.44
  579.8 1.5 collective-permute-start.2
  581.3 1.5 collective-permute-done.2
  583.1 13.8 %multiply_add_fusion = f32[2,8,8,128,128]{4,3,2,1,0:T(8,128)} fusion(f32[2,8,8,128,128]{4,3,2,1,0:T(8,128)} %bitcast.194, f32[2,8,8,128,128]{4,2,3,1,0:T(8,128)} %bitcast.190, f32[8,128,128]{2,1,0:T(8,128)S(1)} %maximum_divide_fusion, f32[2,8,8,128,128]{4,2,3,1,0:T(8,128)} %bitcast.188), kind=kLoop, calls=%fused_computation.14 | loop fusion | flops 16777216 | bytes 34078720 | tf_op jit(solution)/shard_map/add | solution.py:293
  596.9 7.2 fusion.37
  604.1 3.4 collective-permute-start.4
  607.5 38.3 %collective-permute-start.3 = (f32[2,8,3,128,128]{4,3,2,1,0:T(8,128)}, f32[2,8,3,128,128]{4,3,2,1,0:T(8,128)}, u32[]{:S(2)}, u32[]{:S(2)}) collective-permute-start(f32[2,8,3,128,128]{4,3,2,1,0:T(8,128)} %get-tuple-element.59), channel_id=1, source_target_pairs={{0,2},{2,4},{4,6},{6,8},{8,10},{10,12},{12,14},{14,16},{16,18},{18... | collective-permute-start | bytes 9437192 | tf_op jit(solution)/shard_map/ppermute | solution.py:294
  646.4 4.8 fusion.3.x_ref
  651.1 17.6 %shard_map.279 = f32[2,64,128,128]{3,2,1,0:T(8,128)} custom-call(f32[2,64,128,128]{3,2,1,0:T(8,128)} %fusion.3.x_ref, f32[256,256]{1,0:T(8,128)} %constant.123.clone.w_ref.v_ref, f32[256,256]{1,0:T(8,128)} %constant.124.clone.v_ref.w_ref, f32[2,128,128]{2,1,0:T(8,128)} %constant.125.clone.t_ref), custom_call_target="tpu_custom_call" | custom-call | flops 2147483648 | bytes 16777216 | tf_op jit(solution)/shard_map/pallas_call | solution.py:182
  668.7 111.0 %collective-permute-done.4 = f32[2,8,3,128,128]{4,3,2,1,0:T(8,128)} collective-permute-done((f32[2,8,3,128,128]{4,3,2,1,0:T(8,128)}, f32[2,8,3,128,128]{4,3,2,1,0:T(8,128)}, u32[]{:S(2)}, u32[]{:S(2)}) %collective-permute-start.4) | collective-permute-done | bytes 3145760 | tf_op jit(solution)/shard_map/ppermute | solution.py:295
  779.8 50.8 %collective-permute-done.3 = f32[2,8,3,128,128]{4,3,2,1,0:T(8,128)} collective-permute-done((f32[2,8,3,128,128]{4,3,2,1,0:T(8,128)}, f32[2,8,3,128,128]{4,3,2,1,0:T(8,128)}, u32[]{:S(2)}, u32[]{:S(2)}) %collective-permute-start.3) | collective-permute-done | bytes 3145760 | tf_op jit(solution)/shard_map/ppermute | solution.py:294
  830.6 6.3 pad_maximum_fusion.3
  836.9 13.8 %shard_map.280 = f32[2,48,128,128]{3,2,1,0:T(8,128)} custom-call(f32[2,48,128,128]{3,2,1,0:T(8,128)} %bitcast.223, f32[256,256]{1,0:T(8,128)} %constant.123.clone.w_ref.v_ref, f32[256,256]{1,0:T(8,128)} %constant.124.clone.v_ref.w_ref, f32[2,128,128]{2,1,0:T(8,128)} %constant.125.clone.t_ref), custom_call_target="tpu_custom_call" | custom-call | flops 1610612736 | bytes 12582912 | tf_op jit(solution)/shard_map/pallas_call | solution.py:182
  850.7 4.6 fusion.24
  855.6 4.1 subtract_dynamic-update-slice_fusion.4
  859.9 1.0 subtract_dynamic-update-slice_fusion.3
  860.9 0.9 subtract_dynamic-update-slice_fusion.2
  864.5 1.0 fusion.20
  865.5 3.2 copy-done.4
  868.7 12.1 %multiply_subtract_fusion.y_ref = f32[2,64,128,128]{3,2,1,0:T(8,128)} fusion(f32[2,64,128,128]{3,2,1,0:T(8,128)} %bitcast.200, f32[2,64,128,128]{3,2,1,0:T(8,128)} %bitcast.229, f32[64]{0:T(128)S(1)} %mul.805), kind=kLoop, calls=%fused_computation.13 | loop fusion | flops 4194304 | bytes 25166080 | tf_op jit(solution)/shard_map/sub | solution.py:352
  880.8 29.7 %shard_map.281 = f32[2,64,128,128]{3,2,1,0:T(8,128)} custom-call(f32[2,64,128,128]{3,2,1,0:T(8,128)} %multiply_subtract_fusion.y_ref, f32[256,256]{1,0:T(8,128)} %constant.123.clone.w_ref.v_ref, f32[256,256]{1,0:T(8,128)} %constant.124.clone.v_ref.w_ref, f32[2,128,128]{2,1,0:T(8,128)} %constant.126.clone.t_ref), custom_call_target="tpu_custom_call" | custom-call | flops 2147483648 | bytes 16777216 | tf_op jit(solution)/shard_map/pallas_call | solution.py:182
  910.5 10.3 %multiply_reduce_fusion = f32[64,128,128]{2,1,0:T(8,128)} fusion(f32[2,64,128,128]{3,2,1,0:T(8,128)} %fusion.3.x_ref, f32[2,64,128,128]{3,2,1,0:T(8,128)} %shard_map.281), kind=kLoop, calls=%fused_computation.11 | loop fusion | flops 5242880 | bytes 20971520 | tf_op jit(solution)/shard_map/reduce_sum | solution.py:355
  920.8 2.5 reduce_sum.47
  923.3 1.3 collective-permute-start.5
  924.6 9.4 reshape.822
  934.2 9.4 reshape.827
  944.2 19.2 %subtract_multiply_fusion = (f32[2,8,8,16384]{3,2,1,0:T(8,128)}, f32[2,8,8,16384]{3,2,1,0:T(8,128)}) fusion(f32[2,8,8,16384]{3,2,1,0:T(8,128)} %reshape.827, f32[2,8,8,16384]{3,2,1,0:T(8,128)} %param.29, f32[8,16384]{1,0:T(8,128)S(1)} %bitcast.264, f32[8,16384]{1,0:T(8,128)S(1)} %bitcast.263, f32[2,8,8,16384]{3,2,1,0:T(8,128)} %reshape.822, ...), kind=kLoop, calls=%fused_computation.12 | loop fusion | flops 20971520 | bytes 51380224 | tf_op jit(solution)/shard_map/mul | solution.py:362
  (99 shorter events, 10.1 us)
Async XLA Ops:
  0.6 7.1 copy-start
  3.3 4.4 copy-start.8
  3.3 4.9 copy-start.9
  3.3 4.9 copy-start.10
  3.3 5.0 copy-start.5
  3.3 5.0 copy-start.6
  26.0 1.7 copy-start.7
  50.7 393.4 %all-to-all-start = ((f32[2,9,128,1024]{3,1,0,2:T(8,128)}), f32[2,9,128,1024]{3,1,0,2:T(8,128)}, u32[]{:S(2)}, u32[]{:S(2)}) async-start(f32[2,9,128,1024]{3,1,0,2:T(8,128)} %pad_maximum_fusion), calls=%async_computation | async-start | bytes 33554432 | tf_op jit(solution)/shard_map/all_to_all | solution.py:265
  67.2 16.4 %slice-start.6 = ((s8[8388608]{0:T(1024)(128)(4,1)}), s8[4194304]{0:T(1024)(128)(4,1)S(1)}, s32[]{:S(2)}) async-start(s8[8388608]{0:T(1024)(128)(4,1)} %bitcast.191), calls=%async_computation.7 | async-start | bytes 8388608
  69.3 143.1 %collective-permute-start.1 = (f32[2,8,3,128,128]{4,3,2,1,0:T(8,128)}, f32[2,8,3,128,128]{4,3,2,1,0:T(8,128)}, u32[]{:S(2)}, u32[]{:S(2)}) collective-permute-start(f32[2,8,3,128,128]{4,3,2,1,0:T(8,128)} %get-tuple-element.62), channel_id=1, source_target_pairs={{2,0},{4,2},{6,4},{8,6},{10,8},{12,10},{14,12},{16,14},{18,16},{20... | collective-permute-start | bytes 9437192 | tf_op jit(solution)/shard_map/ppermute | solution.py:295
  72.5 342.1 %collective-permute-start = (f32[2,8,3,128,128]{4,3,2,1,0:T(8,128)S(1)}, f32[2,8,3,128,128]{4,3,2,1,0:T(8,128)}, u32[]{:S(2)}, u32[]{:S(2)}) collective-permute-start(f32[2,8,3,128,128]{4,3,2,1,0:T(8,128)S(1)} %get-tuple-element.61), channel_id=1, source_target_pairs={{0,2},{2,4},{4,6},{6,8},{8,10},{10,12},{12,14},{14,16},{16,18},{18... | collective-permute-start | bytes 9437192 | tf_op jit(solution)/shard_map/ppermute | solution.py:294
  75.2 8.4 slice-start.7
  491.7 9.1 slice-start
  496.3 4.5 slice-start.1
  504.1 14.9 %slice-start.10 = ((s8[6291456]{0:T(1024)(128)(4,1)}), s8[2097152]{0:T(1024)(128)(4,1)S(1)}, s32[]{:S(2)}) async-start(s8[6291456]{0:T(1024)(128)(4,1)} %bitcast.206), calls=%async_computation.11 | async-start | bytes 4194304
  504.9 3.4 copy-start.3
  508.6 10.4 %slice-start.2 = ((s8[8388608]{0:T(1024)(128)(4,1)}), s8[4194304]{0:T(1024)(128)(4,1)S(1)}, s32[]{:S(2)}) async-start(s8[8388608]{0:T(1024)(128)(4,1)} %bitcast.173), calls=%async_computation.3 | async-start | bytes 8388608
  508.6 10.4 %slice-start.11 = ((s8[6291456]{0:T(1024)(128)(4,1)}), s8[4194304]{0:T(1024)(128)(4,1)S(1)}, s32[]{:S(2)}) async-start(s8[6291456]{0:T(1024)(128)(4,1)} %bitcast.206), calls=%async_computation.12 | async-start | bytes 8388608
  513.8 5.2 slice-start.3
  579.8 3.1 collective-permute-start.2
  583.1 63.2 %slice-start.8 = ((s8[8388608]{0:T(1024)(128)(4,1)}), s8[4194304]{0:T(1024)(128)(4,1)S(1)}, s32[]{:S(2)}) async-start(s8[8388608]{0:T(1024)(128)(4,1)} %bitcast.196), calls=%async_computation.9 | async-start | bytes 8388608
  583.1 63.2 %slice-start.12 = ((s8[8388608]{0:T(1024)(128)(4,1)}), s8[4194304]{0:T(1024)(128)(4,1)S(1)}, s32[]{:S(2)}) async-start(s8[8388608]{0:T(1024)(128)(4,1)} %bitcast.218), calls=%async_computation.13 | async-start | bytes 8388608
  583.1 63.2 %slice-start.9 = ((s8[8388608]{0:T(1024)(128)(4,1)}), s8[4194304]{0:T(1024)(128)(4,1)S(1)}, s32[]{:S(2)}) async-start(s8[8388608]{0:T(1024)(128)(4,1)} %bitcast.196), calls=%async_computation.10 | async-start | bytes 8388608
  583.1 63.2 %slice-start.13 = ((s8[8388608]{0:T(1024)(128)(4,1)}), s8[4194304]{0:T(1024)(128)(4,1)S(1)}, s32[]{:S(2)}) async-start(s8[8388608]{0:T(1024)(128)(4,1)} %bitcast.218), calls=%async_computation.14 | async-start | bytes 8388608
  604.1 175.6 %collective-permute-start.4 = (f32[2,8,3,128,128]{4,3,2,1,0:T(8,128)}, f32[2,8,3,128,128]{4,3,2,1,0:T(8,128)}, u32[]{:S(2)}, u32[]{:S(2)}) collective-permute-start(f32[2,8,3,128,128]{4,3,2,1,0:T(8,128)} %get-tuple-element.60), channel_id=1, source_target_pairs={{2,0},{4,2},{6,4},{8,6},{10,8},{12,10},{14,12},{16,14},{18,16},{20... | collective-permute-start | bytes 9437192 | tf_op jit(solution)/shard_map/ppermute | solution.py:295
  607.5 223.0 %collective-permute-start.3 = (f32[2,8,3,128,128]{4,3,2,1,0:T(8,128)}, f32[2,8,3,128,128]{4,3,2,1,0:T(8,128)}, u32[]{:S(2)}, u32[]{:S(2)}) collective-permute-start(f32[2,8,3,128,128]{4,3,2,1,0:T(8,128)} %get-tuple-element.59), channel_id=1, source_target_pairs={{0,2},{2,4},{4,6},{6,8},{8,10},{10,12},{12,14},{14,16},{16,18},{18... | collective-permute-start | bytes 9437192 | tf_op jit(solution)/shard_map/ppermute | solution.py:294
  850.7 5.0 copy-start.2
  850.7 9.0 slice-start.4
  855.6 4.2 slice-start.5
  865.4 3.2 copy-start.4
  923.3 20.3 %collective-permute-start.5 = (f32[8,128,128]{2,1,0:T(8,128)S(1)}, f32[8,128,128]{2,1,0:T(8,128)S(1)}, u32[]{:S(2)}, u32[]{:S(2)}) collective-permute-start(f32[8,128,128]{2,1,0:T(8,128)S(1)} %reduce_sum.47), channel_id=1, source_target_pairs={{0,1},{1,0},{2,3},{3,2},{4,5},{5,4},{6,7},{7,6},{8,9},{9,8},{10,11... | collective-permute-start | bytes 1572872 | tf_op jit(solution)/shard_map/ppermute | solution.py:357
  944.1 19.2 %copy-start.1 = (f32[16,4]{0,1:T(4,128)S(1)}, f32[16,4]{0,1:T(4,128)}, u32[]{:S(2)}) copy-start(f32[16,4]{0,1:T(4,128)} %param.35) | copy-start | bytes 772

commit v4 on v3

--- a/solution.py
+++ b/solution.py
@@ -245,6 +245,21 @@
         (group_of[:, None] == levels[None, :]).astype(jnp.float32) * calib_gain[None, :], axis=1
     )
 
+    momenta = momentum_weights()
+    earlier = previous_image.reshape(2, cl, rows, p_len, q_len)
+    latest = current_image.reshape(2, cl, rows, p_len, q_len)
+    forward_pairs = [(i, i + 1) for i in range(lines - 1)]
+    backward_pairs = [(i + 1, i) for i in range(lines - 1)]
+
+    packed = lax.all_gather(jnp.stack([tap_index, range_offset]), "line", axis=1, tiled=True)
+    packed, latest, earlier = lax.optimization_barrier((packed, latest, earlier))
+    taps = tap_table(packed[0], kernel_table)
+    weights = shift_weights(packed[1], taps)
+
+    blended = latest + momenta[0] * (latest - earlier)
+    low = lax.ppermute(blended[:, :, rows - HALO :], "line", forward_pairs)
+    high = lax.ppermute(blended[:, :, :HALO], "line", backward_pairs)
+
     local_taps = tap_table(tap_index, kernel_table)
     local_weights = shift_weights(range_offset, local_taps)
     angles = doppler_phase[None, :, :] + channel_ramp[:, None, :]
@@ -255,19 +270,8 @@
     back_i = gain * (cos_a * observed[1] - sin_a * observed[0])
     data = adjoint_shift(jnp.stack([back_r, back_i]), local_weights)
     data = data * (step_length / math.sqrt(na))
-    extra = jnp.stack(
-        [
-            jnp.broadcast_to(tap_index.astype(jnp.float32)[None, :], data.shape[2:]),
-            jnp.broadcast_to(range_offset.astype(jnp.float32)[None, :], data.shape[2:]),
-        ]
-    )[:, None]
-    payload = jnp.concatenate([data, extra], axis=1)
-    payload = lax.all_to_all(payload, "line", split_axis=2, concat_axis=3, tiled=True)
-    data = swap_minor(payload[:, :cl].reshape(-1, q_len, p_len)).reshape(2, cl, rows, p_len, q_len)
-    all_taps = payload[0, cl, 0].astype(jnp.int32)
-    all_offsets = payload[1, cl, 0].astype(jnp.int32)
-    taps = tap_table(all_taps, kernel_table)
-    weights = shift_weights(all_offsets, taps)
+    data, low, high = lax.optimization_barrier((data, low, high))
+    data = lax.all_to_all(data, "line", split_axis=2, concat_axis=3, tiled=True)
 
     def spectral(v):
         return v.reshape(v.shape[:-1] + (q_len, p_len)).swapaxes(-1, -2)
@@ -278,21 +282,18 @@
     ]
     coef = (channel_gain * channel_gain) * (step_length / na)
 
-    momenta = momentum_weights()
-    earlier = previous_image.reshape(2, cl, rows, p_len, q_len)
-    latest = current_image.reshape(2, cl, rows, p_len, q_len)
-    forward_pairs = [(i, i + 1) for i in range(lines - 1)]
-    backward_pairs = [(i + 1, i) for i in range(lines - 1)]
     first = (me == 0)
     last = (me == lines - 1)
 
     def wgt(d):
         return weights[d - LOWEST]
 
+    undo = None
     for iteration in range(ITERS):
-        blended = latest + momenta[iteration] * (latest - earlier)
-        low = lax.ppermute(blended[:, :, rows - HALO :], "line", forward_pairs)
-        high = lax.ppermute(blended[:, :, :HALO], "line", backward_pairs)
+        if iteration > 0:
+            blended = latest + momenta[iteration] * (latest - earlier)
+            low = lax.ppermute(blended[:, :, rows - HALO :], "line", forward_pairs)
+            high = lax.ppermute(blended[:, :, :HALO], "line", backward_pairs)
         own = forward_transform(blended.reshape(2, -1, p_len, q_len), p_len, q_len)
         own = own.reshape(2, cl, rows, p_len, q_len)
         rim = jnp.concatenate([low, high], axis=2)
@@ -349,9 +350,13 @@
             r = rows - 1 + tt
             gram[r] = gram[r] - jnp.where(last, high_fix[idx], 0.0)
         gram = jnp.stack(gram, axis=2)
-        resid = coef[None, :, None, None, None] * gram - data
+        resid = coef[None, :, None, None, None] * gram
         grad = inverse_transform(resid.reshape(2, -1, p_len, q_len), p_len, q_len)
-        shifted = blended - grad.reshape(blended.shape)
+        if undo is None:
+            undo = swap_minor(data.reshape(-1, q_len, p_len))
+            undo = inverse_transform(undo.reshape(2, -1, p_len, q_len), p_len, q_len)
+            undo = undo.reshape(blended.shape)
+        shifted = blended - grad.reshape(blended.shape) + undo
         squares = jnp.sum(shifted * shifted, axis=(0, 1))
         if chans == 2:
             squares = squares + lax.ppermute(squares, "chan", [(0, 1), (1, 0)])

time: 968 us -> 741 us (0.77)
  waiting for transfers between devices: 469 us -> 302 us
  other arithmetic: 220 us -> 150 us
  Pallas kernels: 135 us -> 166 us
  starting transfers between devices: 56.8 us -> 27.3 us
  blocking collectives: 0 us -> 23 us
  local copies, waits for them, and re-layouts: 79.8 us -> 59 us
    ppermute x2, waiting for transfers between devices: 253 us -> 48.9 us  [body(): low = lax.ppermute(blended[:, :, rows - HALO:], 'line', forward_pairs)]
    all_to_all x1, waiting for transfers between devices: 9.21 us -> 90.9 us  [body(): data = lax.all_to_all(data, 'line', split_axis=2, concat_axis=3, tiled=True)]
    ppermute x2, waiting for transfers between devices: 206 us -> 161 us  [body(): high = lax.ppermute(blended[:, :, :HALO], 'line', backward_pairs)]
    ppermute x2, starting transfers between devices: 40.9 us -> 6.21 us  [body(): low = lax.ppermute(blended[:, :, rows - HALO:], 'line', forward_pairs)]
    pallas_call x6 -> x7, Pallas kernels: 122 us -> 153 us  [run_transform(): pl.pallas_call(kernel, out_shape=jax.ShapeDtypeStruct(data.shape, jnp.flo...]
    sub x2 -> x0, other arithmetic: 24.2 us -> none  [body(): resid = coef[None, :, None, None, None] * gram - data]
    all_gather x0 -> x1, blocking collectives: none -> 23 us  [body(): lax.all_gather(jnp.stack([tap_index, range_offset]), 'line', axis=1, tile...]
    add x4 -> x1, other arithmetic: 40.4 us -> 18.6 us  [body(): blended = latest + momenta[iteration] * (latest - earlier)]
  transfers between devices with their start and end apart: 7 -> 7, of which waited for: 6 -> 5; matrix products, arithmetic and copies ran while one was open for 7% -> 10% of each run, Pallas kernels for 5% -> 11%
where the time goes in v4:
time: 741 us; the launch traced here: 729 us
  waiting for transfers between devices  302 us (41%)
  Pallas kernels  166 us (22%)
  other arithmetic  150 us (20%)
  local copies, waits for them, and re-layouts  59 us (8%)
  starting transfers between devices  27.3 us (4%)
  blocking collectives  23 us (3%)
    ppermute x2, waiting for transfers between devices, body(): high = lax.ppermute(blended[:, :, :HALO], 'line', backward_pairs)  161 us
    pallas_call x7, Pallas kernels, run_transform(): pl.pallas_call(kernel, out_shape=jax.ShapeDtypeStruct(data.shape, jnp.flo...  153 us
    all_to_all x1, waiting for transfers between devices, body(): data = lax.all_to_all(data, 'line', split_axis=2, concat_axis=3, tiled=True)  90.9 us
    ppermute x2, waiting for transfers between devices, body(): low = lax.ppermute(blended[:, :, rows - HALO:], 'line', forward_pairs)  48.9 us
    unnamed x16, other arithmetic  26 us
    all_gather x1, blocking collectives, body(): lax.all_gather(jnp.stack([tap_index, range_offset]), 'line', axis=1, tile...  23 us
    reduce_sum x2, other arithmetic, body(): squares = jnp.sum(shifted * shifted, axis=(0, 1))  22.2 us
    add x1, other arithmetic, body(): blended = latest + momenta[iteration] * (latest - earlier)  18.6 us
  transfers between devices with their start and end apart: 7, of which 5 were waited for; matrix products, arithmetic and copies ran while one was open for 10% of the time, Pallas kernels for 11%

profile of v4, /device:TPU:21, one launch (start us, length us, event | category | flops | bytes accessed | tf_op | source)
XLA Modules:
  0.0 729.5 jit_solution(8516295267476799113)
XLA Ops:
  0.6 0.7 pad_add_fusion
  1.4 23.0 %all_gather.3 = s32[2,16384]{1,0:T(2,128)S(1)} all-gather(s32[2,1024]{1,0:T(2,128)S(1)} %pad_add_fusion), channel_id=1, replica_groups=mesh['line'=16,'chan'=2] {'line'}, dimensions={1}, use_global_device_ids=true | all-gather | bytes 139264 | tf_op jit(solution)/shard_map/all_gather | solution.py:254
  24.3 10.0 %fusion.1 = f32[2,8,8,128,128]{4,3,2,1,0:T(8,128)S(1)} fusion(f32[2,8,8,128,128]{4,2,3,1,0:T(8,128)} %bitcast.204, f32[2,8,8,128,128]{4,2,3,1,0:T(8,128)} %bitcast.196), kind=kLoop, calls=%fused_computation.4 | loop fusion | flops 6291456 | bytes 25165824 | tf_op jit(solution)/shard_map/add | solution.py:259
  34.3 3.3 copy-done.2
  37.6 3.1 fusion.58
  40.7 2.7 collective-permute-start.1
  43.4 3.2 collective-permute-start
  46.6 0.4 fusion.31
  47.2 0.4 fusion.29
  47.6 0.4 multiply_add_fusion.13
  48.7 4.4 fusion.59
  53.1 18.4 %fusion.10 = (f32[1,8,128,1024]{3,1,0,2:T(8,128)S(1)}, f32[1,8,128,1024]{3,1,0,2:T(8,128)}) fusion(f32[1,8,128,1024]{3,2,1,0:T(8,128)S(1)} %get-tuple-element.23, f32[1,8,128,1024]{3,2,1,0:T(8,128)S(1)} %get-tuple-element.22, f32[8,1024]{1,0:T(8,128)S(1)} %copy-done.6, f32[128,1024]{1,0:T(8,128)S(1)} %copy-done.5, f32[8]{0:T(128)S(1)} %select_reduce_fusion), kind=kLoop, calls=%fused_computation.25 | loop fusion | flops 9437184 | bytes 17334304 | tf_op jit(solution)/shard_map/mul | solution.py:269
  71.5 3.7 pad_maximum_fusion
  75.2 10.5 %add_multiply_fusion = f32[2,8,128,1024]{3,1,0,2:T(8,128)} fusion(f32[2,8,128,1024]{3,1,0,2:T(8,128)S(1)} %pad_maximum_fusion, f32[1024]{0:T(1024)S(1)} %get-tuple-element.44, f32[1024]{0:T(1024)S(1)} %get-tuple-element.45, f32[1024]{0:T(1024)S(1)} %get-tuple-element.46, f32[1024]{0:T(1024)S(1)} %get-tuple-element.47, f32[1024]{0:T(1024)S(1)} %get-tuple-element.48, ...), kind=kLoop, calls=%fused_computation.10 | loop fusion | flops 33554432 | bytes 16809984 | tf_op jit(solution)/shard_map/mul | solution.py:272
  85.7 91.6 %collective-permute-done.1 = f32[2,8,3,128,128]{4,3,2,1,0:T(8,128)} collective-permute-done((f32[2,8,3,128,128]{4,3,2,1,0:T(8,128)}, f32[2,8,3,128,128]{4,3,2,1,0:T(8,128)}, u32[]{:S(2)}, u32[]{:S(2)}) %collective-permute-start.1) | collective-permute-done | bytes 3145760 | tf_op jit(solution)/shard_map/ppermute | solution.py:261
  177.3 12.8 %all-to-all-start = ((f32[2,8,128,1024]{3,1,0,2:T(8,128)}), f32[2,8,128,1024]{3,1,0,2:T(8,128)}, u32[]{:S(2)}, u32[]{:S(2)}) async-start(f32[2,8,128,1024]{3,1,0,2:T(8,128)} %add_multiply_fusion), calls=%async_computation | async-start | bytes 16777216 | tf_op jit(solution)/shard_map/all_to_all | solution.py:274
  190.1 0.7 fusion.56
  190.9 0.7 fusion.50
  191.6 0.6 fusion.47
  193.0 17.6 %shard_map.302 = f32[2,64,128,128]{3,2,1,0:T(8,128)} custom-call(f32[2,64,128,128]{3,2,1,0:T(8,128)} %bitcast.178, f32[256,256]{1,0:T(8,128)} %constant.123.clone.w_ref.v_ref, f32[256,256]{1,0:T(8,128)} %constant.124.clone.v_ref.w_ref, f32[2,128,128]{2,1,0:T(8,128)} %constant.125.clone.t_ref), custom_call_target="tpu_custom_call" | custom-call | flops 2147483648 | bytes 16777216 | tf_op jit(solution)/shard_map/pallas_call | solution.py:182
  210.7 6.3 pad_maximum_fusion.1
  217.0 14.0 %shard_map.303 = f32[2,48,128,128]{3,2,1,0:T(8,128)} custom-call(f32[2,48,128,128]{3,2,1,0:T(8,128)} %bitcast.201, f32[256,256]{1,0:T(8,128)} %constant.123.clone.w_ref.v_ref, f32[256,256]{1,0:T(8,128)} %constant.124.clone.v_ref.w_ref, f32[2,128,128]{2,1,0:T(8,128)} %constant.125.clone.t_ref), custom_call_target="tpu_custom_call" | custom-call | flops 1610612736 | bytes 12582912 | tf_op jit(solution)/shard_map/pallas_call | solution.py:182
  231.0 4.6 fusion.28
  236.0 4.1 subtract_dynamic-update-slice_fusion.9
  240.2 1.0 subtract_dynamic-update-slice_fusion.8
  241.2 0.9 subtract_dynamic-update-slice_fusion.7
  242.1 0.7 add_dynamic-update-slice_fusion.1
  242.8 0.9 subtract_dynamic-update-slice_fusion.6
  243.7 0.9 subtract_dynamic-update-slice_fusion.5
  244.6 0.9 fusion.24
  245.5 4.4 broadcast_multiply_fusion.3.y_ref
  249.9 30.0 %shard_map.304 = f32[2,64,128,128]{3,2,1,0:T(8,128)} custom-call(f32[2,64,128,128]{3,2,1,0:T(8,128)} %broadcast_multiply_fusion.3.y_ref, f32[256,256]{1,0:T(8,128)} %constant.123.clone.w_ref.v_ref, f32[256,256]{1,0:T(8,128)} %constant.124.clone.v_ref.w_ref, f32[2,128,128]{2,1,0:T(8,128)} %constant.126.clone.t_ref), custom_call_target="tpu_custom_call" | custom-call | flops 2147483648 | bytes 16777216 | tf_op jit(solution)/shard_map/pallas_call | solution.py:182
  279.9 90.9 %all-to-all-done = f32[2,8,128,1024]{3,1,0,2:T(8,128)} async-done(((f32[2,8,128,1024]{3,1,0,2:T(8,128)}), f32[2,8,128,1024]{3,1,0,2:T(8,128)}, u32[]{:S(2)}, u32[]{:S(2)}) %all-to-all-start) | async-done | bytes 8388640 | tf_op jit(solution)/shard_map/all_to_all | solution.py:274
  370.7 11.6 %copy.108 = f32[2,8,16,8,1024]{4,2,3,1,0:T(8,128)} copy(f32[2,8,16,8,1024]{4,1,0,3,2:T(8,128)} %bitcast.43) | data formatting | bytes 16777216 | tf_op jit(solution)/shard_map/all_to_all | solution.py:274
  382.4 9.2 %reshape.185.x_ref = f32[128,128,128]{2,1,0:T(8,128)} reshape(f32[2,8,8,16,1024]{4,3,2,1,0:T(8,128)} %bitcast.198) | data formatting | bytes 16777216 | tf_op jit(solution)/shard_map/reshape | solution.py:356
  391.6 13.1 %shard_map.305 = f32[128,128,128]{2,1,0:T(8,128)} custom-call(f32[128,128,128]{2,1,0:T(8,128)} %reshape.185.x_ref), custom_call_target="tpu_custom_call" | custom-call | bytes 16777216 | tf_op jit(solution)/shard_map/pallas_call | solution.py:161
  404.8 29.5 %shard_map.306 = f32[2,64,128,128]{3,2,1,0:T(8,128)} custom-call(f32[2,64,128,128]{3,2,1,0:T(8,128)} %bitcast.199, f32[256,256]{1,0:T(8,128)} %constant.123.clone.w_ref.v_ref, f32[256,256]{1,0:T(8,128)} %constant.124.clone.v_ref.w_ref, f32[2,128,128]{2,1,0:T(8,128)} %constant.126.clone.t_ref), custom_call_target="tpu_custom_call" | custom-call | flops 2147483648 | bytes 16777216 | tf_op jit(solution)/shard_map/pallas_call | solution.py:182
  434.2 11.1 %multiply_reduce_fusion.1 = f32[8,128,128]{2,1,0:T(8,128)S(1)} fusion(f32[2,8,8,128,128]{4,3,2,1,0:T(8,128)} %bitcast.174, f32[2,8,8,128,128]{4,3,2,1,0:T(8,128)} %copy-done.2, f32[2,8,8,128,128]{4,3,2,1,0:T(8,128)} %bitcast.180), kind=kLoop, calls=%fused_computation.8 | loop fusion | flops 8257536 | bytes 25690112 | tf_op jit(solution)/shard_map/reduce_sum | solution.py:360
  445.3 1.5 collective-permute-start.2
  446.9 1.5 collective-permute-done.2
  448.6 18.6 %multiply_add_fusion = (f32[2,8,8,128,128]{4,3,2,1,0:T(8,128)}, f32[2,8,8,128,128]{4,3,2,1,0:T(8,128)}) fusion(f32[2,8,8,128,128]{4,2,3,1,0:T(8,128)} %bitcast.197, f32[8,128,128]{2,1,0:T(8,128)S(1)} %maximum_divide_fusion.1, f32[2,8,8,128,128]{4,3,2,1,0:T(8,128)} %bitcast.175, f32[2,8,8,128,128]{4,3,2,1,0:T(8,128)} %copy-done.2, ...), kind=kLoop, calls=%fused_computation.7 | loop fusion | flops 12582912 | bytes 50855936 | tf_op jit(solution)/shard_map/add | solution.py:294
  467.2 6.3 fusion.57
  473.5 3.0 collective-permute-start.3
  476.5 3.5 collective-permute-start.4
  480.0 17.6 %shard_map.307 = f32[2,64,128,128]{3,2,1,0:T(8,128)} custom-call(f32[2,64,128,128]{3,2,1,0:T(8,128)} %bitcast.179, f32[256,256]{1,0:T(8,128)} %constant.123.clone.w_ref.v_ref, f32[256,256]{1,0:T(8,128)} %constant.124.clone.v_ref.w_ref, f32[2,128,128]{2,1,0:T(8,128)} %constant.125.clone.t_ref), custom_call_target="tpu_custom_call" | custom-call | flops 2147483648 | bytes 16777216 | tf_op jit(solution)/shard_map/pallas_call | solution.py:182
  497.7 48.9 %collective-permute-done.3 = f32[2,8,3,128,128]{4,3,2,1,0:T(8,128)} collective-permute-done((f32[2,8,3,128,128]{4,3,2,1,0:T(8,128)}, f32[2,8,3,128,128]{4,3,2,1,0:T(8,128)}, u32[]{:S(2)}, u32[]{:S(2)}) %collective-permute-start.3) | collective-permute-done | bytes 3145760 | tf_op jit(solution)/shard_map/ppermute | solution.py:295
  546.6 69.2 %collective-permute-done.4 = f32[2,8,3,128,128]{4,3,2,1,0:T(8,128)} collective-permute-done((f32[2,8,3,128,128]{4,3,2,1,0:T(8,128)}, f32[2,8,3,128,128]{4,3,2,1,0:T(8,128)}, u32[]{:S(2)}, u32[]{:S(2)}) %collective-permute-start.4) | collective-permute-done | bytes 3145760 | tf_op jit(solution)/shard_map/ppermute | solution.py:296
  615.8 6.3 pad_maximum_fusion.2
  622.1 14.0 %shard_map.308 = f32[2,48,128,128]{3,2,1,0:T(8,128)} custom-call(f32[2,48,128,128]{3,2,1,0:T(8,128)} %bitcast.200, f32[256,256]{1,0:T(8,128)} %constant.123.clone.w_ref.v_ref, f32[256,256]{1,0:T(8,128)} %constant.124.clone.v_ref.w_ref, f32[2,128,128]{2,1,0:T(8,128)} %constant.125.clone.t_ref), custom_call_target="tpu_custom_call" | custom-call | flops 1610612736 | bytes 12582912 | tf_op jit(solution)/shard_map/pallas_call | solution.py:182
  636.1 4.6 fusion.20
  641.0 4.1 subtract_dynamic-update-slice_fusion.4
  645.3 1.0 subtract_dynamic-update-slice_fusion.3
  646.2 0.9 subtract_dynamic-update-slice_fusion.2
  647.1 0.7 add_dynamic-update-slice_fusion
  647.9 0.9 subtract_dynamic-update-slice_fusion.1
  648.7 0.9 subtract_dynamic-update-slice_fusion
  649.6 0.9 fusion.16
  650.6 4.4 broadcast_multiply_fusion.2.y_ref
  655.0 29.8 %shard_map.309 = f32[2,64,128,128]{3,2,1,0:T(8,128)} custom-call(f32[2,64,128,128]{3,2,1,0:T(8,128)} %broadcast_multiply_fusion.2.y_ref, f32[256,256]{1,0:T(8,128)} %constant.123.clone.w_ref.v_ref, f32[256,256]{1,0:T(8,128)} %constant.124.clone.v_ref.w_ref, f32[2,128,128]{2,1,0:T(8,128)} %constant.126.clone.t_ref), custom_call_target="tpu_custom_call" | custom-call | flops 2147483648 | bytes 16777216 | tf_op jit(solution)/shard_map/pallas_call | solution.py:182
  684.8 11.1 %multiply_reduce_fusion = f32[8,128,128]{2,1,0:T(8,128)S(1)} fusion(f32[2,8,8,128,128]{4,3,2,1,0:T(8,128)} %bitcast.176, f32[2,8,8,128,128]{4,3,2,1,0:T(8,128)} %get-tuple-element.14, f32[2,8,8,128,128]{4,3,2,1,0:T(8,128)} %bitcast.182), kind=kLoop, calls=%fused_computation.5 | loop fusion | flops 8257536 | bytes 25690112 | tf_op jit(solution)/shard_map/reduce_sum | solution.py:360
  695.9 0.6 collective-permute-start.5
  696.4 9.4 %reshape.194 = f32[2,8,8,16384]{3,2,1,0:T(8,128)} reshape(f32[2,8,8,128,128]{4,3,2,1,0:T(8,128)} %get-tuple-element.15) | data formatting | bytes 16777216 | tf_op jit(solution)/shard_map/reshape | solution.py:368
  706.0 13.6 %broadcast_multiply_fusion = f32[2,8,8,128,128]{4,3,2,1,0:T(8,128)} fusion(f32[8,128,128]{2,1,0:T(8,128)S(1)} %maximum_divide_fusion, f32[2,8,8,128,128]{4,3,2,1,0:T(8,128)} %bitcast.177, f32[2,8,8,128,128]{4,3,2,1,0:T(8,128)} %get-tuple-element.14, f32[2,8,8,128,128]{4,3,2,1,0:T(8,128)} %bitcast.183), kind=kLoop, calls=%fused_computation.28 | loop fusion | flops 6291456 | bytes 34078720 | tf_op jit(solution)/shard_map/mul | solution.py:367
  719.7 9.4 %reshape.193 = f32[2,8,8,16384]{3,2,1,0:T(8,128)} reshape(f32[2,8,8,128,128]{4,3,2,1,0:T(8,128)} %broadcast_multiply_fusion) | data formatting | bytes 16777216 | tf_op jit(solution)/shard_map/reshape | solution.py:368
  (62 shorter events, 3.0 us)
Async XLA Ops:
  0.6 46.0 %copy-start = (f32[16,4]{0,1:T(4,128)S(1)}, f32[16,4]{0,1:T(4,128)}, u32[]{:S(2)}) copy-start(f32[16,4]{0,1:T(4,128)} %param.38) | copy-start | bytes 772
  34.3 3.3 copy-start.2
  37.6 9.0 %copy-start.8 = (s32[1024]{0:T(1024)S(1)}, s32[1024]{0:T(1024)}, u32[]{:S(2)}) copy-start(s32[1024]{0:T(1024)} %param.37) | copy-start | bytes 12292
  37.6 10.4 %copy-start.9 = (f32[4]{0:T(128)S(1)}, f32[4]{0:T(128)}, u32[]{:S(2)}) copy-start(f32[4]{0:T(128)} %param.40) | copy-start | bytes 52
  37.6 10.4 %copy-start.10 = (s32[8]{0:T(128)S(1)}, s32[8]{0:T(128)}, u32[]{:S(2)}) copy-start(s32[8]{0:T(128)} %param.39) | copy-start | bytes 100
  37.6 10.5 %copy-start.7 = (s32[1024]{0:T(1024)S(1)}, s32[1024]{0:T(1024)}, u32[]{:S(2)}) copy-start(s32[1024]{0:T(1024)} %param.36) | copy-start | bytes 12292
  40.7 136.6 %collective-permute-start.1 = (f32[2,8,3,128,128]{4,3,2,1,0:T(8,128)}, f32[2,8,3,128,128]{4,3,2,1,0:T(8,128)}, u32[]{:S(2)}, u32[]{:S(2)}) collective-permute-start(f32[2,8,3,128,128]{4,3,2,1,0:T(8,128)} %get-tuple-element.20), channel_id=1, source_target_pairs={{2,0},{4,2},{6,4},{8,6},{10,8},{12,10},{14,12},{16,14},{18,16},{20... | collective-permute-start | bytes 9437192 | tf_op jit(solution)/shard_map/ppermute | solution.py:261
  43.4 133.9 %collective-permute-start = (f32[2,8,3,128,128]{4,3,2,1,0:T(8,128)}, f32[2,8,3,128,128]{4,3,2,1,0:T(8,128)}, u32[]{:S(2)}, u32[]{:S(2)}) collective-permute-start(f32[2,8,3,128,128]{4,3,2,1,0:T(8,128)} %get-tuple-element.21), channel_id=1, source_target_pairs={{0,2},{2,4},{4,6},{6,8},{8,10},{10,12},{12,14},{14,16},{16,18},{18... | collective-permute-start | bytes 9437192 | tf_op jit(solution)/shard_map/ppermute | solution.py:260
  48.7 4.4 copy-start.5
  48.7 4.4 copy-start.6
  177.3 193.5 %all-to-all-start = ((f32[2,8,128,1024]{3,1,0,2:T(8,128)}), f32[2,8,128,1024]{3,1,0,2:T(8,128)}, u32[]{:S(2)}, u32[]{:S(2)}) async-start(f32[2,8,128,1024]{3,1,0,2:T(8,128)} %add_multiply_fusion), calls=%async_computation | async-start | bytes 16777216 | tf_op jit(solution)/shard_map/all_to_all | solution.py:274
  231.0 5.0 copy-start.4
  231.0 9.0 %slice-start.2 = ((s8[8388608]{0:T(1024)(128)(4,1)}), s8[4194304]{0:T(1024)(128)(4,1)S(1)}, s32[]{:S(2)}) async-start(s8[8388608]{0:T(1024)(128)(4,1)} %bitcast.166), calls=%async_computation.3 | async-start | bytes 8388608
  236.0 4.2 slice-start.3
  445.3 3.1 collective-permute-start.2
  473.5 73.1 %collective-permute-start.3 = (f32[2,8,3,128,128]{4,3,2,1,0:T(8,128)}, f32[2,8,3,128,128]{4,3,2,1,0:T(8,128)}, u32[]{:S(2)}, u32[]{:S(2)}) collective-permute-start(f32[2,8,3,128,128]{4,3,2,1,0:T(8,128)} %get-tuple-element.18), channel_id=1, source_target_pairs={{0,2},{2,4},{4,6},{6,8},{8,10},{10,12},{12,14},{14,16},{16,18},{18... | collective-permute-start | bytes 9437192 | tf_op jit(solution)/shard_map/ppermute | solution.py:295
  476.5 139.3 %collective-permute-start.4 = (f32[2,8,3,128,128]{4,3,2,1,0:T(8,128)}, f32[2,8,3,128,128]{4,3,2,1,0:T(8,128)}, u32[]{:S(2)}, u32[]{:S(2)}) collective-permute-start(f32[2,8,3,128,128]{4,3,2,1,0:T(8,128)} %get-tuple-element.19), channel_id=1, source_target_pairs={{2,0},{4,2},{6,4},{8,6},{10,8},{12,10},{14,12},{16,14},{18,16},{20... | collective-permute-start | bytes 9437192 | tf_op jit(solution)/shard_map/ppermute | solution.py:296
  636.1 5.0 copy-start.3
  636.1 9.0 %slice-start = ((s8[8388608]{0:T(1024)(128)(4,1)}), s8[4194304]{0:T(1024)(128)(4,1)S(1)}, s32[]{:S(2)}) async-start(s8[8388608]{0:T(1024)(128)(4,1)} %bitcast.156), calls=%async_computation.1 | async-start | bytes 8388608
  641.0 4.2 slice-start.1
  695.9 9.9 %collective-permute-start.5 = (f32[8,128,128]{2,1,0:T(8,128)S(1)}, f32[8,128,128]{2,1,0:T(8,128)S(1)}, u32[]{:S(2)}, u32[]{:S(2)}) collective-permute-start(f32[8,128,128]{2,1,0:T(8,128)S(1)} %multiply_reduce_fusion), channel_id=1, source_target_pairs={{0,1},{1,0},{2,3},{3,2},{4,5},{5,4},{6,7},{7,6},{8,9},{9,8},{10,11... | collective-permute-start | bytes 1572872 | tf_op jit(solution)/shard_map/ppermute | solution.py:362
  706.0 23.0 %copy-start.1 = (f32[16,4]{0,1:T(4,128)S(1)}, f32[16,4]{0,1:T(4,128)}, u32[]{:S(2)}) copy-start(f32[16,4]{0,1:T(4,128)} %param.38) | copy-start | bytes 772

commit v5 on v4

--- a/solution.py
+++ b/solution.py
@@ -246,19 +246,23 @@
     )
 
     momenta = momentum_weights()
+    forward_pairs = [(i, i + 1) for i in range(lines - 1)]
+    backward_pairs = [(i + 1, i) for i in range(lines - 1)]
+
+    def edge_blend(lo, hi):
+        cur = current_image[:, :, lo:hi]
+        return cur + momenta[0] * (cur - previous_image[:, :, lo:hi])
+
+    low = lax.ppermute(edge_blend(rows - HALO, rows), "line", forward_pairs)
+    high = lax.ppermute(edge_blend(0, HALO), "line", backward_pairs)
+
+    table = jnp.stack([tap_index, range_offset])
+    table = jnp.broadcast_to(table[None], (lines,) + table.shape)
+    table = lax.all_to_all(table, "line", split_axis=0, concat_axis=2, tiled=True)[0]
+
     earlier = previous_image.reshape(2, cl, rows, p_len, q_len)
     latest = current_image.reshape(2, cl, rows, p_len, q_len)
-    forward_pairs = [(i, i + 1) for i in range(lines - 1)]
-    backward_pairs = [(i + 1, i) for i in range(lines - 1)]
-
-    packed = lax.all_gather(jnp.stack([tap_index, range_offset]), "line", axis=1, tiled=True)
-    packed, latest, earlier = lax.optimization_barrier((packed, latest, earlier))
-    taps = tap_table(packed[0], kernel_table)
-    weights = shift_weights(packed[1], taps)
-
     blended = latest + momenta[0] * (latest - earlier)
-    low = lax.ppermute(blended[:, :, rows - HALO :], "line", forward_pairs)
-    high = lax.ppermute(blended[:, :, :HALO], "line", backward_pairs)
 
     local_taps = tap_table(tap_index, kernel_table)
     local_weights = shift_weights(range_offset, local_taps)
@@ -270,8 +274,11 @@
     back_i = gain * (cos_a * observed[1] - sin_a * observed[0])
     data = adjoint_shift(jnp.stack([back_r, back_i]), local_weights)
     data = data * (step_length / math.sqrt(na))
-    data, low, high = lax.optimization_barrier((data, low, high))
+    data, low, high, table = lax.optimization_barrier((data, low, high, table))
+    data = data.reshape(2, cl, data.shape[2], data.shape[3] // p_len, p_len)
     data = lax.all_to_all(data, "line", split_axis=2, concat_axis=3, tiled=True)
+    taps = tap_table(table[0], kernel_table)
+    weights = shift_weights(table[1], taps)
 
     def spectral(v):
         return v.reshape(v.shape[:-1] + (q_len, p_len)).swapaxes(-1, -2)
@@ -294,10 +301,15 @@
             blended = latest + momenta[iteration] * (latest - earlier)
             low = lax.ppermute(blended[:, :, rows - HALO :], "line", forward_pairs)
             high = lax.ppermute(blended[:, :, :HALO], "line", backward_pairs)
+            if iteration == ITERS - 1:
+                prior = latest.reshape(current_image.shape)
+                low, high, prior = lax.optimization_barrier((low, high, prior))
+        elif ITERS == 1:
+            prior = current_image
         own = forward_transform(blended.reshape(2, -1, p_len, q_len), p_len, q_len)
         own = own.reshape(2, cl, rows, p_len, q_len)
-        rim = jnp.concatenate([low, high], axis=2)
-        rim = forward_transform(rim.reshape(2, -1, p_len, q_len), p_len, q_len)
+        rim = jnp.concatenate([low, high], axis=2).reshape(2, -1, p_len, q_len)
+        rim = forward_transform(rim, p_len, q_len)
         rim = rim.reshape(2, cl, 2 * HALO, p_len, q_len)
 
         def at(r):
@@ -365,7 +377,7 @@
         factor = shrink(squares)
         earlier = latest
         latest = shifted * factor[None, None]
-    return (latest.reshape(current_image.shape), earlier.reshape(current_image.shape))
+    return (latest.reshape(current_image.shape), prior)
 
 
 def solution(mesh):

time: 741 us -> 744 us (level)
  waiting for transfers between devices: 302 us -> 224 us
  other arithmetic: 150 us -> 217 us
  local copies, waits for them, and re-layouts: 59 us -> 96.4 us
  blocking collectives: 23 us -> 0 us
    ppermute x2 -> x1, waiting for transfers between devices: 161 us -> 83.3 us  [body(): high = lax.ppermute(blended[:, :, :HALO], 'line', backward_pairs)]
    ppermute x2 -> x1, waiting for transfers between devices: 48.9 us -> 0.01 us  [body(): low = lax.ppermute(blended[:, :, rows - HALO:], 'line', forward_pairs)]
    ppermute x0 -> x2, waiting for transfers between devices: none -> 38.9 us  [the longest x1 38.9 us: body(): high = lax.ppermute(edge_blend(0, HALO), 'line', backward_pairs)]
    all_gather x1 -> x0, blocking collectives: 23 us -> none  [body(): lax.all_gather(jnp.stack([tap_index, range_offset]), 'line', axis=1, tile...]
    reshape x3 -> x6, local copies, waits for them, and re-layouts: 28 us -> 48.9 us  [the longest x2 18.7 us: body(): shifted = blended - grad.reshape(blended.shape) + undo]
    mul x1 -> x2, other arithmetic: 13.6 us -> 31.2 us  [body(): latest = shifted * factor[None, None]]
    mul x1, other arithmetic: 10.5 us -> 26.8 us  [body(): data = data * (step_length / math.sqrt(na))]
    add x0 -> x2, other arithmetic: none -> 14.2 us  [edge_blend(): return cur + momenta[0] * (cur - previous_image[:, :, lo:hi])]
  transfers between devices with their start and end apart: 7 -> 8, of which waited for: 5 -> 3; matrix products, arithmetic and copies ran while one was open for 10% -> 28% of each run, Pallas kernels for 11% -> 11%
where the time goes in v5:
time: 744 us; the launch traced here: 731 us
  waiting for transfers between devices  224 us (30%)
  other arithmetic  217 us (29%)
  Pallas kernels  165 us (22%)
  local copies, waits for them, and re-layouts  96.4 us (13%)
  starting transfers between devices  26.1 us (4%)
    pallas_call x7, Pallas kernels, run_transform(): pl.pallas_call(kernel, out_shape=jax.ShapeDtypeStruct(data.shape, jnp.flo...  152 us
    all_to_all x1, waiting for transfers between devices, body(): data = lax.all_to_all(data, 'line', split_axis=2, concat_axis=3, tiled=True)  102 us
    ppermute x1, waiting for transfers between devices, body(): high = lax.ppermute(blended[:, :, :HALO], 'line', backward_pairs)  83.3 us
    ppermute x1, waiting for transfers between devices, body(): high = lax.ppermute(edge_blend(0, HALO), 'line', backward_pairs)  38.9 us
    mul x2, other arithmetic, body(): latest = shifted * factor[None, None]  31.2 us
    add x2, other arithmetic, body(): blended = latest + momenta[iteration] * (latest - earlier)  31.1 us
    reduce_sum x4, other arithmetic, body(): squares = jnp.sum(shifted * shifted, axis=(0, 1))  29.5 us
    mul x1, other arithmetic, body(): data = data * (step_length / math.sqrt(na))  26.8 us
  transfers between devices with their start and end apart: 8, of which 3 were waited for; matrix products, arithmetic and copies ran while one was open for 28% of the time, Pallas kernels for 11%

profile of v5, /device:TPU:21, one launch (start us, length us, event | category | flops | bytes accessed | tf_op | source)
XLA Modules:
  0.0 731.5 jit_solution(984384262069955067)
XLA Ops:
  2.1 6.5 all-to-all-start
  8.6 17.2 %fusion.69 = (f32[2,8,3,16384]{3,2,1,0:T(4,128)}, f32[2,8,3,16384]{3,2,1,0:T(4,128)}, f32[2,8,3,16384]{3,2,1,0:T(4,128)}, f32[2,8,3,16384]{3,2,1,0:T(4,128)}) fusion(f32[2,8,8,16384]{3,2,1,0:T(8,128)} %param.32, f32[2,8,8,16384]{3,2,1,0:T(8,128)} %param.33), kind=kLoop, calls=%fused_computation.188 | loop fusion | bytes 25165824 | tf_op jit(solution)/shard_map/slice | solution.py:253
  25.8 8.9 %fusion.23 = f32[2,8,3,16384]{3,1,2,0:T(8,128)} fusion(f32[2,8,3,16384]{3,2,1,0:T(4,128)} %get-tuple-element.55, f32[2,8,3,16384]{3,2,1,0:T(4,128)} %get-tuple-element.21), kind=kLoop, calls=%fused_computation.44 | loop fusion | flops 2359296 | bytes 9437184 | tf_op jit(solution)/shard_map/add | solution.py:254
  34.8 3.2 collective-permute-start
  38.0 5.3 fusion.21
  43.3 3.3 collective-permute-start.1
  47.2 18.4 %fusion.17 = (f32[1,8,128,1024]{3,2,1,0:T(8,128)S(1)}, f32[1,8,128,1024]{3,2,1,0:T(8,128)}) fusion(f32[2,8,128,1024]{3,2,1,0:T(8,128)} %param.31, f32[8,1024]{1,0:T(8,128)S(1)} %copy-done.8, f32[128,1024]{1,0:T(8,128)S(1)} %copy-done.7, f32[8]{0:T(128)S(1)} %select_reduce_fusion), kind=kLoop, calls=%fused_computation.34 | loop fusion | flops 9437184 | bytes 17334304 | tf_op jit(solution)/shard_map/mul | solution.py:273
  65.7 4.7 copy.115
  70.4 4.9 copy.116
  75.3 4.2 pad_maximum_fusion
  79.5 12.0 %fusion.1.x_ref = f32[2,64,128,128]{3,2,1,0:T(8,128)} fusion(f32[2,64,128,128]{3,2,1,0:T(8,128)} %bitcast.240, f32[2,64,128,128]{3,2,1,0:T(8,128)} %bitcast.226), kind=kLoop, calls=%fused_computation.2 | loop fusion | flops 6291456 | bytes 25165824 | tf_op jit(solution)/shard_map/add | solution.py:265
  91.5 26.8 %add_multiply_fusion.2 = f32[2,8,128,1024]{3,2,1,0:T(8,128)} fusion(f32[2,8,128,1024]{3,2,1,0:T(8,128)} %pad_maximum_fusion, f32[1024]{0:T(1024)S(1)} %get-tuple-element.44, f32[1024]{0:T(1024)S(1)} %get-tuple-element.45, f32[1024]{0:T(1024)S(1)} %get-tuple-element.46, f32[1024]{0:T(1024)S(1)} %get-tuple-element.47, f32[1024]{0:T(1024)S(1)} %get-tuple-element.48, ...), kind=kLoop, calls=%fused_computation.19 | loop fusion | flops 33554432 | bytes 16809984 | tf_op jit(solution)/shard_map/mul | solution.py:276
  118.4 18.1 %shard_map.302 = f32[2,64,128,128]{3,2,1,0:T(8,128)} custom-call(f32[2,64,128,128]{3,2,1,0:T(8,128)} %fusion.1.x_ref, f32[256,256]{1,0:T(8,128)} %constant.124.clone.w_ref.v_ref, f32[256,256]{1,0:T(8,128)} %constant.125.clone.v_ref.w_ref, f32[2,128,128]{2,1,0:T(8,128)} %constant.126.clone.t_ref), custom_call_target="tpu_custom_call" | custom-call | flops 2147483648 | bytes 16777216 | tf_op jit(solution)/shard_map/pallas_call | solution.py:182
  136.6 38.9 %collective-permute-done.1 = f32[2,8,3,16384]{3,1,2,0:T(8,128)} collective-permute-done((f32[2,8,3,16384]{3,1,2,0:T(8,128)}, f32[2,8,3,16384]{3,1,2,0:T(8,128)}, u32[]{:S(2)}, u32[]{:S(2)}) %collective-permute-start.1) | collective-permute-done | bytes 3145760 | tf_op jit(solution)/shard_map/ppermute | solution.py:257
  176.7 5.5 copy.117
  182.1 4.6 copy.108
  186.7 5.5 all-to-all-start.1
  195.1 3.3 pad_maximum_fusion.1
  198.4 7.2 copy.107
  205.6 9.0 %reshape.223.x_ref = f32[2,48,128,128]{3,2,1,0:T(8,128)} reshape(f32[2,8,6,16384]{3,2,1,0:T(8,128)} %copy.107) | data formatting | bytes 12582912 | tf_op jit(solution)/shard_map/reshape | solution.py:311
  214.5 13.9 %shard_map.303 = f32[2,48,128,128]{3,2,1,0:T(8,128)} custom-call(f32[2,48,128,128]{3,2,1,0:T(8,128)} %reshape.223.x_ref, f32[256,256]{1,0:T(8,128)} %constant.124.clone.w_ref.v_ref, f32[256,256]{1,0:T(8,128)} %constant.125.clone.v_ref.w_ref, f32[2,128,128]{2,1,0:T(8,128)} %constant.126.clone.t_ref), custom_call_target="tpu_custom_call" | custom-call | flops 1610612736 | bytes 12582912 | tf_op jit(solution)/shard_map/pallas_call | solution.py:182
  228.5 4.6 fusion.39
  233.4 4.1 subtract_dynamic-update-slice_fusion.9
  237.7 1.0 subtract_dynamic-update-slice_fusion.8
  238.6 0.9 subtract_dynamic-update-slice_fusion.7
  239.5 0.7 add_dynamic-update-slice_fusion.1
  240.3 0.9 subtract_dynamic-update-slice_fusion.6
  241.1 0.9 subtract_dynamic-update-slice_fusion.5
  242.0 0.9 fusion.35
  243.0 4.4 broadcast_multiply_fusion.1.y_ref
  247.4 29.7 %shard_map.304 = f32[2,64,128,128]{3,2,1,0:T(8,128)} custom-call(f32[2,64,128,128]{3,2,1,0:T(8,128)} %broadcast_multiply_fusion.1.y_ref, f32[256,256]{1,0:T(8,128)} %constant.124.clone.w_ref.v_ref, f32[256,256]{1,0:T(8,128)} %constant.125.clone.v_ref.w_ref, f32[2,128,128]{2,1,0:T(8,128)} %constant.127.clone.t_ref), custom_call_target="tpu_custom_call" | custom-call | flops 2147483648 | bytes 16777216 | tf_op jit(solution)/shard_map/pallas_call | solution.py:182
  277.1 101.8 %all-to-all-done.1 = f32[2,8,128,8,128]{4,3,1,0,2:T(8,128)} async-done(((f32[2,8,128,8,128]{4,3,1,0,2:T(8,128)}), f32[2,8,128,8,128]{4,3,1,0,2:T(8,128)}, u32[]{:S(2)}, u32[]{:S(2)}) %all-to-all-start.1) | async-done | bytes 8388640 | tf_op jit(solution)/shard_map/all_to_all | solution.py:279
  378.9 7.9 %copy.102 = f32[2,8,8,16,8,128]{5,4,3,2,1,0:T(8,128)} copy(f32[2,8,8,16,8,128]{5,4,1,0,2,3:T(8,128)} %bitcast.43) | data formatting | bytes 16777216 | tf_op jit(solution)/shard_map/all_to_all | solution.py:279
  386.9 13.1 %shard_map.305 = f32[128,128,128]{2,1,0:T(8,128)} custom-call(f32[128,128,128]{2,1,0:T(8,128)} %bitcast.243), custom_call_target="tpu_custom_call" | custom-call | bytes 16777216 | tf_op jit(solution)/shard_map/pallas_call | solution.py:161
  400.0 29.5 %shard_map.306 = f32[2,64,128,128]{3,2,1,0:T(8,128)} custom-call(f32[2,64,128,128]{3,2,1,0:T(8,128)} %bitcast.244, f32[256,256]{1,0:T(8,128)} %constant.124.clone.w_ref.v_ref, f32[256,256]{1,0:T(8,128)} %constant.125.clone.v_ref.w_ref, f32[2,128,128]{2,1,0:T(8,128)} %constant.127.clone.t_ref), custom_call_target="tpu_custom_call" | custom-call | flops 2147483648 | bytes 16777216 | tf_op jit(solution)/shard_map/pallas_call | solution.py:182
  429.5 12.2 %multiply_reduce_fusion.1 = f32[64,128,128]{2,1,0:T(8,128)} fusion(f32[2,64,128,128]{3,2,1,0:T(8,128)} %shard_map.306, f32[2,64,128,128]{3,2,1,0:T(8,128)} %fusion.1.x_ref, f32[2,64,128,128]{3,2,1,0:T(8,128)} %shard_map.304), kind=kLoop, calls=%fused_computation.16 | loop fusion | flops 7340032 | bytes 29360128 | tf_op jit(solution)/shard_map/reduce_sum | solution.py:372
  441.7 2.5 reduce_sum.44
  444.1 1.5 collective-permute-start.2
  445.6 9.4 %reshape.210 = f32[2,8,8,16384]{3,2,1,0:T(8,128)} reshape(f32[2,64,128,128]{3,2,1,0:T(8,128)} %shard_map.304) | data formatting | bytes 16777216 | tf_op jit(solution)/shard_map/reshape | solution.py:371
  455.0 9.5 %reshape.214 = f32[2,8,8,16384]{3,2,1,0:T(8,128)} reshape(f32[2,64,128,128]{3,2,1,0:T(8,128)} %shard_map.306) | data formatting | bytes 16777216 | tf_op jit(solution)/shard_map/reshape | solution.py:370
  465.0 14.1 %multiply_add_fusion = f32[2,8,8,128,128]{4,3,2,1,0:T(8,128)S(1)} fusion(f32[2,8,8,128,128]{4,3,2,1,0:T(8,128)} %bitcast.216, f32[2,8,8,128,128]{4,3,2,1,0:T(8,128)} %bitcast.217, f32[2,8,8,128,128]{4,2,3,1,0:T(8,128)} %bitcast.222, f32[2,8,8,128,128]{4,2,3,1,0:T(8,128)} %bitcast.218, f32[8,128,128]{2,1,0:T(8,128)S(1)} %maximum_divide_fusion), kind=kLoop, calls=%fused_computation.15 | loop fusion | flops 18874368 | bytes 42467328 | tf_op jit(solution)/shard_map/add | solution.py:301
  479.1 3.0 fusion.68
  482.1 2.9 collective-permute-start.4
  485.0 2.4 collective-permute-start.3
  487.9 17.0 %fusion.3.x_ref = f32[2,64,128,128]{3,2,1,0:T(8,128)} fusion(f32[64,128,128]{2,1,0:T(8,128)S(1)} %bitcast.248, f32[2,64,128,128]{3,2,1,0:T(8,128)} %shard_map.306, f32[2,64,128,128]{3,2,1,0:T(8,128)} %fusion.1.x_ref, f32[2,64,128,128]{3,2,1,0:T(8,128)} %shard_map.304, f32[2,64,128,128]{3,2,1,0:T(8,128)} %bitcast.227), kind=kLoop, calls=%fused_computation.5 | loop fusion | flops 12582912 | bytes 46137344 | tf_op jit(solution)/shard_map/add | solution.py:301
  504.9 17.6 %shard_map.307 = f32[2,64,128,128]{3,2,1,0:T(8,128)} custom-call(f32[2,64,128,128]{3,2,1,0:T(8,128)} %fusion.3.x_ref, f32[256,256]{1,0:T(8,128)} %constant.124.clone.w_ref.v_ref, f32[256,256]{1,0:T(8,128)} %constant.125.clone.v_ref.w_ref, f32[2,128,128]{2,1,0:T(8,128)} %constant.126.clone.t_ref), custom_call_target="tpu_custom_call" | custom-call | flops 2147483648 | bytes 16777216 | tf_op jit(solution)/shard_map/pallas_call | solution.py:182
  522.6 15.6 %add_multiply_fusion.1 = f32[2,8,8,16384]{3,2,1,0:T(8,128)} fusion(f32[2,8,8,16384]{3,2,1,0:T(8,128)} %reshape.214, f32[2,8,8,16384]{3,2,1,0:T(8,128)} %reshape.210, f32[2,8,8,16384]{3,2,1,0:T(8,128)} %param.32, f32[2,8,8,16384]{3,2,1,0:T(8,128)} %param.33, f32[8,16384]{1,0:T(8,128)S(1)} %bitcast.252), kind=kLoop, calls=%fused_computation.18 | loop fusion | flops 12582912 | bytes 42467328 | tf_op jit(solution)/shard_map/mul | solution.py:379
  538.2 83.3 %collective-permute-done.4 = f32[2,8,3,128,128]{4,3,2,1,0:T(8,128)} collective-permute-done((f32[2,8,3,128,128]{4,3,2,1,0:T(8,128)}, f32[2,8,3,128,128]{4,3,2,1,0:T(8,128)}, u32[]{:S(2)}, u32[]{:S(2)}) %collective-permute-start.4) | collective-permute-done | bytes 3145760 | tf_op jit(solution)/shard_map/ppermute | solution.py:303
  621.4 6.3 pad_maximum_fusion.2
  627.8 14.0 %shard_map.308 = f32[2,48,128,128]{3,2,1,0:T(8,128)} custom-call(f32[2,48,128,128]{3,2,1,0:T(8,128)} %bitcast.245, f32[256,256]{1,0:T(8,128)} %constant.124.clone.w_ref.v_ref, f32[256,256]{1,0:T(8,128)} %constant.125.clone.v_ref.w_ref, f32[2,128,128]{2,1,0:T(8,128)} %constant.126.clone.t_ref), custom_call_target="tpu_custom_call" | custom-call | flops 1610612736 | bytes 12582912 | tf_op jit(solution)/shard_map/pallas_call | solution.py:182
  641.8 4.6 fusion.31
  646.7 4.1 subtract_dynamic-update-slice_fusion.4
  650.9 1.0 subtract_dynamic-update-slice_fusion.3
  651.9 0.9 subtract_dynamic-update-slice_fusion.2
  653.6 0.9 subtract_dynamic-update-slice_fusion.1
  654.4 0.9 subtract_dynamic-update-slice_fusion
  655.3 0.9 fusion.27
  656.2 4.2 broadcast_multiply_fusion.y_ref
  660.5 29.5 %shard_map.309 = f32[2,64,128,128]{3,2,1,0:T(8,128)} custom-call(f32[2,64,128,128]{3,2,1,0:T(8,128)} %broadcast_multiply_fusion.y_ref, f32[256,256]{1,0:T(8,128)} %constant.124.clone.w_ref.v_ref, f32[256,256]{1,0:T(8,128)} %constant.125.clone.v_ref.w_ref, f32[2,128,128]{2,1,0:T(8,128)} %constant.127.clone.t_ref), custom_call_target="tpu_custom_call" | custom-call | flops 2147483648 | bytes 16777216 | tf_op jit(solution)/shard_map/pallas_call | solution.py:182
  690.0 12.4 %multiply_reduce_fusion = f32[64,128,128]{2,1,0:T(8,128)} fusion(f32[2,64,128,128]{3,2,1,0:T(8,128)} %shard_map.306, f32[2,64,128,128]{3,2,1,0:T(8,128)} %fusion.3.x_ref, f32[2,64,128,128]{3,2,1,0:T(8,128)} %shard_map.309), kind=kLoop, calls=%fused_computation.13 | loop fusion | flops 7340032 | bytes 29360128 | tf_op jit(solution)/shard_map/reduce_sum | solution.py:372
  702.4 2.5 reduce_sum.47
  704.9 0.9 collective-permute-start.5
  705.7 9.4 %reshape.222 = f32[2,8,8,16384]{3,2,1,0:T(8,128)} reshape(f32[2,64,128,128]{3,2,1,0:T(8,128)} %shard_map.309) | data formatting | bytes 16777216 | tf_op jit(solution)/shard_map/reshape | solution.py:371
  715.7 15.6 %add_multiply_fusion = f32[2,8,8,16384]{3,2,1,0:T(8,128)} fusion(f32[2,8,8,16384]{3,2,1,0:T(8,128)} %reshape.214, f32[2,8,8,16384]{3,2,1,0:T(8,128)} %reshape.222, f32[2,8,8,16384]{3,2,1,0:T(8,128)} %add_multiply_fusion.1, f32[2,8,8,16384]{3,2,1,0:T(8,128)} %param.32, f32[8,16384]{1,0:T(8,128)S(1)} %bitcast.253), kind=kLoop, calls=%fused_computation.14 | loop fusion | flops 12582912 | bytes 42467328 | tf_op jit(solution)/shard_map/mul | solution.py:379
  (92 shorter events, 9.6 us)
Async XLA Ops:
  0.6 45.9 %copy-start = (f32[16,4]{0,1:T(4,128)S(1)}, f32[16,4]{0,1:T(4,128)}, u32[]{:S(2)}) copy-start(f32[16,4]{0,1:T(4,128)} %param.38) | copy-start | bytes 772
  2.1 134.5 %all-to-all-start = ((s32[16,2,1024]{2,1,0:T(2,128)}), s32[16,2,1024]{2,1,0:T(2,128)S(1)}, u32[]{:S(2)}, u32[]{:S(2)}) async-start(s32[16,2,1024]{2,1,0:T(2,128)} %broadcast_in_dim.18), calls=%async_computation | async-start | bytes 262144 | tf_op jit(solution)/shard_map/all_to_all | solution.py:261
  25.8 12.2 %copy-start.5 = (f32[2,8,3,16384]{3,2,1,0:T(4,128)S(1)}, f32[2,8,3,16384]{3,2,1,0:T(4,128)}, u32[]{:S(2)}) copy-start(f32[2,8,3,16384]{3,2,1,0:T(4,128)} %get-tuple-element.20) | copy-start | bytes 9437188
  25.8 12.2 %copy-start.6 = (f32[2,8,3,16384]{3,2,1,0:T(4,128)S(1)}, f32[2,8,3,16384]{3,2,1,0:T(4,128)}, u32[]{:S(2)}) copy-start(f32[2,8,3,16384]{3,2,1,0:T(4,128)} %get-tuple-element.56) | copy-start | bytes 9437188
  34.7 11.9 %copy-start.10 = (s32[1024]{0:T(1024)S(1)}, s32[1024]{0:T(1024)}, u32[]{:S(2)}) copy-start(s32[1024]{0:T(1024)} %param.37) | copy-start | bytes 12292
  34.7 12.3 %copy-start.11 = (f32[4]{0:T(128)S(1)}, f32[4]{0:T(128)}, u32[]{:S(2)}) copy-start(f32[4]{0:T(128)} %param.40) | copy-start | bytes 52
  34.7 12.3 %copy-start.12 = (s32[8]{0:T(128)S(1)}, s32[8]{0:T(128)}, u32[]{:S(2)}) copy-start(s32[8]{0:T(128)} %param.39) | copy-start | bytes 100
  34.7 12.4 %copy-start.7 = (f32[128,1024]{1,0:T(8,128)S(1)}, f32[128,1024]{1,0:T(8,128)}, u32[]{:S(2)}) copy-start(f32[128,1024]{1,0:T(8,128)} %param.34) | copy-start | bytes 1572868
  34.7 12.4 %copy-start.8 = (f32[8,1024]{1,0:T(8,128)S(1)}, f32[8,1024]{1,0:T(8,128)}, u32[]{:S(2)}) copy-start(f32[8,1024]{1,0:T(8,128)} %param.35) | copy-start | bytes 98308
  34.8 101.8 %collective-permute-start = (f32[2,8,3,16384]{3,1,2,0:T(8,128)}, f32[2,8,3,16384]{3,1,2,0:T(8,128)}, u32[]{:S(2)}, u32[]{:S(2)}) collective-permute-start(f32[2,8,3,16384]{3,1,2,0:T(8,128)} %fusion.23), channel_id=1, source_target_pairs={{0,2},{2,4},{4,6},{6,8},{8,10},{10,12},{12,14},{14,16},{16,18},{18... | collective-permute-start | bytes 9437192 | tf_op jit(solution)/shard_map/ppermute | solution.py:256
  38.0 27.6 %slice-start.4 = ((s8[8388608]{0:T(1024)(128)(4,1)}), s8[4194304]{0:T(1024)(128)(4,1)S(1)}, s32[]{:S(2)}) async-start(s8[8388608]{0:T(1024)(128)(4,1)} %bitcast.219), calls=%async_computation.6 | async-start | bytes 8388608
  38.0 32.4 %slice-start.6 = ((s8[8388608]{0:T(1024)(128)(4,1)}), s8[4194304]{0:T(1024)(128)(4,1)S(1)}, s32[]{:S(2)}) async-start(s8[8388608]{0:T(1024)(128)(4,1)} %bitcast.223), calls=%async_computation.8 | async-start | bytes 8388608
  43.3 132.1 %collective-permute-start.1 = (f32[2,8,3,16384]{3,1,2,0:T(8,128)}, f32[2,8,3,16384]{3,1,2,0:T(8,128)}, u32[]{:S(2)}, u32[]{:S(2)}) collective-permute-start(f32[2,8,3,16384]{3,1,2,0:T(8,128)} %fusion.21), channel_id=1, source_target_pairs={{2,0},{4,2},{6,4},{8,6},{10,8},{12,10},{14,12},{16,14},{18,16},{20... | collective-permute-start | bytes 9437192 | tf_op jit(solution)/shard_map/ppermute | solution.py:257
  47.2 18.4 %copy-start.9 = (s32[1024]{0:T(1024)S(1)}, s32[1024]{0:T(1024)}, u32[]{:S(2)}) copy-start(s32[1024]{0:T(1024)} %param.36) | copy-start | bytes 12292
  47.2 18.5 %slice-start.5 = ((s8[8388608]{0:T(1024)(128)(4,1)}), s8[4194304]{0:T(1024)(128)(4,1)S(1)}, s32[]{:S(2)}) async-start(s8[8388608]{0:T(1024)(128)(4,1)} %bitcast.219), calls=%async_computation.7 | async-start | bytes 8388608
  47.2 23.2 %slice-start.7 = ((s8[8388608]{0:T(1024)(128)(4,1)}), s8[4194304]{0:T(1024)(128)(4,1)S(1)}, s32[]{:S(2)}) async-start(s8[8388608]{0:T(1024)(128)(4,1)} %bitcast.223), calls=%async_computation.9 | async-start | bytes 8388608
  70.4 4.9 copy-start.4
  186.7 192.2 %all-to-all-start.1 = ((f32[2,8,128,8,128]{4,3,1,0,2:T(8,128)}), f32[2,8,128,8,128]{4,3,1,0,2:T(8,128)}, u32[]{:S(2)}, u32[]{:S(2)}) async-start(f32[2,8,128,8,128]{4,3,1,0,2:T(8,128)} %copy.108), calls=%async_computation.1 | async-start | bytes 16777216 | tf_op jit(solution)/shard_map/all_to_all | solution.py:279
  228.5 5.0 copy-start.3
  228.5 9.0 %slice-start = ((s8[8388608]{0:T(1024)(128)(4,1)}), s8[4194304]{0:T(1024)(128)(4,1)S(1)}, s32[]{:S(2)}) async-start(s8[8388608]{0:T(1024)(128)(4,1)} %bitcast.198), calls=%async_computation.2 | async-start | bytes 8388608
  233.4 4.2 slice-start.1
  444.1 20.3 %collective-permute-start.2 = (f32[8,128,128]{2,1,0:T(8,128)S(1)}, f32[8,128,128]{2,1,0:T(8,128)S(1)}, u32[]{:S(2)}, u32[]{:S(2)}) collective-permute-start(f32[8,128,128]{2,1,0:T(8,128)S(1)} %reduce_sum.44), channel_id=1, source_target_pairs={{0,1},{1,0},{2,3},{3,2},{4,5},{5,4},{6,7},{7,6},{8,9},{9,8},{10,11... | collective-permute-start | bytes 1572872 | tf_op jit(solution)/shard_map/ppermute | solution.py:374
  482.1 139.3 %collective-permute-start.4 = (f32[2,8,3,128,128]{4,3,2,1,0:T(8,128)}, f32[2,8,3,128,128]{4,3,2,1,0:T(8,128)}, u32[]{:S(2)}, u32[]{:S(2)}) collective-permute-start(f32[2,8,3,128,128]{4,3,2,1,0:T(8,128)} %get-tuple-element.18), channel_id=1, source_target_pairs={{2,0},{4,2},{6,4},{8,6},{10,8},{12,10},{14,12},{16,14},{18,16},{20... | collective-permute-start | bytes 9437192 | tf_op jit(solution)/shard_map/ppermute | solution.py:303
  485.0 136.4 %collective-permute-start.3 = (f32[2,8,3,128,128]{4,3,2,1,0:T(8,128)}, f32[2,8,3,128,128]{4,3,2,1,0:T(8,128)}, u32[]{:S(2)}, u32[]{:S(2)}) collective-permute-start(f32[2,8,3,128,128]{4,3,2,1,0:T(8,128)} %get-tuple-element.19), channel_id=1, source_target_pairs={{0,2},{2,4},{4,6},{6,8},{8,10},{10,12},{12,14},{14,16},{16,18},{18... | collective-permute-start | bytes 9437192 | tf_op jit(solution)/shard_map/ppermute | solution.py:302
  641.7 5.0 copy-start.2
  641.8 9.0 %slice-start.2 = ((s8[8388608]{0:T(1024)(128)(4,1)}), s8[4194304]{0:T(1024)(128)(4,1)S(1)}, s32[]{:S(2)}) async-start(s8[8388608]{0:T(1024)(128)(4,1)} %bitcast.208), calls=%async_computation.4 | async-start | bytes 8388608
  646.7 4.2 slice-start.3
  704.9 10.2 %collective-permute-start.5 = (f32[8,128,128]{2,1,0:T(8,128)S(1)}, f32[8,128,128]{2,1,0:T(8,128)S(1)}, u32[]{:S(2)}, u32[]{:S(2)}) collective-permute-start(f32[8,128,128]{2,1,0:T(8,128)S(1)} %reduce_sum.47), channel_id=1, source_target_pairs={{0,1},{1,0},{2,3},{3,2},{4,5},{5,4},{6,7},{7,6},{8,9},{9,8},{10,11... | collective-permute-start | bytes 1572872 | tf_op jit(solution)/shard_map/ppermute | solution.py:374
  715.6 15.6 %copy-start.1 = (f32[16,4]{0,1:T(4,128)S(1)}, f32[16,4]{0,1:T(4,128)}, u32[]{:S(2)}) copy-start(f32[16,4]{0,1:T(4,128)} %param.38) | copy-start | bytes 772

commit v6 on v5

--- a/solution.py
+++ b/solution.py
@@ -93,7 +93,7 @@
 
 
 def dot(a, b):
-    return jnp.dot(a, b, precision=lax.Precision.HIGHEST, preferred_element_type=jnp.float32)
+    return jnp.dot(a, b, precision=lax.Precision.HIGH, preferred_element_type=jnp.float32)
 
 
 def forward_kernel(x_ref, w_ref, v_ref, t_ref, o_ref):

time: 744 us -> 715 us (0.961)
  Pallas kernels: 165 us -> 108 us
  waiting for transfers between devices: 224 us -> 251 us
    pallas_call x7, Pallas kernels: 152 us -> 95.4 us  [run_transform(): pl.pallas_call(kernel, out_shape=jax.ShapeDtypeStruct(data.shape, jnp.flo...]
    all_to_all x1, waiting for transfers between devices: 102 us -> 119 us  [body(): data = lax.all_to_all(data, 'line', split_axis=2, concat_axis=3, tiled=True)]
  transfers between devices with their start and end apart: 8 -> 8, of which waited for: 3 -> 3; matrix products, arithmetic and copies ran while one was open for 28% -> 29% of each run, Pallas kernels for 11% -> 7%
where the time goes in v6:
time: 715 us; the launch traced here: 702 us
  waiting for transfers between devices  251 us (35%)
  other arithmetic  217 us (30%)
  Pallas kernels  108 us (15%)
  local copies, waits for them, and re-layouts  96.4 us (13%)
  starting transfers between devices  26.1 us (4%)
    all_to_all x1, waiting for transfers between devices, body(): data = lax.all_to_all(data, 'line', split_axis=2, concat_axis=3, tiled=True)  119 us
    pallas_call x7, Pallas kernels, run_transform(): pl.pallas_call(kernel, out_shape=jax.ShapeDtypeStruct(data.shape, jnp.flo...  95.4 us
    ppermute x1, waiting for transfers between devices, body(): high = lax.ppermute(blended[:, :, :HALO], 'line', backward_pairs)  88.6 us
    ppermute x1, waiting for transfers between devices, body(): high = lax.ppermute(edge_blend(0, HALO), 'line', backward_pairs)  43.8 us
    mul x2, other arithmetic, body(): latest = shifted * factor[None, None]  31.2 us
    add x2, other arithmetic, body(): blended = latest + momenta[iteration] * (latest - earlier)  30.7 us
    reduce_sum x4, other arithmetic, body(): squares = jnp.sum(shifted * shifted, axis=(0, 1))  29.5 us
    mul x1, other arithmetic, body(): data = data * (step_length / math.sqrt(na))  26.8 us
  transfers between devices with their start and end apart: 8, of which 3 were waited for; matrix products, arithmetic and copies ran while one was open for 29% of the time, Pallas kernels for 7%

profile of v6, /device:TPU:21, one launch (start us, length us, event | category | flops | bytes accessed | tf_op | source)
XLA Modules:
  0.0 701.6 jit_solution(15557444421141896263)
XLA Ops:
  2.1 6.5 all-to-all-start
  8.6 17.2 %fusion.69 = (f32[2,8,3,16384]{3,2,1,0:T(4,128)}, f32[2,8,3,16384]{3,2,1,0:T(4,128)}, f32[2,8,3,16384]{3,2,1,0:T(4,128)}, f32[2,8,3,16384]{3,2,1,0:T(4,128)}) fusion(f32[2,8,8,16384]{3,2,1,0:T(8,128)} %param.32, f32[2,8,8,16384]{3,2,1,0:T(8,128)} %param.33), kind=kLoop, calls=%fused_computation.188 | loop fusion | bytes 25165824 | tf_op jit(solution)/shard_map/slice | solution.py:253
  25.8 8.9 %fusion.23 = f32[2,8,3,16384]{3,1,2,0:T(8,128)} fusion(f32[2,8,3,16384]{3,2,1,0:T(4,128)} %get-tuple-element.55, f32[2,8,3,16384]{3,2,1,0:T(4,128)} %get-tuple-element.21), kind=kLoop, calls=%fused_computation.44 | loop fusion | flops 2359296 | bytes 9437184 | tf_op jit(solution)/shard_map/add | solution.py:254
  34.8 3.2 collective-permute-start
  38.0 5.3 fusion.21
  43.3 3.3 collective-permute-start.1
  47.3 18.4 %fusion.17 = (f32[1,8,128,1024]{3,2,1,0:T(8,128)S(1)}, f32[1,8,128,1024]{3,2,1,0:T(8,128)}) fusion(f32[2,8,128,1024]{3,2,1,0:T(8,128)} %param.31, f32[8,1024]{1,0:T(8,128)S(1)} %copy-done.8, f32[128,1024]{1,0:T(8,128)S(1)} %copy-done.7, f32[8]{0:T(128)S(1)} %select_reduce_fusion), kind=kLoop, calls=%fused_computation.34 | loop fusion | flops 9437184 | bytes 17334304 | tf_op jit(solution)/shard_map/mul | solution.py:273
  65.7 4.7 copy.115
  70.4 4.9 copy.116
  75.3 4.2 pad_maximum_fusion
  79.6 12.0 %fusion.1.x_ref = f32[2,64,128,128]{3,2,1,0:T(8,128)} fusion(f32[2,64,128,128]{3,2,1,0:T(8,128)} %bitcast.240, f32[2,64,128,128]{3,2,1,0:T(8,128)} %bitcast.226), kind=kLoop, calls=%fused_computation.2 | loop fusion | flops 6291456 | bytes 25165824 | tf_op jit(solution)/shard_map/add | solution.py:265
  91.5 26.8 %add_multiply_fusion.2 = f32[2,8,128,1024]{3,2,1,0:T(8,128)} fusion(f32[2,8,128,1024]{3,2,1,0:T(8,128)} %pad_maximum_fusion, f32[1024]{0:T(1024)S(1)} %get-tuple-element.44, f32[1024]{0:T(1024)S(1)} %get-tuple-element.45, f32[1024]{0:T(1024)S(1)} %get-tuple-element.46, f32[1024]{0:T(1024)S(1)} %get-tuple-element.47, f32[1024]{0:T(1024)S(1)} %get-tuple-element.48, ...), kind=kLoop, calls=%fused_computation.19 | loop fusion | flops 33554432 | bytes 16809984 | tf_op jit(solution)/shard_map/mul | solution.py:276
  118.5 13.2 %shard_map.302 = f32[2,64,128,128]{3,2,1,0:T(8,128)} custom-call(f32[2,64,128,128]{3,2,1,0:T(8,128)} %fusion.1.x_ref, f32[256,256]{1,0:T(8,128)} %constant.124.clone.w_ref.v_ref, f32[256,256]{1,0:T(8,128)} %constant.125.clone.v_ref.w_ref, f32[2,128,128]{2,1,0:T(8,128)} %constant.126.clone.t_ref), custom_call_target="tpu_custom_call" | custom-call | flops 2147483648 | bytes 16777216 | tf_op jit(solution)/shard_map/pallas_call | solution.py:182
  131.7 43.8 %collective-permute-done.1 = f32[2,8,3,16384]{3,1,2,0:T(8,128)} collective-permute-done((f32[2,8,3,16384]{3,1,2,0:T(8,128)}, f32[2,8,3,16384]{3,1,2,0:T(8,128)}, u32[]{:S(2)}, u32[]{:S(2)}) %collective-permute-start.1) | collective-permute-done | bytes 3145760 | tf_op jit(solution)/shard_map/ppermute | solution.py:257
  176.7 5.5 copy.117
  182.1 4.6 copy.108
  186.7 5.5 all-to-all-start.1
  195.1 3.3 pad_maximum_fusion.1
  198.4 7.2 %copy.107 = f32[2,8,6,16384]{3,2,1,0:T(8,128)} copy(f32[2,8,6,16384]{3,1,2,0:T(8,128)S(1)} %pad_maximum_fusion.1) | data formatting | bytes 12582912 | tf_op jit(solution)/shard_map/reshape | solution.py:311
  205.6 9.0 %reshape.223.x_ref = f32[2,48,128,128]{3,2,1,0:T(8,128)} reshape(f32[2,8,6,16384]{3,2,1,0:T(8,128)} %copy.107) | data formatting | bytes 12582912 | tf_op jit(solution)/shard_map/reshape | solution.py:311
  214.5 10.1 %shard_map.303 = f32[2,48,128,128]{3,2,1,0:T(8,128)} custom-call(f32[2,48,128,128]{3,2,1,0:T(8,128)} %reshape.223.x_ref, f32[256,256]{1,0:T(8,128)} %constant.124.clone.w_ref.v_ref, f32[256,256]{1,0:T(8,128)} %constant.125.clone.v_ref.w_ref, f32[2,128,128]{2,1,0:T(8,128)} %constant.126.clone.t_ref), custom_call_target="tpu_custom_call" | custom-call | flops 1610612736 | bytes 12582912 | tf_op jit(solution)/shard_map/pallas_call | solution.py:182
  224.7 4.6 fusion.39
  229.6 4.1 subtract_dynamic-update-slice_fusion.9
  233.8 1.0 subtract_dynamic-update-slice_fusion.8
  234.8 0.9 subtract_dynamic-update-slice_fusion.7
  235.7 0.7 add_dynamic-update-slice_fusion.1
  236.4 0.9 subtract_dynamic-update-slice_fusion.6
  237.3 0.9 subtract_dynamic-update-slice_fusion.5
  238.2 0.9 fusion.35
  239.1 4.4 broadcast_multiply_fusion.1.y_ref
  243.5 16.3 %shard_map.304 = f32[2,64,128,128]{3,2,1,0:T(8,128)} custom-call(f32[2,64,128,128]{3,2,1,0:T(8,128)} %broadcast_multiply_fusion.1.y_ref, f32[256,256]{1,0:T(8,128)} %constant.124.clone.w_ref.v_ref, f32[256,256]{1,0:T(8,128)} %constant.125.clone.v_ref.w_ref, f32[2,128,128]{2,1,0:T(8,128)} %constant.127.clone.t_ref), custom_call_target="tpu_custom_call" | custom-call | flops 2147483648 | bytes 16777216 | tf_op jit(solution)/shard_map/pallas_call | solution.py:182
  259.8 119.1 %all-to-all-done.1 = f32[2,8,128,8,128]{4,3,1,0,2:T(8,128)} async-done(((f32[2,8,128,8,128]{4,3,1,0,2:T(8,128)}), f32[2,8,128,8,128]{4,3,1,0,2:T(8,128)}, u32[]{:S(2)}, u32[]{:S(2)}) %all-to-all-start.1) | async-done | bytes 8388640 | tf_op jit(solution)/shard_map/all_to_all | solution.py:279
  379.0 7.9 %copy.102 = f32[2,8,8,16,8,128]{5,4,3,2,1,0:T(8,128)} copy(f32[2,8,8,16,8,128]{5,4,1,0,2,3:T(8,128)} %bitcast.43) | data formatting | bytes 16777216 | tf_op jit(solution)/shard_map/all_to_all | solution.py:279
  386.9 13.1 %shard_map.305 = f32[128,128,128]{2,1,0:T(8,128)} custom-call(f32[128,128,128]{2,1,0:T(8,128)} %bitcast.243), custom_call_target="tpu_custom_call" | custom-call | bytes 16777216 | tf_op jit(solution)/shard_map/pallas_call | solution.py:161
  400.0 16.6 %shard_map.306 = f32[2,64,128,128]{3,2,1,0:T(8,128)} custom-call(f32[2,64,128,128]{3,2,1,0:T(8,128)} %bitcast.244, f32[256,256]{1,0:T(8,128)} %constant.124.clone.w_ref.v_ref, f32[256,256]{1,0:T(8,128)} %constant.125.clone.v_ref.w_ref, f32[2,128,128]{2,1,0:T(8,128)} %constant.127.clone.t_ref), custom_call_target="tpu_custom_call" | custom-call | flops 2147483648 | bytes 16777216 | tf_op jit(solution)/shard_map/pallas_call | solution.py:182
  416.7 12.2 %multiply_reduce_fusion.1 = f32[64,128,128]{2,1,0:T(8,128)} fusion(f32[2,64,128,128]{3,2,1,0:T(8,128)} %shard_map.306, f32[2,64,128,128]{3,2,1,0:T(8,128)} %fusion.1.x_ref, f32[2,64,128,128]{3,2,1,0:T(8,128)} %shard_map.304), kind=kLoop, calls=%fused_computation.16 | loop fusion | flops 7340032 | bytes 29360128 | tf_op jit(solution)/shard_map/reduce_sum | solution.py:372
  428.8 2.5 reduce_sum.44
  431.3 1.5 collective-permute-start.2
  432.8 9.4 %reshape.210 = f32[2,8,8,16384]{3,2,1,0:T(8,128)} reshape(f32[2,64,128,128]{3,2,1,0:T(8,128)} %shard_map.304) | data formatting | bytes 16777216 | tf_op jit(solution)/shard_map/reshape | solution.py:371
  442.2 9.5 %reshape.214 = f32[2,8,8,16384]{3,2,1,0:T(8,128)} reshape(f32[2,64,128,128]{3,2,1,0:T(8,128)} %shard_map.306) | data formatting | bytes 16777216 | tf_op jit(solution)/shard_map/reshape | solution.py:370
  452.2 14.1 %multiply_add_fusion = f32[2,8,8,128,128]{4,3,2,1,0:T(8,128)S(1)} fusion(f32[2,8,8,128,128]{4,3,2,1,0:T(8,128)} %bitcast.216, f32[2,8,8,128,128]{4,3,2,1,0:T(8,128)} %bitcast.217, f32[2,8,8,128,128]{4,2,3,1,0:T(8,128)} %bitcast.222, f32[2,8,8,128,128]{4,2,3,1,0:T(8,128)} %bitcast.218, f32[8,128,128]{2,1,0:T(8,128)S(1)} %maximum_divide_fusion), kind=kLoop, calls=%fused_computation.15 | loop fusion | flops 18874368 | bytes 42467328 | tf_op jit(solution)/shard_map/add | solution.py:301
  466.3 3.0 fusion.68
  469.3 2.9 collective-permute-start.4
  472.2 2.4 collective-permute-start.3
  475.1 16.6 %fusion.3.x_ref = f32[2,64,128,128]{3,2,1,0:T(8,128)} fusion(f32[64,128,128]{2,1,0:T(8,128)S(1)} %bitcast.248, f32[2,64,128,128]{3,2,1,0:T(8,128)} %shard_map.306, f32[2,64,128,128]{3,2,1,0:T(8,128)} %fusion.1.x_ref, f32[2,64,128,128]{3,2,1,0:T(8,128)} %shard_map.304, f32[2,64,128,128]{3,2,1,0:T(8,128)} %bitcast.227), kind=kLoop, calls=%fused_computation.5 | loop fusion | flops 12582912 | bytes 46137344 | tf_op jit(solution)/shard_map/add | solution.py:301
  491.7 12.7 %shard_map.307 = f32[2,64,128,128]{3,2,1,0:T(8,128)} custom-call(f32[2,64,128,128]{3,2,1,0:T(8,128)} %fusion.3.x_ref, f32[256,256]{1,0:T(8,128)} %constant.124.clone.w_ref.v_ref, f32[256,256]{1,0:T(8,128)} %constant.125.clone.v_ref.w_ref, f32[2,128,128]{2,1,0:T(8,128)} %constant.126.clone.t_ref), custom_call_target="tpu_custom_call" | custom-call | flops 2147483648 | bytes 16777216 | tf_op jit(solution)/shard_map/pallas_call | solution.py:182
  504.4 15.6 %add_multiply_fusion.1 = f32[2,8,8,16384]{3,2,1,0:T(8,128)} fusion(f32[2,8,8,16384]{3,2,1,0:T(8,128)} %reshape.214, f32[2,8,8,16384]{3,2,1,0:T(8,128)} %reshape.210, f32[2,8,8,16384]{3,2,1,0:T(8,128)} %param.32, f32[2,8,8,16384]{3,2,1,0:T(8,128)} %param.33, f32[8,16384]{1,0:T(8,128)S(1)} %bitcast.252), kind=kLoop, calls=%fused_computation.18 | loop fusion | flops 12582912 | bytes 42467328 | tf_op jit(solution)/shard_map/mul | solution.py:379
  520.0 88.6 %collective-permute-done.4 = f32[2,8,3,128,128]{4,3,2,1,0:T(8,128)} collective-permute-done((f32[2,8,3,128,128]{4,3,2,1,0:T(8,128)}, f32[2,8,3,128,128]{4,3,2,1,0:T(8,128)}, u32[]{:S(2)}, u32[]{:S(2)}) %collective-permute-start.4) | collective-permute-done | bytes 3145760 | tf_op jit(solution)/shard_map/ppermute | solution.py:303
  608.6 6.3 pad_maximum_fusion.2
  614.9 10.1 %shard_map.308 = f32[2,48,128,128]{3,2,1,0:T(8,128)} custom-call(f32[2,48,128,128]{3,2,1,0:T(8,128)} %bitcast.245, f32[256,256]{1,0:T(8,128)} %constant.124.clone.w_ref.v_ref, f32[256,256]{1,0:T(8,128)} %constant.125.clone.v_ref.w_ref, f32[2,128,128]{2,1,0:T(8,128)} %constant.126.clone.t_ref), custom_call_target="tpu_custom_call" | custom-call | flops 1610612736 | bytes 12582912 | tf_op jit(solution)/shard_map/pallas_call | solution.py:182
  625.1 4.6 fusion.31
  630.0 4.1 subtract_dynamic-update-slice_fusion.4
  634.3 1.0 subtract_dynamic-update-slice_fusion.3
  635.2 0.9 subtract_dynamic-update-slice_fusion.2
  636.9 0.9 subtract_dynamic-update-slice_fusion.1
  637.7 0.9 subtract_dynamic-update-slice_fusion
  638.6 0.9 fusion.27
  639.6 4.2 broadcast_multiply_fusion.y_ref
  643.8 16.3 %shard_map.309 = f32[2,64,128,128]{3,2,1,0:T(8,128)} custom-call(f32[2,64,128,128]{3,2,1,0:T(8,128)} %broadcast_multiply_fusion.y_ref, f32[256,256]{1,0:T(8,128)} %constant.124.clone.w_ref.v_ref, f32[256,256]{1,0:T(8,128)} %constant.125.clone.v_ref.w_ref, f32[2,128,128]{2,1,0:T(8,128)} %constant.127.clone.t_ref), custom_call_target="tpu_custom_call" | custom-call | flops 2147483648 | bytes 16777216 | tf_op jit(solution)/shard_map/pallas_call | solution.py:182
  660.1 12.4 %multiply_reduce_fusion = f32[64,128,128]{2,1,0:T(8,128)} fusion(f32[2,64,128,128]{3,2,1,0:T(8,128)} %shard_map.306, f32[2,64,128,128]{3,2,1,0:T(8,128)} %fusion.3.x_ref, f32[2,64,128,128]{3,2,1,0:T(8,128)} %shard_map.309), kind=kLoop, calls=%fused_computation.13 | loop fusion | flops 7340032 | bytes 29360128 | tf_op jit(solution)/shard_map/reduce_sum | solution.py:372
  672.5 2.5 reduce_sum.47
  675.0 0.9 collective-permute-start.5
  675.8 9.4 %reshape.222 = f32[2,8,8,16384]{3,2,1,0:T(8,128)} reshape(f32[2,64,128,128]{3,2,1,0:T(8,128)} %shard_map.309) | data formatting | bytes 16777216 | tf_op jit(solution)/shard_map/reshape | solution.py:371
  685.7 15.6 %add_multiply_fusion = f32[2,8,8,16384]{3,2,1,0:T(8,128)} fusion(f32[2,8,8,16384]{3,2,1,0:T(8,128)} %reshape.214, f32[2,8,8,16384]{3,2,1,0:T(8,128)} %reshape.222, f32[2,8,8,16384]{3,2,1,0:T(8,128)} %add_multiply_fusion.1, f32[2,8,8,16384]{3,2,1,0:T(8,128)} %param.32, f32[8,16384]{1,0:T(8,128)S(1)} %bitcast.253), kind=kLoop, calls=%fused_computation.14 | loop fusion | flops 12582912 | bytes 42467328 | tf_op jit(solution)/shard_map/mul | solution.py:379
  (92 shorter events, 9.6 us)
Async XLA Ops:
  0.6 46.0 %copy-start = (f32[16,4]{0,1:T(4,128)S(1)}, f32[16,4]{0,1:T(4,128)}, u32[]{:S(2)}) copy-start(f32[16,4]{0,1:T(4,128)} %param.38) | copy-start | bytes 772
  2.1 129.6 %all-to-all-start = ((s32[16,2,1024]{2,1,0:T(2,128)}), s32[16,2,1024]{2,1,0:T(2,128)S(1)}, u32[]{:S(2)}, u32[]{:S(2)}) async-start(s32[16,2,1024]{2,1,0:T(2,128)} %broadcast_in_dim.18), calls=%async_computation | async-start | bytes 262144 | tf_op jit(solution)/shard_map/all_to_all | solution.py:261
  25.8 12.2 %copy-start.5 = (f32[2,8,3,16384]{3,2,1,0:T(4,128)S(1)}, f32[2,8,3,16384]{3,2,1,0:T(4,128)}, u32[]{:S(2)}) copy-start(f32[2,8,3,16384]{3,2,1,0:T(4,128)} %get-tuple-element.20) | copy-start | bytes 9437188
  25.8 12.2 %copy-start.6 = (f32[2,8,3,16384]{3,2,1,0:T(4,128)S(1)}, f32[2,8,3,16384]{3,2,1,0:T(4,128)}, u32[]{:S(2)}) copy-start(f32[2,8,3,16384]{3,2,1,0:T(4,128)} %get-tuple-element.56) | copy-start | bytes 9437188
  34.7 11.9 %copy-start.10 = (s32[1024]{0:T(1024)S(1)}, s32[1024]{0:T(1024)}, u32[]{:S(2)}) copy-start(s32[1024]{0:T(1024)} %param.37) | copy-start | bytes 12292
  34.7 12.4 %copy-start.11 = (f32[4]{0:T(128)S(1)}, f32[4]{0:T(128)}, u32[]{:S(2)}) copy-start(f32[4]{0:T(128)} %param.40) | copy-start | bytes 52
  34.7 12.4 %copy-start.12 = (s32[8]{0:T(128)S(1)}, s32[8]{0:T(128)}, u32[]{:S(2)}) copy-start(s32[8]{0:T(128)} %param.39) | copy-start | bytes 100
  34.7 12.5 %copy-start.7 = (f32[128,1024]{1,0:T(8,128)S(1)}, f32[128,1024]{1,0:T(8,128)}, u32[]{:S(2)}) copy-start(f32[128,1024]{1,0:T(8,128)} %param.34) | copy-start | bytes 1572868
  34.7 12.5 %copy-start.8 = (f32[8,1024]{1,0:T(8,128)S(1)}, f32[8,1024]{1,0:T(8,128)}, u32[]{:S(2)}) copy-start(f32[8,1024]{1,0:T(8,128)} %param.35) | copy-start | bytes 98308
  34.8 96.9 %collective-permute-start = (f32[2,8,3,16384]{3,1,2,0:T(8,128)}, f32[2,8,3,16384]{3,1,2,0:T(8,128)}, u32[]{:S(2)}, u32[]{:S(2)}) collective-permute-start(f32[2,8,3,16384]{3,1,2,0:T(8,128)} %fusion.23), channel_id=1, source_target_pairs={{0,2},{2,4},{4,6},{6,8},{8,10},{10,12},{12,14},{14,16},{16,18},{18... | collective-permute-start | bytes 9437192 | tf_op jit(solution)/shard_map/ppermute | solution.py:256
  38.0 27.7 %slice-start.4 = ((s8[8388608]{0:T(1024)(128)(4,1)}), s8[4194304]{0:T(1024)(128)(4,1)S(1)}, s32[]{:S(2)}) async-start(s8[8388608]{0:T(1024)(128)(4,1)} %bitcast.219), calls=%async_computation.6 | async-start | bytes 8388608
  38.0 32.4 %slice-start.6 = ((s8[8388608]{0:T(1024)(128)(4,1)}), s8[4194304]{0:T(1024)(128)(4,1)S(1)}, s32[]{:S(2)}) async-start(s8[8388608]{0:T(1024)(128)(4,1)} %bitcast.223), calls=%async_computation.8 | async-start | bytes 8388608
  43.3 132.1 %collective-permute-start.1 = (f32[2,8,3,16384]{3,1,2,0:T(8,128)}, f32[2,8,3,16384]{3,1,2,0:T(8,128)}, u32[]{:S(2)}, u32[]{:S(2)}) collective-permute-start(f32[2,8,3,16384]{3,1,2,0:T(8,128)} %fusion.21), channel_id=1, source_target_pairs={{2,0},{4,2},{6,4},{8,6},{10,8},{12,10},{14,12},{16,14},{18,16},{20... | collective-permute-start | bytes 9437192 | tf_op jit(solution)/shard_map/ppermute | solution.py:257
  47.2 18.4 %copy-start.9 = (s32[1024]{0:T(1024)S(1)}, s32[1024]{0:T(1024)}, u32[]{:S(2)}) copy-start(s32[1024]{0:T(1024)} %param.36) | copy-start | bytes 12292
  47.2 18.5 %slice-start.5 = ((s8[8388608]{0:T(1024)(128)(4,1)}), s8[4194304]{0:T(1024)(128)(4,1)S(1)}, s32[]{:S(2)}) async-start(s8[8388608]{0:T(1024)(128)(4,1)} %bitcast.219), calls=%async_computation.7 | async-start | bytes 8388608
  47.2 23.2 %slice-start.7 = ((s8[8388608]{0:T(1024)(128)(4,1)}), s8[4194304]{0:T(1024)(128)(4,1)S(1)}, s32[]{:S(2)}) async-start(s8[8388608]{0:T(1024)(128)(4,1)} %bitcast.223), calls=%async_computation.9 | async-start | bytes 8388608
  70.4 4.9 copy-start.4
  186.7 192.2 %all-to-all-start.1 = ((f32[2,8,128,8,128]{4,3,1,0,2:T(8,128)}), f32[2,8,128,8,128]{4,3,1,0,2:T(8,128)}, u32[]{:S(2)}, u32[]{:S(2)}) async-start(f32[2,8,128,8,128]{4,3,1,0,2:T(8,128)} %copy.108), calls=%async_computation.1 | async-start | bytes 16777216 | tf_op jit(solution)/shard_map/all_to_all | solution.py:279
  224.6 5.0 copy-start.3
  224.6 9.0 %slice-start = ((s8[8388608]{0:T(1024)(128)(4,1)}), s8[4194304]{0:T(1024)(128)(4,1)S(1)}, s32[]{:S(2)}) async-start(s8[8388608]{0:T(1024)(128)(4,1)} %bitcast.198), calls=%async_computation.2 | async-start | bytes 8388608
  229.6 4.2 slice-start.1
  431.3 20.3 %collective-permute-start.2 = (f32[8,128,128]{2,1,0:T(8,128)S(1)}, f32[8,128,128]{2,1,0:T(8,128)S(1)}, u32[]{:S(2)}, u32[]{:S(2)}) collective-permute-start(f32[8,128,128]{2,1,0:T(8,128)S(1)} %reduce_sum.44), channel_id=1, source_target_pairs={{0,1},{1,0},{2,3},{3,2},{4,5},{5,4},{6,7},{7,6},{8,9},{9,8},{10,11... | collective-permute-start | bytes 1572872 | tf_op jit(solution)/shard_map/ppermute | solution.py:374
  469.3 139.3 %collective-permute-start.4 = (f32[2,8,3,128,128]{4,3,2,1,0:T(8,128)}, f32[2,8,3,128,128]{4,3,2,1,0:T(8,128)}, u32[]{:S(2)}, u32[]{:S(2)}) collective-permute-start(f32[2,8,3,128,128]{4,3,2,1,0:T(8,128)} %get-tuple-element.18), channel_id=1, source_target_pairs={{2,0},{4,2},{6,4},{8,6},{10,8},{12,10},{14,12},{16,14},{18,16},{20... | collective-permute-start | bytes 9437192 | tf_op jit(solution)/shard_map/ppermute | solution.py:303
  472.2 136.4 %collective-permute-start.3 = (f32[2,8,3,128,128]{4,3,2,1,0:T(8,128)}, f32[2,8,3,128,128]{4,3,2,1,0:T(8,128)}, u32[]{:S(2)}, u32[]{:S(2)}) collective-permute-start(f32[2,8,3,128,128]{4,3,2,1,0:T(8,128)} %get-tuple-element.19), channel_id=1, source_target_pairs={{0,2},{2,4},{4,6},{6,8},{8,10},{10,12},{12,14},{14,16},{16,18},{18... | collective-permute-start | bytes 9437192 | tf_op jit(solution)/shard_map/ppermute | solution.py:302
  625.1 5.0 copy-start.2
  625.1 9.0 %slice-start.2 = ((s8[8388608]{0:T(1024)(128)(4,1)}), s8[4194304]{0:T(1024)(128)(4,1)S(1)}, s32[]{:S(2)}) async-start(s8[8388608]{0:T(1024)(128)(4,1)} %bitcast.208), calls=%async_computation.4 | async-start | bytes 8388608
  630.0 4.2 slice-start.3
  675.0 10.2 %collective-permute-start.5 = (f32[8,128,128]{2,1,0:T(8,128)S(1)}, f32[8,128,128]{2,1,0:T(8,128)S(1)}, u32[]{:S(2)}, u32[]{:S(2)}) collective-permute-start(f32[8,128,128]{2,1,0:T(8,128)S(1)} %reduce_sum.47), channel_id=1, source_target_pairs={{0,1},{1,0},{2,3},{3,2},{4,5},{5,4},{6,7},{7,6},{8,9},{9,8},{10,11... | collective-permute-start | bytes 1572872 | tf_op jit(solution)/shard_map/ppermute | solution.py:374
  685.7 15.6 %copy-start.1 = (f32[16,4]{0,1:T(4,128)S(1)}, f32[16,4]{0,1:T(4,128)}, u32[]{:S(2)}) copy-start(f32[16,4]{0,1:T(4,128)} %param.38) | copy-start | bytes 772

commit v7 on v6

--- a/solution.py
+++ b/solution.py
@@ -249,9 +249,12 @@
     forward_pairs = [(i, i + 1) for i in range(lines - 1)]
     backward_pairs = [(i + 1, i) for i in range(lines - 1)]
 
+    earlier = previous_image.reshape(2, cl, rows, p_len, q_len)
+    latest = current_image.reshape(2, cl, rows, p_len, q_len)
+
     def edge_blend(lo, hi):
-        cur = current_image[:, :, lo:hi]
-        return cur + momenta[0] * (cur - previous_image[:, :, lo:hi])
+        cur = latest[:, :, lo:hi]
+        return cur + momenta[0] * (cur - earlier[:, :, lo:hi])
 
     low = lax.ppermute(edge_blend(rows - HALO, rows), "line", forward_pairs)
     high = lax.ppermute(edge_blend(0, HALO), "line", backward_pairs)
@@ -260,8 +263,6 @@
     table = jnp.broadcast_to(table[None], (lines,) + table.shape)
     table = lax.all_to_all(table, "line", split_axis=0, concat_axis=2, tiled=True)[0]
 
-    earlier = previous_image.reshape(2, cl, rows, p_len, q_len)
-    latest = current_image.reshape(2, cl, rows, p_len, q_len)
     blended = latest + momenta[0] * (latest - earlier)
 
     local_taps = tap_table(tap_index, kernel_table)

time: 715 us -> 708 us (level)
  local copies, waits for them, and re-layouts: 96.4 us -> 77.2 us
  waiting for transfers between devices: 251 us -> 267 us
    slice x1 -> x0, local copies, waits for them, and re-layouts: 17.2 us -> none  [edge_blend(): cur = current_image[:, :, lo:hi]]
    all_to_all x1, waiting for transfers between devices: 119 us -> 132 us  [body(): data = lax.all_to_all(data, 'line', split_axis=2, concat_axis=3, tiled=True)]
    unnamed x54 -> x50, local copies, waits for them, and re-layouts: 16.8 us -> 17.8 us
    unnamed x19 -> x18, other arithmetic: 26.2 us -> 26.2 us
  transfers between devices with their start and end apart: 8 -> 8, of which waited for: 3 -> 3; matrix products, arithmetic and copies ran while one was open for 29% -> 26% of each run, Pallas kernels for 7% -> 8%
where the time goes in v7:
time: 708 us; the launch traced here: 698 us
  waiting for transfers between devices  267 us (38%)
  other arithmetic  215 us (30%)
  Pallas kernels  108 us (15%)
  local copies, waits for them, and re-layouts  77.2 us (11%)
  starting transfers between devices  27.6 us (4%)
    all_to_all x1, waiting for transfers between devices, body(): data = lax.all_to_all(data, 'line', split_axis=2, concat_axis=3, tiled=True)  132 us
    pallas_call x7, Pallas kernels, run_transform(): pl.pallas_call(kernel, out_shape=jax.ShapeDtypeStruct(data.shape, jnp.flo...  95.3 us
    ppermute x1, waiting for transfers between devices, body(): high = lax.ppermute(blended[:, :, :HALO], 'line', backward_pairs)  88.6 us
    ppermute x1, waiting for transfers between devices, body(): high = lax.ppermute(edge_blend(0, HALO), 'line', backward_pairs)  46.7 us
    mul x2, other arithmetic, body(): latest = shifted * factor[None, None]  31.2 us
    add x2, other arithmetic, body(): blended = latest + momenta[iteration] * (latest - earlier)  30.7 us
    reduce_sum x4, other arithmetic, body(): squares = jnp.sum(shifted * shifted, axis=(0, 1))  29.6 us
    mul x1, other arithmetic, body(): data = data * (step_length / math.sqrt(na))  26.8 us
  transfers between devices with their start and end apart: 8, of which 3 were waited for; matrix products, arithmetic and copies ran while one was open for 26% of the time, Pallas kernels for 8%

profile of v7, /device:TPU:21, one launch (start us, length us, event | category | flops | bytes accessed | tf_op | source)
XLA Modules:
  0.0 698.0 jit_solution(10407092024957094360)
XLA Ops:
  2.1 6.5 all-to-all-start
  8.6 8.4 %copy.87 = f32[2,8,8,128,128]{4,3,2,1,0:T(8,128)} copy(f32[2,8,8,128,128]{4,2,3,1,0:T(8,128)} %bitcast.219) | data formatting | bytes 16777216 | tf_op jit(solution)/shard_map/reshape | solution.py:253
  17.0 4.9 copy.88
  21.9 9.6 %fusion.16 = (f32[2,8,3,128,128]{4,3,2,1,0:T(8,128)}, f32[2,8,3,128,128]{4,3,2,1,0:T(8,128)}) fusion(f32[2,8,8,128,128]{4,3,2,1,0:T(8,128)} %copy.88, f32[2,8,8,128,128]{4,3,2,1,0:T(8,128)} %copy.87), kind=kLoop, calls=%fused_computation.35 | loop fusion | flops 4718592 | bytes 18874368 | tf_op jit(solution)/shard_map/add | solution.py:257
  31.5 3.1 collective-permute-start.1
  34.6 2.4 collective-permute-start
  37.6 18.4 %fusion.12 = (f32[1,8,128,1024]{3,2,1,0:T(8,128)}, f32[1,8,128,1024]{3,2,1,0:T(8,128)}) fusion(f32[2,8,128,1024]{3,2,1,0:T(8,128)} %param.31, f32[8,1024]{1,0:T(8,128)S(1)} %copy-done.8, f32[128,1024]{1,0:T(8,128)S(1)} %copy-done.7, f32[8]{0:T(128)S(1)} %select_reduce_fusion), kind=kLoop, calls=%fused_computation.28 | loop fusion | flops 9437184 | bytes 17334304 | tf_op jit(solution)/shard_map/mul | solution.py:274
  56.0 4.7 copy.111
  60.7 5.4 copy.112
  66.6 4.2 pad_maximum_fusion
  70.8 12.0 %fusion.1.x_ref = f32[2,64,128,128]{3,2,1,0:T(8,128)} fusion(f32[2,64,128,128]{3,2,1,0:T(8,128)} %bitcast.241, f32[2,64,128,128]{3,2,1,0:T(8,128)} %bitcast.227), kind=kLoop, calls=%fused_computation.2 | loop fusion | flops 6291456 | bytes 25165824 | tf_op jit(solution)/shard_map/add | solution.py:266
  82.8 26.8 %add_multiply_fusion.2 = f32[2,8,128,1024]{3,2,1,0:T(8,128)} fusion(f32[2,8,128,1024]{3,2,1,0:T(8,128)} %pad_maximum_fusion, f32[1024]{0:T(1024)S(1)} %get-tuple-element.42, f32[1024]{0:T(1024)S(1)} %get-tuple-element.43, f32[1024]{0:T(1024)S(1)} %get-tuple-element.44, f32[1024]{0:T(1024)S(1)} %get-tuple-element.45, f32[1024]{0:T(1024)S(1)} %get-tuple-element.46, ...), kind=kLoop, calls=%fused_computation.13 | loop fusion | flops 33554432 | bytes 16809984 | tf_op jit(solution)/shard_map/mul | solution.py:277
  109.7 13.0 %shard_map.302 = f32[2,64,128,128]{3,2,1,0:T(8,128)} custom-call(f32[2,64,128,128]{3,2,1,0:T(8,128)} %fusion.1.x_ref, f32[256,256]{1,0:T(8,128)} %constant.124.clone.w_ref.v_ref, f32[256,256]{1,0:T(8,128)} %constant.125.clone.v_ref.w_ref, f32[2,128,128]{2,1,0:T(8,128)} %constant.126.clone.t_ref), custom_call_target="tpu_custom_call" | custom-call | flops 2147483648 | bytes 16777216 | tf_op jit(solution)/shard_map/pallas_call | solution.py:182
  122.7 46.7 %collective-permute-done.1 = f32[2,8,3,128,128]{4,3,2,1,0:T(8,128)} collective-permute-done((f32[2,8,3,128,128]{4,3,2,1,0:T(8,128)}, f32[2,8,3,128,128]{4,3,2,1,0:T(8,128)}, u32[]{:S(2)}, u32[]{:S(2)}) %collective-permute-start.1) | collective-permute-done | bytes 3145760 | tf_op jit(solution)/shard_map/ppermute | solution.py:260
  170.7 5.5 copy.113
  176.2 4.6 copy.109
  180.8 8.0 %all-to-all-start.1 = ((f32[2,8,128,8,128]{4,3,1,0,2:T(8,128)}), f32[2,8,128,8,128]{4,3,1,0,2:T(8,128)}, u32[]{:S(2)}, u32[]{:S(2)}) async-start(f32[2,8,128,8,128]{4,3,1,0,2:T(8,128)} %copy.109), calls=%async_computation.1 | async-start | bytes 16777216 | tf_op jit(solution)/shard_map/all_to_all | solution.py:280
  189.5 0.7 fusion.56
  191.7 6.4 pad_maximum_fusion.1
  198.1 10.4 %shard_map.303 = f32[2,48,128,128]{3,2,1,0:T(8,128)} custom-call(f32[2,48,128,128]{3,2,1,0:T(8,128)} %bitcast.247, f32[256,256]{1,0:T(8,128)} %constant.124.clone.w_ref.v_ref, f32[256,256]{1,0:T(8,128)} %constant.125.clone.v_ref.w_ref, f32[2,128,128]{2,1,0:T(8,128)} %constant.126.clone.t_ref), custom_call_target="tpu_custom_call" | custom-call | flops 1610612736 | bytes 12582912 | tf_op jit(solution)/shard_map/pallas_call | solution.py:182
  208.5 4.6 fusion.34
  213.4 4.1 subtract_dynamic-update-slice_fusion.9
  217.6 1.0 subtract_dynamic-update-slice_fusion.8
  218.6 0.9 subtract_dynamic-update-slice_fusion.7
  219.5 0.7 add_dynamic-update-slice_fusion.1
  220.3 0.9 subtract_dynamic-update-slice_fusion.6
  221.1 0.9 subtract_dynamic-update-slice_fusion.5
  222.0 0.9 fusion.30
  223.0 4.4 broadcast_multiply_fusion.1.y_ref
  227.4 16.3 %shard_map.304 = f32[2,64,128,128]{3,2,1,0:T(8,128)} custom-call(f32[2,64,128,128]{3,2,1,0:T(8,128)} %broadcast_multiply_fusion.1.y_ref, f32[256,256]{1,0:T(8,128)} %constant.124.clone.w_ref.v_ref, f32[256,256]{1,0:T(8,128)} %constant.125.clone.v_ref.w_ref, f32[2,128,128]{2,1,0:T(8,128)} %constant.127.clone.t_ref), custom_call_target="tpu_custom_call" | custom-call | flops 2147483648 | bytes 16777216 | tf_op jit(solution)/shard_map/pallas_call | solution.py:182
  243.7 131.9 %all-to-all-done.1 = f32[2,8,128,8,128]{4,3,1,0,2:T(8,128)} async-done(((f32[2,8,128,8,128]{4,3,1,0,2:T(8,128)}), f32[2,8,128,8,128]{4,3,1,0,2:T(8,128)}, u32[]{:S(2)}, u32[]{:S(2)}) %all-to-all-start.1) | async-done | bytes 8388640 | tf_op jit(solution)/shard_map/all_to_all | solution.py:280
  375.5 7.9 %copy.104 = f32[2,8,8,16,8,128]{5,4,3,2,1,0:T(8,128)} copy(f32[2,8,8,16,8,128]{5,4,1,0,2,3:T(8,128)} %bitcast.46) | data formatting | bytes 16777216 | tf_op jit(solution)/shard_map/all_to_all | solution.py:280
  383.5 13.1 %shard_map.305 = f32[128,128,128]{2,1,0:T(8,128)} custom-call(f32[128,128,128]{2,1,0:T(8,128)} %bitcast.244), custom_call_target="tpu_custom_call" | custom-call | bytes 16777216 | tf_op jit(solution)/shard_map/pallas_call | solution.py:161
  396.6 16.4 %shard_map.306 = f32[2,64,128,128]{3,2,1,0:T(8,128)} custom-call(f32[2,64,128,128]{3,2,1,0:T(8,128)} %bitcast.245, f32[256,256]{1,0:T(8,128)} %constant.124.clone.w_ref.v_ref, f32[256,256]{1,0:T(8,128)} %constant.125.clone.v_ref.w_ref, f32[2,128,128]{2,1,0:T(8,128)} %constant.127.clone.t_ref), custom_call_target="tpu_custom_call" | custom-call | flops 2147483648 | bytes 16777216 | tf_op jit(solution)/shard_map/pallas_call | solution.py:182
  413.0 12.2 %multiply_reduce_fusion.1 = f32[64,128,128]{2,1,0:T(8,128)} fusion(f32[2,64,128,128]{3,2,1,0:T(8,128)} %shard_map.306, f32[2,64,128,128]{3,2,1,0:T(8,128)} %fusion.1.x_ref, f32[2,64,128,128]{3,2,1,0:T(8,128)} %shard_map.304), kind=kLoop, calls=%fused_computation.10 | loop fusion | flops 7340032 | bytes 29360128 | tf_op jit(solution)/shard_map/reduce_sum | solution.py:373
  425.2 2.5 reduce_sum.44
  427.7 1.5 collective-permute-start.2
  429.2 9.4 %reshape.212 = f32[2,8,8,16384]{3,2,1,0:T(8,128)} reshape(f32[2,64,128,128]{3,2,1,0:T(8,128)} %shard_map.304) | data formatting | bytes 16777216 | tf_op jit(solution)/shard_map/reshape | solution.py:372
  438.5 9.5 %reshape.216 = f32[2,8,8,16384]{3,2,1,0:T(8,128)} reshape(f32[2,64,128,128]{3,2,1,0:T(8,128)} %shard_map.306) | data formatting | bytes 16777216 | tf_op jit(solution)/shard_map/reshape | solution.py:371
  448.5 14.1 %multiply_add_fusion = f32[2,8,8,128,128]{4,3,2,1,0:T(8,128)S(1)} fusion(f32[2,8,8,128,128]{4,3,2,1,0:T(8,128)} %bitcast.217, f32[2,8,8,128,128]{4,3,2,1,0:T(8,128)} %bitcast.218, f32[8,128,128]{2,1,0:T(8,128)S(1)} %maximum_divide_fusion, f32[2,8,8,128,128]{4,2,3,1,0:T(8,128)} %bitcast.224, f32[2,8,8,128,128]{4,2,3,1,0:T(8,128)} %bitcast.220), kind=kLoop, calls=%fused_computation.9 | loop fusion | flops 18874368 | bytes 42467328 | tf_op jit(solution)/shard_map/add | solution.py:302
  462.6 3.0 fusion.63
  465.6 2.9 collective-permute-start.4
  468.5 2.4 collective-permute-start.3
  471.5 16.6 %fusion.3.x_ref = f32[2,64,128,128]{3,2,1,0:T(8,128)} fusion(f32[64,128,128]{2,1,0:T(8,128)S(1)} %bitcast.250, f32[2,64,128,128]{3,2,1,0:T(8,128)} %shard_map.306, f32[2,64,128,128]{3,2,1,0:T(8,128)} %fusion.1.x_ref, f32[2,64,128,128]{3,2,1,0:T(8,128)} %shard_map.304, f32[2,64,128,128]{3,2,1,0:T(8,128)} %bitcast.228), kind=kLoop, calls=%fused_computation.5 | loop fusion | flops 12582912 | bytes 46137344 | tf_op jit(solution)/shard_map/add | solution.py:302
  488.1 12.7 %shard_map.307 = f32[2,64,128,128]{3,2,1,0:T(8,128)} custom-call(f32[2,64,128,128]{3,2,1,0:T(8,128)} %fusion.3.x_ref, f32[256,256]{1,0:T(8,128)} %constant.124.clone.w_ref.v_ref, f32[256,256]{1,0:T(8,128)} %constant.125.clone.v_ref.w_ref, f32[2,128,128]{2,1,0:T(8,128)} %constant.126.clone.t_ref), custom_call_target="tpu_custom_call" | custom-call | flops 2147483648 | bytes 16777216 | tf_op jit(solution)/shard_map/pallas_call | solution.py:182
  500.8 15.6 %add_multiply_fusion.1 = f32[2,8,8,16384]{3,2,1,0:T(8,128)} fusion(f32[2,8,8,16384]{3,2,1,0:T(8,128)} %reshape.216, f32[2,8,8,16384]{3,2,1,0:T(8,128)} %reshape.212, f32[2,8,8,16384]{3,2,1,0:T(8,128)} %param.32, f32[2,8,8,16384]{3,2,1,0:T(8,128)} %param.33, f32[8,16384]{1,0:T(8,128)S(1)} %bitcast.254), kind=kLoop, calls=%fused_computation.12 | loop fusion | flops 12582912 | bytes 42467328 | tf_op jit(solution)/shard_map/mul | solution.py:380
  516.4 88.6 %collective-permute-done.4 = f32[2,8,3,128,128]{4,3,2,1,0:T(8,128)} collective-permute-done((f32[2,8,3,128,128]{4,3,2,1,0:T(8,128)}, f32[2,8,3,128,128]{4,3,2,1,0:T(8,128)}, u32[]{:S(2)}, u32[]{:S(2)}) %collective-permute-start.4) | collective-permute-done | bytes 3145760 | tf_op jit(solution)/shard_map/ppermute | solution.py:304
  605.0 6.3 pad_maximum_fusion.2
  611.3 10.1 %shard_map.308 = f32[2,48,128,128]{3,2,1,0:T(8,128)} custom-call(f32[2,48,128,128]{3,2,1,0:T(8,128)} %bitcast.246, f32[256,256]{1,0:T(8,128)} %constant.124.clone.w_ref.v_ref, f32[256,256]{1,0:T(8,128)} %constant.125.clone.v_ref.w_ref, f32[2,128,128]{2,1,0:T(8,128)} %constant.126.clone.t_ref), custom_call_target="tpu_custom_call" | custom-call | flops 1610612736 | bytes 12582912 | tf_op jit(solution)/shard_map/pallas_call | solution.py:182
  621.5 4.6 fusion.26
  626.4 4.1 subtract_dynamic-update-slice_fusion.4
  630.6 1.0 subtract_dynamic-update-slice_fusion.3
  631.6 0.9 subtract_dynamic-update-slice_fusion.2
  632.5 0.7 add_dynamic-update-slice_fusion
  633.3 0.9 subtract_dynamic-update-slice_fusion.1
  634.1 0.9 subtract_dynamic-update-slice_fusion
  635.0 0.9 fusion.22
  636.0 4.2 broadcast_multiply_fusion.y_ref
  640.2 16.3 %shard_map.309 = f32[2,64,128,128]{3,2,1,0:T(8,128)} custom-call(f32[2,64,128,128]{3,2,1,0:T(8,128)} %broadcast_multiply_fusion.y_ref, f32[256,256]{1,0:T(8,128)} %constant.124.clone.w_ref.v_ref, f32[256,256]{1,0:T(8,128)} %constant.125.clone.v_ref.w_ref, f32[2,128,128]{2,1,0:T(8,128)} %constant.127.clone.t_ref), custom_call_target="tpu_custom_call" | custom-call | flops 2147483648 | bytes 16777216 | tf_op jit(solution)/shard_map/pallas_call | solution.py:182
  656.5 12.4 %multiply_reduce_fusion = f32[64,128,128]{2,1,0:T(8,128)} fusion(f32[2,64,128,128]{3,2,1,0:T(8,128)} %shard_map.306, f32[2,64,128,128]{3,2,1,0:T(8,128)} %fusion.3.x_ref, f32[2,64,128,128]{3,2,1,0:T(8,128)} %shard_map.309), kind=kLoop, calls=%fused_computation.7 | loop fusion | flops 7340032 | bytes 29360128 | tf_op jit(solution)/shard_map/reduce_sum | solution.py:373
  668.9 2.5 reduce_sum.47
  671.4 0.9 collective-permute-start.5
  672.3 9.4 %reshape.222 = f32[2,8,8,16384]{3,2,1,0:T(8,128)} reshape(f32[2,64,128,128]{3,2,1,0:T(8,128)} %shard_map.309) | data formatting | bytes 16777216 | tf_op jit(solution)/shard_map/reshape | solution.py:372
  682.2 15.6 %add_multiply_fusion = f32[2,8,8,16384]{3,2,1,0:T(8,128)} fusion(f32[2,8,8,16384]{3,2,1,0:T(8,128)} %reshape.216, f32[2,8,8,16384]{3,2,1,0:T(8,128)} %reshape.222, f32[2,8,8,16384]{3,2,1,0:T(8,128)} %add_multiply_fusion.1, f32[2,8,8,16384]{3,2,1,0:T(8,128)} %param.32, f32[8,16384]{1,0:T(8,128)S(1)} %bitcast.255), kind=kLoop, calls=%fused_computation.8 | loop fusion | flops 12582912 | bytes 42467328 | tf_op jit(solution)/shard_map/mul | solution.py:380
  (85 shorter events, 8.5 us)
Async XLA Ops:
  0.6 36.3 %copy-start = (f32[16,4]{0,1:T(4,128)S(1)}, f32[16,4]{0,1:T(4,128)}, u32[]{:S(2)}) copy-start(f32[16,4]{0,1:T(4,128)} %param.38) | copy-start | bytes 772
  2.1 120.7 %all-to-all-start = ((s32[16,2,1024]{2,1,0:T(2,128)}), s32[16,2,1024]{2,1,0:T(2,128)S(1)}, u32[]{:S(2)}, u32[]{:S(2)}) async-start(s32[16,2,1024]{2,1,0:T(2,128)} %broadcast_in_dim.18), calls=%async_computation | async-start | bytes 262144 | tf_op jit(solution)/shard_map/all_to_all | solution.py:264
  8.5 8.4 %copy-start.2 = (f32[2,8,8,16384]{3,2,1,0:T(8,128)S(1)}, f32[2,8,8,16384]{3,2,1,0:T(8,128)}, u32[]{:S(2)}) copy-start(f32[2,8,8,16384]{3,2,1,0:T(8,128)} %param.33) | copy-start | bytes 25165828
  17.0 39.0 %slice-start.4 = ((s8[8388608]{0:T(1024)(128)(4,1)}), s8[4194304]{0:T(1024)(128)(4,1)S(1)}, s32[]{:S(2)}) async-start(s8[8388608]{0:T(1024)(128)(4,1)} %bitcast.221), calls=%async_computation.6 | async-start | bytes 8388608
  21.8 15.1 %copy-start.10 = (s32[1024]{0:T(1024)S(1)}, s32[1024]{0:T(1024)}, u32[]{:S(2)}) copy-start(s32[1024]{0:T(1024)} %param.37) | copy-start | bytes 12292
  21.8 15.6 %copy-start.11 = (f32[4]{0:T(128)S(1)}, f32[4]{0:T(128)}, u32[]{:S(2)}) copy-start(f32[4]{0:T(128)} %param.40) | copy-start | bytes 52
  21.8 15.6 %copy-start.12 = (s32[8]{0:T(128)S(1)}, s32[8]{0:T(128)}, u32[]{:S(2)}) copy-start(s32[8]{0:T(128)} %param.39) | copy-start | bytes 100
  21.8 15.7 %copy-start.7 = (f32[128,1024]{1,0:T(8,128)S(1)}, f32[128,1024]{1,0:T(8,128)}, u32[]{:S(2)}) copy-start(f32[128,1024]{1,0:T(8,128)} %param.34) | copy-start | bytes 1572868
  21.8 15.7 %copy-start.8 = (f32[8,1024]{1,0:T(8,128)S(1)}, f32[8,1024]{1,0:T(8,128)}, u32[]{:S(2)}) copy-start(f32[8,1024]{1,0:T(8,128)} %param.35) | copy-start | bytes 98308
  21.8 34.1 %slice-start.5 = ((s8[8388608]{0:T(1024)(128)(4,1)}), s8[4194304]{0:T(1024)(128)(4,1)S(1)}, s32[]{:S(2)}) async-start(s8[8388608]{0:T(1024)(128)(4,1)} %bitcast.221), calls=%async_computation.7 | async-start | bytes 8388608
  31.5 138.0 %collective-permute-start.1 = (f32[2,8,3,128,128]{4,3,2,1,0:T(8,128)}, f32[2,8,3,128,128]{4,3,2,1,0:T(8,128)}, u32[]{:S(2)}, u32[]{:S(2)}) collective-permute-start(f32[2,8,3,128,128]{4,3,2,1,0:T(8,128)} %get-tuple-element.16), channel_id=1, source_target_pairs={{2,0},{4,2},{6,4},{8,6},{10,8},{12,10},{14,12},{16,14},{18,16},{20... | collective-permute-start | bytes 9437192 | tf_op jit(solution)/shard_map/ppermute | solution.py:260
  34.6 134.9 %collective-permute-start = (f32[2,8,3,128,128]{4,3,2,1,0:T(8,128)}, f32[2,8,3,128,128]{4,3,2,1,0:T(8,128)}, u32[]{:S(2)}, u32[]{:S(2)}) collective-permute-start(f32[2,8,3,128,128]{4,3,2,1,0:T(8,128)} %get-tuple-element.17), channel_id=1, source_target_pairs={{0,2},{2,4},{4,6},{6,8},{8,10},{10,12},{12,14},{14,16},{16,18},{18... | collective-permute-start | bytes 9437192 | tf_op jit(solution)/shard_map/ppermute | solution.py:259
  37.6 18.4 %copy-start.9 = (s32[1024]{0:T(1024)S(1)}, s32[1024]{0:T(1024)}, u32[]{:S(2)}) copy-start(s32[1024]{0:T(1024)} %param.36) | copy-start | bytes 12292
  60.7 5.4 copy-start.5
  60.7 5.9 copy-start.6
  180.8 194.8 %all-to-all-start.1 = ((f32[2,8,128,8,128]{4,3,1,0,2:T(8,128)}), f32[2,8,128,8,128]{4,3,1,0,2:T(8,128)}, u32[]{:S(2)}, u32[]{:S(2)}) async-start(f32[2,8,128,8,128]{4,3,1,0,2:T(8,128)} %copy.109), calls=%async_computation.1 | async-start | bytes 16777216 | tf_op jit(solution)/shard_map/all_to_all | solution.py:280
  208.4 5.0 copy-start.4
  208.5 9.0 %slice-start = ((s8[8388608]{0:T(1024)(128)(4,1)}), s8[4194304]{0:T(1024)(128)(4,1)S(1)}, s32[]{:S(2)}) async-start(s8[8388608]{0:T(1024)(128)(4,1)} %bitcast.199), calls=%async_computation.2 | async-start | bytes 8388608
  213.4 4.2 slice-start.1
  427.7 20.3 %collective-permute-start.2 = (f32[8,128,128]{2,1,0:T(8,128)S(1)}, f32[8,128,128]{2,1,0:T(8,128)S(1)}, u32[]{:S(2)}, u32[]{:S(2)}) collective-permute-start(f32[8,128,128]{2,1,0:T(8,128)S(1)} %reduce_sum.44), channel_id=1, source_target_pairs={{0,1},{1,0},{2,3},{3,2},{4,5},{5,4},{6,7},{7,6},{8,9},{9,8},{10,11... | collective-permute-start | bytes 1572872 | tf_op jit(solution)/shard_map/ppermute | solution.py:375
  465.6 139.3 %collective-permute-start.4 = (f32[2,8,3,128,128]{4,3,2,1,0:T(8,128)}, f32[2,8,3,128,128]{4,3,2,1,0:T(8,128)}, u32[]{:S(2)}, u32[]{:S(2)}) collective-permute-start(f32[2,8,3,128,128]{4,3,2,1,0:T(8,128)} %get-tuple-element.20), channel_id=1, source_target_pairs={{2,0},{4,2},{6,4},{8,6},{10,8},{12,10},{14,12},{16,14},{18,16},{20... | collective-permute-start | bytes 9437192 | tf_op jit(solution)/shard_map/ppermute | solution.py:304
  468.5 136.4 %collective-permute-start.3 = (f32[2,8,3,128,128]{4,3,2,1,0:T(8,128)}, f32[2,8,3,128,128]{4,3,2,1,0:T(8,128)}, u32[]{:S(2)}, u32[]{:S(2)}) collective-permute-start(f32[2,8,3,128,128]{4,3,2,1,0:T(8,128)} %get-tuple-element.21), channel_id=1, source_target_pairs={{0,2},{2,4},{4,6},{6,8},{8,10},{10,12},{12,14},{14,16},{16,18},{18... | collective-permute-start | bytes 9437192 | tf_op jit(solution)/shard_map/ppermute | solution.py:303
  621.5 5.0 copy-start.3
  621.5 9.0 %slice-start.2 = ((s8[8388608]{0:T(1024)(128)(4,1)}), s8[4194304]{0:T(1024)(128)(4,1)S(1)}, s32[]{:S(2)}) async-start(s8[8388608]{0:T(1024)(128)(4,1)} %bitcast.209), calls=%async_computation.4 | async-start | bytes 8388608
  626.4 4.2 slice-start.3
  671.4 10.2 %collective-permute-start.5 = (f32[8,128,128]{2,1,0:T(8,128)S(1)}, f32[8,128,128]{2,1,0:T(8,128)S(1)}, u32[]{:S(2)}, u32[]{:S(2)}) collective-permute-start(f32[8,128,128]{2,1,0:T(8,128)S(1)} %reduce_sum.47), channel_id=1, source_target_pairs={{0,1},{1,0},{2,3},{3,2},{4,5},{5,4},{6,7},{7,6},{8,9},{9,8},{10,11... | collective-permute-start | bytes 1572872 | tf_op jit(solution)/shard_map/ppermute | solution.py:375
  682.2 15.6 %copy-start.1 = (f32[16,4]{0,1:T(4,128)S(1)}, f32[16,4]{0,1:T(4,128)}, u32[]{:S(2)}) copy-start(f32[16,4]{0,1:T(4,128)} %param.38) | copy-start | bytes 772

commit v8 on v7

--- a/solution.py
+++ b/solution.py
@@ -277,7 +277,13 @@
     data = data * (step_length / math.sqrt(na))
     data, low, high, table = lax.optimization_barrier((data, low, high, table))
     data = data.reshape(2, cl, data.shape[2], data.shape[3] // p_len, p_len)
-    data = lax.all_to_all(data, "line", split_axis=2, concat_axis=3, tiled=True)
+    halves = 2 if cl % 2 == 0 else 1
+    pieces = []
+    for h in range(halves):
+        piece = data[:, h * cl // halves : (h + 1) * cl // halves]
+        if pieces:
+            piece, pieces[-1] = lax.optimization_barrier((piece, pieces[-1]))
+        pieces.append(lax.all_to_all(piece, "line", split_axis=2, concat_axis=3, tiled=True))
     taps = tap_table(table[0], kernel_table)
     weights = shift_weights(table[1], taps)
 
@@ -366,9 +372,12 @@
         resid = coef[None, :, None, None, None] * gram
         grad = inverse_transform(resid.reshape(2, -1, p_len, q_len), p_len, q_len)
         if undo is None:
-            undo = swap_minor(data.reshape(-1, q_len, p_len))
-            undo = inverse_transform(undo.reshape(2, -1, p_len, q_len), p_len, q_len)
-            undo = undo.reshape(blended.shape)
+            undo = []
+            for piece in pieces:
+                part = swap_minor(piece.reshape(-1, q_len, p_len))
+                part = inverse_transform(part.reshape(2, -1, p_len, q_len), p_len, q_len)
+                undo.append(part.reshape(2, -1, rows, p_len, q_len))
+            undo = jnp.concatenate(undo, axis=1)
         shifted = blended - grad.reshape(blended.shape) + undo
         squares = jnp.sum(shifted * shifted, axis=(0, 1))
         if chans == 2:

time: 708 us -> 687 us (0.970)
  waiting for transfers between devices: 267 us -> 214 us
  local copies, waits for them, and re-layouts: 77.2 us -> 101 us
    ppermute x1, waiting for transfers between devices: 46.7 us -> 0.01 us  [body(): high = lax.ppermute(edge_blend(0, HALO), 'line', backward_pairs)]
    all_to_all x1 -> x2, waiting for transfers between devices: 132 us -> 87.5 us  [body(): lax.all_to_all(piece, 'line', split_axis=2, concat_axis=3, tiled=True)]
    all_to_all x1, waiting for transfers between devices: 0.01 us -> 37.3 us  [body(): lax.all_to_all(table, 'line', split_axis=0, concat_axis=2, tiled=True)[0]]
    ppermute x1, waiting for transfers between devices: 0.01 us -> 20.7 us  [body(): low = lax.ppermute(blended[:, :, rows - HALO:], 'line', forward_pairs)]
    ppermute x1, waiting for transfers between devices: 88.6 us -> 68.8 us  [body(): high = lax.ppermute(blended[:, :, :HALO], 'line', backward_pairs)]
    concatenate x0 -> x3, local copies, waits for them, and re-layouts: none -> 15.1 us  [body(): undo = jnp.concatenate(undo, axis=1)]
    unnamed x50, local copies, waits for them, and re-layouts: 17.8 us -> 31.8 us
    reshape x2 -> x0, local copies, waits for them, and re-layouts: 14 us -> none  [the longest x1 9.45 us: body(): undo = undo.reshape(blended.shape)]
  transfers between devices with their start and end apart: 8 -> 9, of which waited for: 3 -> 5; matrix products, arithmetic and copies ran while one was open for 26% -> 26% of each run, Pallas kernels for 8% -> 10%
where the time goes in v8:
time: 687 us; the launch traced here: 679 us
  other arithmetic  215 us (31%)
  waiting for transfers between devices  214 us (31%)
  Pallas kernels  112 us (16%)
  local copies, waits for them, and re-layouts  101 us (15%)
  starting transfers between devices  34.5 us (5%)
    pallas_call x8, Pallas kernels, run_transform(): pl.pallas_call(kernel, out_shape=jax.ShapeDtypeStruct(data.shape, jnp.flo...  97.2 us
    all_to_all x2, waiting for transfers between devices, body(): lax.all_to_all(piece, 'line', split_axis=2, concat_axis=3, tiled=True)  87.5 us
    ppermute x1, waiting for transfers between devices, body(): high = lax.ppermute(blended[:, :, :HALO], 'line', backward_pairs)  68.8 us
    all_to_all x1, waiting for transfers between devices, body(): lax.all_to_all(table, 'line', split_axis=0, concat_axis=2, tiled=True)[0]  37.3 us
    unnamed x50, local copies, waits for them, and re-layouts  31.8 us
    mul x2, other arithmetic, body(): latest = shifted * factor[None, None]  31.2 us
    add x2, other arithmetic, body(): blended = latest + momenta[iteration] * (latest - earlier)  30.4 us
    reduce_sum x4, other arithmetic, body(): squares = jnp.sum(shifted * shifted, axis=(0, 1))  29.9 us
  transfers between devices with their start and end apart: 9, of which 5 were waited for; matrix products, arithmetic and copies ran while one was open for 26% of the time, Pallas kernels for 10%

profile of v8, /device:TPU:21, one launch (start us, length us, event | category | flops | bytes accessed | tf_op | source)
XLA Modules:
  0.0 678.9 jit_solution(4003010687339694675)
XLA Ops:
  0.7 5.0 copy.94
  6.4 4.9 copy.93
  11.3 5.7 fusion.16
  17.0 3.1 collective-permute-start
  20.1 3.1 collective-permute-start.1
  23.9 7.5 %all-to-all-start = ((s32[16,2,1024]{2,1,0:T(2,128)}), s32[16,2,1024]{2,1,0:T(2,128)S(1)}, u32[]{:S(2)}, u32[]{:S(2)}) async-start(s32[16,2,1024]{2,1,0:T(2,128)} %broadcast_in_dim.18), calls=%async_computation | async-start | bytes 262144 | tf_op jit(solution)/shard_map/all_to_all | solution.py:264
  32.0 17.2 %fusion.12 = (f32[1,8,128,1024]{3,2,1,0:T(8,128)S(1)}, f32[1,8,128,1024]{3,2,1,0:T(8,128)S(1)}) fusion(f32[2,8,128,1024]{3,2,1,0:T(8,128)} %param.34, f32[8,1024]{1,0:T(8,128)S(1)} %copy-done.9, f32[128,1024]{1,0:T(8,128)} %param.37, f32[8]{0:T(128)S(1)} %select_reduce_fusion), kind=kLoop, calls=%fused_computation.29 | loop fusion | flops 9437184 | bytes 17334304 | tf_op jit(solution)/shard_map/mul | solution.py:274
  49.2 8.2 %copy.121 = f32[16,8,128,128]{3,2,1,0:T(8,128)} copy(f32[16,8,128,128]{3,1,2,0:T(8,128)} %bitcast.237) | data formatting | bytes 16777216
  57.5 8.1 %copy.120 = f32[16,8,128,128]{3,2,1,0:T(8,128)} copy(f32[16,8,128,128]{3,1,2,0:T(8,128)} %bitcast.230) | data formatting | bytes 16777216
  65.6 4.2 pad_maximum_fusion
  69.8 11.9 %fusion.1.x_ref = f32[2,64,128,128]{3,2,1,0:T(8,128)} fusion(f32[2,64,128,128]{3,2,1,0:T(8,128)} %bitcast.257, f32[2,64,128,128]{3,2,1,0:T(8,128)} %bitcast.239), kind=kLoop, calls=%fused_computation.2 | loop fusion | flops 6291456 | bytes 25165824 | tf_op jit(solution)/shard_map/add | solution.py:266
  81.7 26.6 %add_multiply_fusion.2 = f32[2,8,128,1024]{3,2,1,0:T(8,128)} fusion(f32[2,8,128,1024]{3,2,1,0:T(8,128)} %pad_maximum_fusion, f32[1024]{0:T(1024)S(1)} %get-tuple-element.48, f32[1024]{0:T(1024)S(1)} %get-tuple-element.49, f32[1024]{0:T(1024)S(1)} %get-tuple-element.50, f32[1024]{0:T(1024)S(1)} %get-tuple-element.51, f32[1024]{0:T(1024)S(1)} %get-tuple-element.52, ...), kind=kLoop, calls=%fused_computation.14 | loop fusion | flops 33554432 | bytes 16809984 | tf_op jit(solution)/shard_map/mul | solution.py:277
  108.6 12.9 %shard_map.329 = f32[2,64,128,128]{3,2,1,0:T(8,128)} custom-call(f32[2,64,128,128]{3,2,1,0:T(8,128)} %fusion.1.x_ref, f32[256,256]{1,0:T(8,128)} %constant.124.clone.w_ref.v_ref, f32[256,256]{1,0:T(8,128)} %constant.125.clone.v_ref.w_ref, f32[2,128,128]{2,1,0:T(8,128)} %constant.126.clone.t_ref), custom_call_target="tpu_custom_call" | custom-call | flops 2147483648 | bytes 16777216 | tf_op jit(solution)/shard_map/pallas_call | solution.py:182
  121.5 37.3 %all-to-all-done = s32[16,2,1024]{2,1,0:T(2,128)S(1)} async-done(((s32[16,2,1024]{2,1,0:T(2,128)}), s32[16,2,1024]{2,1,0:T(2,128)S(1)}, u32[]{:S(2)}, u32[]{:S(2)}) %all-to-all-start) | async-done | bytes 131104 | tf_op jit(solution)/shard_map/all_to_all | solution.py:264
  158.8 5.5 copy.122
  164.2 2.7 fusion.64
  166.9 2.6 copy.119
  169.5 5.6 all-to-all-start.1
  176.1 4.8 copy.118
  182.4 85.2 %all-to-all-done.1 = f32[2,4,128,8,128]{4,3,1,0,2:T(8,128)} async-done(((f32[2,4,128,8,128]{4,3,1,0,2:T(8,128)}), f32[2,4,128,8,128]{4,3,1,0,2:T(8,128)}, u32[]{:S(2)}, u32[]{:S(2)}) %all-to-all-start.1) | async-done | bytes 4194336 | tf_op jit(solution)/shard_map/all_to_all | solution.py:286
  267.6 4.8 copy.130
  272.4 7.1 %all-to-all-start.2 = ((f32[2,4,128,8,128]{4,3,1,0,2:T(8,128)}), f32[2,4,128,8,128]{4,3,1,0,2:T(8,128)}, u32[]{:S(2)}, u32[]{:S(2)}) async-start(f32[2,4,128,8,128]{4,3,1,0,2:T(8,128)} %copy.118), calls=%async_computation.2 | async-start | bytes 8388608 | tf_op jit(solution)/shard_map/all_to_all | solution.py:286
  281.1 6.4 pad_maximum_fusion.2
  287.5 9.9 %shard_map.330 = f32[2,48,128,128]{3,2,1,0:T(8,128)} custom-call(f32[2,48,128,128]{3,2,1,0:T(8,128)} %bitcast.261, f32[256,256]{1,0:T(8,128)} %constant.124.clone.w_ref.v_ref, f32[256,256]{1,0:T(8,128)} %constant.125.clone.v_ref.w_ref, f32[2,128,128]{2,1,0:T(8,128)} %constant.126.clone.t_ref), custom_call_target="tpu_custom_call" | custom-call | flops 1610612736 | bytes 12582912 | tf_op jit(solution)/shard_map/pallas_call | solution.py:182
  297.4 4.4 fusion.34
  302.4 4.0 subtract_dynamic-update-slice_fusion.9
  306.6 1.0 subtract_dynamic-update-slice_fusion.8
  312.2 4.4 broadcast_multiply_fusion.1.y_ref
  316.6 16.4 %shard_map.331 = f32[2,64,128,128]{3,2,1,0:T(8,128)} custom-call(f32[2,64,128,128]{3,2,1,0:T(8,128)} %broadcast_multiply_fusion.1.y_ref, f32[256,256]{1,0:T(8,128)} %constant.124.clone.w_ref.v_ref, f32[256,256]{1,0:T(8,128)} %constant.125.clone.v_ref.w_ref, f32[2,128,128]{2,1,0:T(8,128)} %constant.127.clone.t_ref), custom_call_target="tpu_custom_call" | custom-call | flops 2147483648 | bytes 16777216 | tf_op jit(solution)/shard_map/pallas_call | solution.py:182
  333.0 9.4 %reshape.228 = f32[2,8,8,16384]{3,2,1,0:T(8,128)} reshape(f32[2,64,128,128]{3,2,1,0:T(8,128)} %shard_map.331) | data formatting | bytes 16777216 | tf_op jit(solution)/shard_map/reshape | solution.py:381
  342.4 7.2 %shard_map.332 = f32[64,128,128]{2,1,0:T(8,128)} custom-call(f32[64,128,128]{2,1,0:T(8,128)} %bitcast.264), custom_call_target="tpu_custom_call" | custom-call | bytes 8388608 | tf_op jit(solution)/shard_map/pallas_call | solution.py:161
  349.6 9.3 %shard_map.333 = f32[2,32,128,128]{3,2,1,0:T(8,128)} custom-call(f32[2,32,128,128]{3,2,1,0:T(8,128)} %bitcast.265, f32[256,256]{1,0:T(8,128)} %constant.124.clone.w_ref.v_ref, f32[256,256]{1,0:T(8,128)} %constant.125.clone.v_ref.w_ref, f32[2,128,128]{2,1,0:T(8,128)} %constant.127.clone.t_ref), custom_call_target="tpu_custom_call" | custom-call | flops 1073741824 | bytes 8388608 | tf_op jit(solution)/shard_map/pallas_call | solution.py:182
  358.9 4.9 concatenate.21
  363.8 4.5 constant_dynamic-update-slice_fusion.9
  368.3 2.3 all-to-all-done.2
  370.6 4.8 copy.111
  375.3 7.3 %shard_map.334 = f32[64,128,128]{2,1,0:T(8,128)} custom-call(f32[64,128,128]{2,1,0:T(8,128)} %bitcast.266), custom_call_target="tpu_custom_call" | custom-call | bytes 8388608 | tf_op jit(solution)/shard_map/pallas_call | solution.py:161
  382.6 9.3 %shard_map.335 = f32[2,32,128,128]{3,2,1,0:T(8,128)} custom-call(f32[2,32,128,128]{3,2,1,0:T(8,128)} %bitcast.267, f32[256,256]{1,0:T(8,128)} %constant.124.clone.w_ref.v_ref, f32[256,256]{1,0:T(8,128)} %constant.125.clone.v_ref.w_ref, f32[2,128,128]{2,1,0:T(8,128)} %constant.127.clone.t_ref), custom_call_target="tpu_custom_call" | custom-call | flops 1073741824 | bytes 8388608 | tf_op jit(solution)/shard_map/pallas_call | solution.py:182
  391.9 4.9 concatenate.22
  396.9 4.0 pad_maximum_fusion.1
  400.9 12.5 %multiply_reduce_fusion.1 = f32[64,128,128]{2,1,0:T(8,128)} fusion(f32[2,64,128,128]{3,2,1,0:T(8,128)S(1)} %bitcast.233, f32[2,64,128,128]{3,2,1,0:T(8,128)} %fusion.1.x_ref, f32[2,64,128,128]{3,2,1,0:T(8,128)} %shard_map.331), kind=kLoop, calls=%fused_computation.11 | loop fusion | flops 7340032 | bytes 29360128 | tf_op jit(solution)/shard_map/reduce_sum | solution.py:382
  413.4 2.5 reduce_sum.44
  415.9 1.5 collective-permute-start.2
  417.5 5.3 constant_dynamic-update-slice_fusion.8
  422.7 1.3 maximum_divide_fusion
  424.0 13.8 %multiply_add_fusion = f32[2,8,8,128,128]{4,3,2,1,0:T(8,128)} fusion(f32[2,8,8,128,128]{4,3,2,1,0:T(8,128)} %bitcast.229, f32[8,128,128]{2,1,0:T(8,128)S(1)} %maximum_divide_fusion, f32[2,8,8,128,128]{4,2,3,1,0:T(8,128)} %bitcast.238, f32[2,8,8,128,128]{4,2,3,1,0:T(8,128)} %bitcast.231, f32[2,4,8,128,128]{4,3,2,1,0:T(8,128)S(1)} %bitcast.244, ...), kind=kLoop, calls=%fused_computation.10 | loop fusion | flops 20971520 | bytes 42467328 | tf_op jit(solution)/shard_map/add | solution.py:308
  437.9 6.3 fusion.63
  444.2 1.9 collective-permute-start.3
  446.1 4.3 collective-permute-start.4
  451.2 16.5 %fusion.3.x_ref = f32[2,64,128,128]{3,2,1,0:T(8,128)} fusion(f32[64,128,128]{2,1,0:T(8,128)S(1)} %bitcast.268, f32[2,64,128,128]{3,2,1,0:T(8,128)} %bitcast.234, f32[2,64,128,128]{3,2,1,0:T(8,128)} %fusion.1.x_ref, f32[2,64,128,128]{3,2,1,0:T(8,128)} %shard_map.331, f32[2,64,128,128]{3,2,1,0:T(8,128)} %bitcast.240), kind=kLoop, calls=%fused_computation.5 | loop fusion | flops 12582912 | bytes 46137344 | tf_op jit(solution)/shard_map/add | solution.py:308
  467.8 12.8 %shard_map.336 = f32[2,64,128,128]{3,2,1,0:T(8,128)} custom-call(f32[2,64,128,128]{3,2,1,0:T(8,128)} %fusion.3.x_ref, f32[256,256]{1,0:T(8,128)} %constant.124.clone.w_ref.v_ref, f32[256,256]{1,0:T(8,128)} %constant.125.clone.v_ref.w_ref, f32[2,128,128]{2,1,0:T(8,128)} %constant.126.clone.t_ref), custom_call_target="tpu_custom_call" | custom-call | flops 2147483648 | bytes 16777216 | tf_op jit(solution)/shard_map/pallas_call | solution.py:182
  480.5 15.6 %add_multiply_fusion.1 = f32[2,8,8,16384]{3,2,1,0:T(8,128)} fusion(f32[2,8,8,16384]{3,2,1,0:T(8,128)} %constant_dynamic-update-slice_fusion.8, f32[2,8,8,16384]{3,2,1,0:T(8,128)} %reshape.228, f32[2,8,8,16384]{3,2,1,0:T(8,128)} %param.35, f32[2,8,8,16384]{3,2,1,0:T(8,128)} %param.36, f32[8,16384]{1,0:T(8,128)S(1)} %bitcast.272), kind=kLoop, calls=%fused_computation.13 | loop fusion | flops 12582912 | bytes 42467328 | tf_op jit(solution)/shard_map/mul | solution.py:389
  496.1 20.7 %collective-permute-done.3 = f32[2,8,3,128,128]{4,3,2,1,0:T(8,128)} collective-permute-done((f32[2,8,3,128,128]{4,3,2,1,0:T(8,128)}, f32[2,8,3,128,128]{4,3,2,1,0:T(8,128)}, u32[]{:S(2)}, u32[]{:S(2)}) %collective-permute-start.3) | collective-permute-done | bytes 3145760 | tf_op jit(solution)/shard_map/ppermute | solution.py:309
  516.8 68.8 %collective-permute-done.4 = f32[2,8,3,128,128]{4,3,2,1,0:T(8,128)} collective-permute-done((f32[2,8,3,128,128]{4,3,2,1,0:T(8,128)}, f32[2,8,3,128,128]{4,3,2,1,0:T(8,128)}, u32[]{:S(2)}, u32[]{:S(2)}) %collective-permute-start.4) | collective-permute-done | bytes 3145760 | tf_op jit(solution)/shard_map/ppermute | solution.py:310
  585.6 6.3 pad_maximum_fusion.3
  591.9 10.2 %shard_map.337 = f32[2,48,128,128]{3,2,1,0:T(8,128)} custom-call(f32[2,48,128,128]{3,2,1,0:T(8,128)} %bitcast.260, f32[256,256]{1,0:T(8,128)} %constant.124.clone.w_ref.v_ref, f32[256,256]{1,0:T(8,128)} %constant.125.clone.v_ref.w_ref, f32[2,128,128]{2,1,0:T(8,128)} %constant.126.clone.t_ref), custom_call_target="tpu_custom_call" | custom-call | flops 1610612736 | bytes 12582912 | tf_op jit(solution)/shard_map/pallas_call | solution.py:182
  602.1 4.5 fusion.26
  607.1 4.0 subtract_dynamic-update-slice_fusion.4
  616.8 4.2 broadcast_multiply_fusion.y_ref
  621.1 16.3 %shard_map.338 = f32[2,64,128,128]{3,2,1,0:T(8,128)} custom-call(f32[2,64,128,128]{3,2,1,0:T(8,128)} %broadcast_multiply_fusion.y_ref, f32[256,256]{1,0:T(8,128)} %constant.124.clone.w_ref.v_ref, f32[256,256]{1,0:T(8,128)} %constant.125.clone.v_ref.w_ref, f32[2,128,128]{2,1,0:T(8,128)} %constant.127.clone.t_ref), custom_call_target="tpu_custom_call" | custom-call | flops 2147483648 | bytes 16777216 | tf_op jit(solution)/shard_map/pallas_call | solution.py:182
  637.4 12.4 %multiply_reduce_fusion = f32[64,128,128]{2,1,0:T(8,128)} fusion(f32[2,64,128,128]{3,2,1,0:T(8,128)} %bitcast.235, f32[2,64,128,128]{3,2,1,0:T(8,128)} %fusion.3.x_ref, f32[2,64,128,128]{3,2,1,0:T(8,128)} %shard_map.338), kind=kLoop, calls=%fused_computation.8 | loop fusion | flops 7340032 | bytes 29360128 | tf_op jit(solution)/shard_map/reduce_sum | solution.py:382
  649.8 2.5 reduce_sum.47
  652.8 9.4 %reshape.240 = f32[2,8,8,16384]{3,2,1,0:T(8,128)} reshape(f32[2,64,128,128]{3,2,1,0:T(8,128)} %shard_map.338) | data formatting | bytes 16777216 | tf_op jit(solution)/shard_map/reshape | solution.py:381
  662.8 15.6 %add_multiply_fusion = f32[2,8,8,16384]{3,2,1,0:T(8,128)} fusion(f32[2,8,8,16384]{3,2,1,0:T(8,128)} %constant_dynamic-update-slice_fusion.8, f32[2,8,8,16384]{3,2,1,0:T(8,128)} %reshape.240, f32[2,8,8,16384]{3,2,1,0:T(8,128)} %add_multiply_fusion.1, f32[2,8,8,16384]{3,2,1,0:T(8,128)} %param.35, f32[8,16384]{1,0:T(8,128)S(1)} %bitcast.273), kind=kLoop, calls=%fused_computation.9 | loop fusion | flops 12582912 | bytes 42467328 | tf_op jit(solution)/shard_map/mul | solution.py:389
  (93 shorter events, 19.6 us)
Async XLA Ops:
  0.6 30.8 %copy-start = (f32[16,4]{0,1:T(4,128)S(1)}, f32[16,4]{0,1:T(4,128)}, u32[]{:S(2)}) copy-start(f32[16,4]{0,1:T(4,128)} %param.41) | copy-start | bytes 772
  0.6 5.8 copy-start.2
  11.3 11.9 %copy-start.10 = (s32[1024]{0:T(1024)S(1)}, s32[1024]{0:T(1024)}, u32[]{:S(2)}) copy-start(s32[1024]{0:T(1024)} %param.39) | copy-start | bytes 12292
  11.3 11.9 %copy-start.11 = (s32[1024]{0:T(1024)S(1)}, s32[1024]{0:T(1024)}, u32[]{:S(2)}) copy-start(s32[1024]{0:T(1024)} %param.40) | copy-start | bytes 12292
  11.3 20.6 %copy-start.12 = (f32[4]{0:T(128)S(1)}, f32[4]{0:T(128)}, u32[]{:S(2)}) copy-start(f32[4]{0:T(128)} %param.43) | copy-start | bytes 52
  11.3 20.6 %copy-start.13 = (s32[8]{0:T(128)S(1)}, s32[8]{0:T(128)}, u32[]{:S(2)}) copy-start(s32[8]{0:T(128)} %param.42) | copy-start | bytes 100
  11.3 20.7 %copy-start.9 = (f32[8,1024]{1,0:T(8,128)S(1)}, f32[8,1024]{1,0:T(8,128)}, u32[]{:S(2)}) copy-start(f32[8,1024]{1,0:T(8,128)} %param.38) | copy-start | bytes 98308
  17.0 141.8 %collective-permute-start = (f32[2,8,3,128,128]{4,3,2,1,0:T(8,128)}, f32[2,8,3,128,128]{4,3,2,1,0:T(8,128)}, u32[]{:S(2)}, u32[]{:S(2)}) collective-permute-start(f32[2,8,3,128,128]{4,3,2,1,0:T(8,128)} %get-tuple-element.21), channel_id=1, source_target_pairs={{0,2},{2,4},{4,6},{6,8},{8,10},{10,12},{12,14},{14,16},{16,18},{18... | collective-permute-start | bytes 9437192 | tf_op jit(solution)/shard_map/ppermute | solution.py:259
  20.1 138.7 %collective-permute-start.1 = (f32[2,8,3,128,128]{4,3,2,1,0:T(8,128)S(1)}, f32[2,8,3,128,128]{4,3,2,1,0:T(8,128)}, u32[]{:S(2)}, u32[]{:S(2)}) collective-permute-start(f32[2,8,3,128,128]{4,3,2,1,0:T(8,128)S(1)} %get-tuple-element.20), channel_id=1, source_target_pairs={{2,0},{4,2},{6,4},{8,6},{10,8},{12,10},{14,12},{16,14},{18,16},{20... | collective-permute-start | bytes 9437192 | tf_op jit(solution)/shard_map/ppermute | solution.py:260
  23.9 134.9 %all-to-all-start = ((s32[16,2,1024]{2,1,0:T(2,128)}), s32[16,2,1024]{2,1,0:T(2,128)S(1)}, u32[]{:S(2)}, u32[]{:S(2)}) async-start(s32[16,2,1024]{2,1,0:T(2,128)} %broadcast_in_dim.18), calls=%async_computation | async-start | bytes 262144 | tf_op jit(solution)/shard_map/all_to_all | solution.py:264
  169.5 98.1 %all-to-all-start.1 = ((f32[2,4,128,8,128]{4,3,1,0,2:T(8,128)}), f32[2,4,128,8,128]{4,3,1,0,2:T(8,128)}, u32[]{:S(2)}, u32[]{:S(2)}) async-start(f32[2,4,128,8,128]{4,3,1,0,2:T(8,128)} %copy.119), calls=%async_computation.1 | async-start | bytes 8388608 | tf_op jit(solution)/shard_map/all_to_all | solution.py:286
  272.4 98.2 %all-to-all-start.2 = ((f32[2,4,128,8,128]{4,3,1,0,2:T(8,128)}), f32[2,4,128,8,128]{4,3,1,0,2:T(8,128)}, u32[]{:S(2)}, u32[]{:S(2)}) async-start(f32[2,4,128,8,128]{4,3,1,0,2:T(8,128)} %copy.118), calls=%async_computation.2 | async-start | bytes 8388608 | tf_op jit(solution)/shard_map/all_to_all | solution.py:286
  297.4 5.0 copy-start.7
  297.4 9.0 %slice-start = ((s8[8388608]{0:T(1024)(128)(4,1)}), s8[4194304]{0:T(1024)(128)(4,1)S(1)}, s32[]{:S(2)}) async-start(s8[8388608]{0:T(1024)(128)(4,1)} %bitcast.211), calls=%async_computation.3 | async-start | bytes 8388608
  302.4 4.2 slice-start.1
  400.9 12.5 %copy-start.3 = (f32[2,8,8,128,128]{4,3,2,1,0:T(8,128)}, f32[2,8,8,128,128]{4,3,2,1,0:T(8,128)S(1)}, u32[]{:S(2)}) copy-start(f32[2,8,8,128,128]{4,3,2,1,0:T(8,128)S(1)} %pad_maximum_fusion.1) | copy-start | bytes 25165828
  415.9 6.8 %copy-start.8 = (f32[8,128,128]{2,1,0:T(8,128)}, f32[8,128,128]{2,1,0:T(8,128)S(1)}, u32[]{:S(2)}) copy-start(f32[8,128,128]{2,1,0:T(8,128)S(1)} %reduce_sum.44) | copy-start | bytes 1572868
  415.9 8.1 %copy-start.4 = (f32[2,32,128,128]{3,2,1,0:T(8,128)S(1)}, f32[2,32,128,128]{3,2,1,0:T(8,128)}, u32[]{:S(2)}) copy-start(f32[2,32,128,128]{3,2,1,0:T(8,128)} %shard_map.333) | copy-start | bytes 12582916
  415.9 8.1 %copy-start.5 = (f32[2,32,128,128]{3,2,1,0:T(8,128)S(1)}, f32[2,32,128,128]{3,2,1,0:T(8,128)}, u32[]{:S(2)}) copy-start(f32[2,32,128,128]{3,2,1,0:T(8,128)} %shard_map.335) | copy-start | bytes 12582916
  415.9 6.8 collective-permute-start.2
  444.2 72.6 %collective-permute-start.3 = (f32[2,8,3,128,128]{4,3,2,1,0:T(8,128)}, f32[2,8,3,128,128]{4,3,2,1,0:T(8,128)}, u32[]{:S(2)}, u32[]{:S(2)}) collective-permute-start(f32[2,8,3,128,128]{4,3,2,1,0:T(8,128)} %get-tuple-element.25), channel_id=1, source_target_pairs={{0,2},{2,4},{4,6},{6,8},{8,10},{10,12},{12,14},{14,16},{16,18},{18... | collective-permute-start | bytes 9437192 | tf_op jit(solution)/shard_map/ppermute | solution.py:309
  446.1 139.4 %collective-permute-start.4 = (f32[2,8,3,128,128]{4,3,2,1,0:T(8,128)}, f32[2,8,3,128,128]{4,3,2,1,0:T(8,128)}, u32[]{:S(2)}, u32[]{:S(2)}) collective-permute-start(f32[2,8,3,128,128]{4,3,2,1,0:T(8,128)} %get-tuple-element.24), channel_id=1, source_target_pairs={{2,0},{4,2},{6,4},{8,6},{10,8},{12,10},{14,12},{16,14},{18,16},{20... | collective-permute-start | bytes 9437192 | tf_op jit(solution)/shard_map/ppermute | solution.py:310
  602.1 5.0 copy-start.6
  602.1 9.0 %slice-start.2 = ((s8[8388608]{0:T(1024)(128)(4,1)}), s8[4194304]{0:T(1024)(128)(4,1)S(1)}, s32[]{:S(2)}) async-start(s8[8388608]{0:T(1024)(128)(4,1)} %bitcast.221), calls=%async_computation.5 | async-start | bytes 8388608
  607.0 4.2 slice-start.3
  652.3 9.9 %collective-permute-start.5 = (f32[8,128,128]{2,1,0:T(8,128)S(1)}, f32[8,128,128]{2,1,0:T(8,128)S(1)}, u32[]{:S(2)}, u32[]{:S(2)}) collective-permute-start(f32[8,128,128]{2,1,0:T(8,128)S(1)} %reduce_sum.47), channel_id=1, source_target_pairs={{0,1},{1,0},{2,3},{3,2},{4,5},{5,4},{6,7},{7,6},{8,9},{9,8},{10,11... | collective-permute-start | bytes 1572872 | tf_op jit(solution)/shard_map/ppermute | solution.py:384
  662.8 15.6 %copy-start.1 = (f32[16,4]{0,1:T(4,128)S(1)}, f32[16,4]{0,1:T(4,128)}, u32[]{:S(2)}) copy-start(f32[16,4]{0,1:T(4,128)} %param.41) | copy-start | bytes 772

commit v9 on v8

--- a/solution.py
+++ b/solution.py
@@ -169,7 +169,7 @@
 
 
 def block_count(total):
-    for nb in (8, 7, 6, 5, 4, 3, 2, 1):
+    for nb in (16, 8, 7, 6, 5, 4, 3, 2, 1):
         if total % nb == 0:
             return nb
     return 1

time: 687 us -> 682 us (level)
  Pallas kernels: 112 us -> 102 us
  transfers between devices with their start and end apart: 9 -> 9, of which waited for: 5 -> 5; matrix products, arithmetic and copies ran while one was open for 26% -> 26% of each run, Pallas kernels for 10% -> 9%
where the time goes in v9:
time: 682 us; the launch traced here: 675 us
  waiting for transfers between devices  220 us (32%)
  other arithmetic  214 us (31%)
  Pallas kernels  102 us (15%)
  local copies, waits for them, and re-layouts  101 us (15%)
  starting transfers between devices  33.9 us (5%)
    pallas_call x8, Pallas kernels, run_transform(): pl.pallas_call(kernel, out_shape=jax.ShapeDtypeStruct(data.shape, jnp.flo...  91.7 us
    all_to_all x2, waiting for transfers between devices, body(): lax.all_to_all(piece, 'line', split_axis=2, concat_axis=3, tiled=True)  90.9 us
    ppermute x1, waiting for transfers between devices, body(): high = lax.ppermute(blended[:, :, :HALO], 'line', backward_pairs)  68.7 us
    all_to_all x1, waiting for transfers between devices, body(): lax.all_to_all(table, 'line', split_axis=0, concat_axis=2, tiled=True)[0]  38.7 us
    unnamed x50, local copies, waits for them, and re-layouts  31.8 us
    mul x2, other arithmetic, body(): latest = shifted * factor[None, None]  31.2 us
    add x2, other arithmetic, body(): blended = latest + momenta[iteration] * (latest - earlier)  30.4 us
    reduce_sum x4, other arithmetic, body(): squares = jnp.sum(shifted * shifted, axis=(0, 1))  29.8 us
  transfers between devices with their start and end apart: 9, of which 5 were waited for; matrix products, arithmetic and copies ran while one was open for 26% of the time, Pallas kernels for 9%

profile of v9, /device:TPU:21, one launch (start us, length us, event | category | flops | bytes accessed | tf_op | source)
XLA Modules:
  0.0 674.7 jit_solution(9798687958193773230)
XLA Ops:
  0.7 5.0 copy.94
  6.4 4.9 copy.93
  11.3 5.7 fusion.16
  17.0 3.1 collective-permute-start
  20.1 3.1 collective-permute-start.1
  23.9 7.5 %all-to-all-start = ((s32[16,2,1024]{2,1,0:T(2,128)}), s32[16,2,1024]{2,1,0:T(2,128)S(1)}, u32[]{:S(2)}, u32[]{:S(2)}) async-start(s32[16,2,1024]{2,1,0:T(2,128)} %broadcast_in_dim.18), calls=%async_computation | async-start | bytes 262144 | tf_op jit(solution)/shard_map/all_to_all | solution.py:264
  32.0 17.2 %fusion.12 = (f32[1,8,128,1024]{3,2,1,0:T(8,128)S(1)}, f32[1,8,128,1024]{3,2,1,0:T(8,128)S(1)}) fusion(f32[2,8,128,1024]{3,2,1,0:T(8,128)} %param.34, f32[8,1024]{1,0:T(8,128)S(1)} %copy-done.9, f32[128,1024]{1,0:T(8,128)} %param.37, f32[8]{0:T(128)S(1)} %select_reduce_fusion), kind=kLoop, calls=%fused_computation.29 | loop fusion | flops 9437184 | bytes 17334304 | tf_op jit(solution)/shard_map/mul | solution.py:274
  49.2 8.2 %copy.121 = f32[16,8,128,128]{3,2,1,0:T(8,128)} copy(f32[16,8,128,128]{3,1,2,0:T(8,128)} %bitcast.237) | data formatting | bytes 16777216
  57.4 8.1 %copy.120 = f32[16,8,128,128]{3,2,1,0:T(8,128)} copy(f32[16,8,128,128]{3,1,2,0:T(8,128)} %bitcast.230) | data formatting | bytes 16777216
  65.5 4.2 pad_maximum_fusion
  69.8 11.9 %fusion.1.x_ref = f32[2,64,128,128]{3,2,1,0:T(8,128)} fusion(f32[2,64,128,128]{3,2,1,0:T(8,128)} %bitcast.257, f32[2,64,128,128]{3,2,1,0:T(8,128)} %bitcast.239), kind=kLoop, calls=%fused_computation.2 | loop fusion | flops 6291456 | bytes 25165824 | tf_op jit(solution)/shard_map/add | solution.py:266
  81.7 26.6 %add_multiply_fusion.2 = f32[2,8,128,1024]{3,2,1,0:T(8,128)} fusion(f32[2,8,128,1024]{3,2,1,0:T(8,128)} %pad_maximum_fusion, f32[1024]{0:T(1024)S(1)} %get-tuple-element.48, f32[1024]{0:T(1024)S(1)} %get-tuple-element.49, f32[1024]{0:T(1024)S(1)} %get-tuple-element.50, f32[1024]{0:T(1024)S(1)} %get-tuple-element.51, f32[1024]{0:T(1024)S(1)} %get-tuple-element.52, ...), kind=kLoop, calls=%fused_computation.14 | loop fusion | flops 33554432 | bytes 16809984 | tf_op jit(solution)/shard_map/mul | solution.py:277
  108.5 11.5 %shard_map.329 = f32[2,64,128,128]{3,2,1,0:T(8,128)} custom-call(f32[2,64,128,128]{3,2,1,0:T(8,128)} %fusion.1.x_ref, f32[256,256]{1,0:T(8,128)} %constant.124.clone.w_ref.v_ref, f32[256,256]{1,0:T(8,128)} %constant.125.clone.v_ref.w_ref, f32[2,128,128]{2,1,0:T(8,128)} %constant.126.clone.t_ref), custom_call_target="tpu_custom_call" | custom-call | flops 2147483648 | bytes 16777216 | tf_op jit(solution)/shard_map/pallas_call | solution.py:182
  120.0 38.7 %all-to-all-done = s32[16,2,1024]{2,1,0:T(2,128)S(1)} async-done(((s32[16,2,1024]{2,1,0:T(2,128)}), s32[16,2,1024]{2,1,0:T(2,128)S(1)}, u32[]{:S(2)}, u32[]{:S(2)}) %all-to-all-start) | async-done | bytes 131104 | tf_op jit(solution)/shard_map/all_to_all | solution.py:264
  158.8 5.5 copy.122
  164.2 2.7 fusion.64
  166.9 2.6 copy.119
  169.5 5.6 all-to-all-start.1
  176.1 4.8 copy.118
  182.4 85.2 %all-to-all-done.1 = f32[2,4,128,8,128]{4,3,1,0,2:T(8,128)} async-done(((f32[2,4,128,8,128]{4,3,1,0,2:T(8,128)}), f32[2,4,128,8,128]{4,3,1,0,2:T(8,128)}, u32[]{:S(2)}, u32[]{:S(2)}) %all-to-all-start.1) | async-done | bytes 4194336 | tf_op jit(solution)/shard_map/all_to_all | solution.py:286
  267.6 4.8 copy.130
  272.4 6.5 all-to-all-start.2
  280.5 6.4 pad_maximum_fusion.2
  286.9 9.6 %shard_map.330 = f32[2,48,128,128]{3,2,1,0:T(8,128)} custom-call(f32[2,48,128,128]{3,2,1,0:T(8,128)} %bitcast.261, f32[256,256]{1,0:T(8,128)} %constant.124.clone.w_ref.v_ref, f32[256,256]{1,0:T(8,128)} %constant.125.clone.v_ref.w_ref, f32[2,128,128]{2,1,0:T(8,128)} %constant.126.clone.t_ref), custom_call_target="tpu_custom_call" | custom-call | flops 1610612736 | bytes 12582912 | tf_op jit(solution)/shard_map/pallas_call | solution.py:182
  296.5 4.5 fusion.34
  301.5 4.0 subtract_dynamic-update-slice_fusion.9
  305.7 1.0 subtract_dynamic-update-slice_fusion.8
  311.2 4.4 broadcast_multiply_fusion.1.y_ref
  315.7 15.4 %shard_map.331 = f32[2,64,128,128]{3,2,1,0:T(8,128)} custom-call(f32[2,64,128,128]{3,2,1,0:T(8,128)} %broadcast_multiply_fusion.1.y_ref, f32[256,256]{1,0:T(8,128)} %constant.124.clone.w_ref.v_ref, f32[256,256]{1,0:T(8,128)} %constant.125.clone.v_ref.w_ref, f32[2,128,128]{2,1,0:T(8,128)} %constant.127.clone.t_ref), custom_call_target="tpu_custom_call" | custom-call | flops 2147483648 | bytes 16777216 | tf_op jit(solution)/shard_map/pallas_call | solution.py:182
  331.1 9.4 %reshape.228 = f32[2,8,8,16384]{3,2,1,0:T(8,128)} reshape(f32[2,64,128,128]{3,2,1,0:T(8,128)} %shard_map.331) | data formatting | bytes 16777216 | tf_op jit(solution)/shard_map/reshape | solution.py:381
  340.5 5.4 shard_map.332
  345.8 9.2 %shard_map.333 = f32[2,32,128,128]{3,2,1,0:T(8,128)} custom-call(f32[2,32,128,128]{3,2,1,0:T(8,128)} %bitcast.265, f32[256,256]{1,0:T(8,128)} %constant.124.clone.w_ref.v_ref, f32[256,256]{1,0:T(8,128)} %constant.125.clone.v_ref.w_ref, f32[2,128,128]{2,1,0:T(8,128)} %constant.127.clone.t_ref), custom_call_target="tpu_custom_call" | custom-call | flops 1073741824 | bytes 8388608 | tf_op jit(solution)/shard_map/pallas_call | solution.py:182
  355.0 4.9 concatenate.21
  360.0 4.5 constant_dynamic-update-slice_fusion.9
  364.5 5.7 all-to-all-done.2
  370.2 4.8 copy.111
  374.9 5.2 shard_map.334
  380.1 9.3 %shard_map.335 = f32[2,32,128,128]{3,2,1,0:T(8,128)} custom-call(f32[2,32,128,128]{3,2,1,0:T(8,128)} %bitcast.267, f32[256,256]{1,0:T(8,128)} %constant.124.clone.w_ref.v_ref, f32[256,256]{1,0:T(8,128)} %constant.125.clone.v_ref.w_ref, f32[2,128,128]{2,1,0:T(8,128)} %constant.127.clone.t_ref), custom_call_target="tpu_custom_call" | custom-call | flops 1073741824 | bytes 8388608 | tf_op jit(solution)/shard_map/pallas_call | solution.py:182
  389.4 4.9 concatenate.22
  394.4 4.0 pad_maximum_fusion.1
  398.5 12.5 %multiply_reduce_fusion.1 = f32[64,128,128]{2,1,0:T(8,128)} fusion(f32[2,64,128,128]{3,2,1,0:T(8,128)S(1)} %bitcast.233, f32[2,64,128,128]{3,2,1,0:T(8,128)} %fusion.1.x_ref, f32[2,64,128,128]{3,2,1,0:T(8,128)} %shard_map.331), kind=kLoop, calls=%fused_computation.11 | loop fusion | flops 7340032 | bytes 29360128 | tf_op jit(solution)/shard_map/reduce_sum | solution.py:382
  411.0 2.5 reduce_sum.44
  413.5 1.5 collective-permute-start.2
  415.0 5.3 constant_dynamic-update-slice_fusion.8
  420.3 1.3 maximum_divide_fusion
  421.6 13.8 %multiply_add_fusion = f32[2,8,8,128,128]{4,3,2,1,0:T(8,128)} fusion(f32[2,8,8,128,128]{4,3,2,1,0:T(8,128)} %bitcast.229, f32[8,128,128]{2,1,0:T(8,128)S(1)} %maximum_divide_fusion, f32[2,8,8,128,128]{4,2,3,1,0:T(8,128)} %bitcast.238, f32[2,8,8,128,128]{4,2,3,1,0:T(8,128)} %bitcast.231, f32[2,4,8,128,128]{4,3,2,1,0:T(8,128)S(1)} %bitcast.244, ...), kind=kLoop, calls=%fused_computation.10 | loop fusion | flops 20971520 | bytes 42467328 | tf_op jit(solution)/shard_map/add | solution.py:308
  435.4 6.3 fusion.63
  441.8 1.9 collective-permute-start.3
  443.7 4.3 collective-permute-start.4
  448.8 16.5 %fusion.3.x_ref = f32[2,64,128,128]{3,2,1,0:T(8,128)} fusion(f32[64,128,128]{2,1,0:T(8,128)S(1)} %bitcast.268, f32[2,64,128,128]{3,2,1,0:T(8,128)} %bitcast.234, f32[2,64,128,128]{3,2,1,0:T(8,128)} %fusion.1.x_ref, f32[2,64,128,128]{3,2,1,0:T(8,128)} %shard_map.331, f32[2,64,128,128]{3,2,1,0:T(8,128)} %bitcast.240), kind=kLoop, calls=%fused_computation.5 | loop fusion | flops 12582912 | bytes 46137344 | tf_op jit(solution)/shard_map/add | solution.py:308
  465.3 11.4 %shard_map.336 = f32[2,64,128,128]{3,2,1,0:T(8,128)} custom-call(f32[2,64,128,128]{3,2,1,0:T(8,128)} %fusion.3.x_ref, f32[256,256]{1,0:T(8,128)} %constant.124.clone.w_ref.v_ref, f32[256,256]{1,0:T(8,128)} %constant.125.clone.v_ref.w_ref, f32[2,128,128]{2,1,0:T(8,128)} %constant.126.clone.t_ref), custom_call_target="tpu_custom_call" | custom-call | flops 2147483648 | bytes 16777216 | tf_op jit(solution)/shard_map/pallas_call | solution.py:182
  476.7 15.6 %add_multiply_fusion.1 = f32[2,8,8,16384]{3,2,1,0:T(8,128)} fusion(f32[2,8,8,16384]{3,2,1,0:T(8,128)} %constant_dynamic-update-slice_fusion.8, f32[2,8,8,16384]{3,2,1,0:T(8,128)} %reshape.228, f32[2,8,8,16384]{3,2,1,0:T(8,128)} %param.35, f32[2,8,8,16384]{3,2,1,0:T(8,128)} %param.36, f32[8,16384]{1,0:T(8,128)S(1)} %bitcast.272), kind=kLoop, calls=%fused_computation.13 | loop fusion | flops 12582912 | bytes 42467328 | tf_op jit(solution)/shard_map/mul | solution.py:389
  492.3 22.1 %collective-permute-done.3 = f32[2,8,3,128,128]{4,3,2,1,0:T(8,128)} collective-permute-done((f32[2,8,3,128,128]{4,3,2,1,0:T(8,128)}, f32[2,8,3,128,128]{4,3,2,1,0:T(8,128)}, u32[]{:S(2)}, u32[]{:S(2)}) %collective-permute-start.3) | collective-permute-done | bytes 3145760 | tf_op jit(solution)/shard_map/ppermute | solution.py:309
  514.4 68.7 %collective-permute-done.4 = f32[2,8,3,128,128]{4,3,2,1,0:T(8,128)} collective-permute-done((f32[2,8,3,128,128]{4,3,2,1,0:T(8,128)}, f32[2,8,3,128,128]{4,3,2,1,0:T(8,128)}, u32[]{:S(2)}, u32[]{:S(2)}) %collective-permute-start.4) | collective-permute-done | bytes 3145760 | tf_op jit(solution)/shard_map/ppermute | solution.py:310
  583.1 6.3 pad_maximum_fusion.3
  589.4 9.7 %shard_map.337 = f32[2,48,128,128]{3,2,1,0:T(8,128)} custom-call(f32[2,48,128,128]{3,2,1,0:T(8,128)} %bitcast.260, f32[256,256]{1,0:T(8,128)} %constant.124.clone.w_ref.v_ref, f32[256,256]{1,0:T(8,128)} %constant.125.clone.v_ref.w_ref, f32[2,128,128]{2,1,0:T(8,128)} %constant.126.clone.t_ref), custom_call_target="tpu_custom_call" | custom-call | flops 1610612736 | bytes 12582912 | tf_op jit(solution)/shard_map/pallas_call | solution.py:182
  599.1 4.5 fusion.26
  604.1 4.0 subtract_dynamic-update-slice_fusion.4
  613.8 4.2 broadcast_multiply_fusion.y_ref
  618.1 15.5 %shard_map.338 = f32[2,64,128,128]{3,2,1,0:T(8,128)} custom-call(f32[2,64,128,128]{3,2,1,0:T(8,128)} %broadcast_multiply_fusion.y_ref, f32[256,256]{1,0:T(8,128)} %constant.124.clone.w_ref.v_ref, f32[256,256]{1,0:T(8,128)} %constant.125.clone.v_ref.w_ref, f32[2,128,128]{2,1,0:T(8,128)} %constant.127.clone.t_ref), custom_call_target="tpu_custom_call" | custom-call | flops 2147483648 | bytes 16777216 | tf_op jit(solution)/shard_map/pallas_call | solution.py:182
  633.6 12.3 %multiply_reduce_fusion = f32[64,128,128]{2,1,0:T(8,128)} fusion(f32[2,64,128,128]{3,2,1,0:T(8,128)} %bitcast.235, f32[2,64,128,128]{3,2,1,0:T(8,128)} %fusion.3.x_ref, f32[2,64,128,128]{3,2,1,0:T(8,128)} %shard_map.338), kind=kLoop, calls=%fused_computation.8 | loop fusion | flops 7340032 | bytes 29360128 | tf_op jit(solution)/shard_map/reduce_sum | solution.py:382
  645.9 2.5 reduce_sum.47
  648.9 9.4 %reshape.240 = f32[2,8,8,16384]{3,2,1,0:T(8,128)} reshape(f32[2,64,128,128]{3,2,1,0:T(8,128)} %shard_map.338) | data formatting | bytes 16777216 | tf_op jit(solution)/shard_map/reshape | solution.py:381
  658.9 15.6 %add_multiply_fusion = f32[2,8,8,16384]{3,2,1,0:T(8,128)} fusion(f32[2,8,8,16384]{3,2,1,0:T(8,128)} %constant_dynamic-update-slice_fusion.8, f32[2,8,8,16384]{3,2,1,0:T(8,128)} %reshape.240, f32[2,8,8,16384]{3,2,1,0:T(8,128)} %add_multiply_fusion.1, f32[2,8,8,16384]{3,2,1,0:T(8,128)} %param.35, f32[8,16384]{1,0:T(8,128)S(1)} %bitcast.273), kind=kLoop, calls=%fused_computation.9 | loop fusion | flops 12582912 | bytes 42467328 | tf_op jit(solution)/shard_map/mul | solution.py:389
  (93 shorter events, 19.6 us)
Async XLA Ops:
  0.6 30.7 %copy-start = (f32[16,4]{0,1:T(4,128)S(1)}, f32[16,4]{0,1:T(4,128)}, u32[]{:S(2)}) copy-start(f32[16,4]{0,1:T(4,128)} %param.41) | copy-start | bytes 772
  0.6 5.8 copy-start.2
  11.3 11.9 %copy-start.10 = (s32[1024]{0:T(1024)S(1)}, s32[1024]{0:T(1024)}, u32[]{:S(2)}) copy-start(s32[1024]{0:T(1024)} %param.39) | copy-start | bytes 12292
  11.3 11.9 %copy-start.11 = (s32[1024]{0:T(1024)S(1)}, s32[1024]{0:T(1024)}, u32[]{:S(2)}) copy-start(s32[1024]{0:T(1024)} %param.40) | copy-start | bytes 12292
  11.3 20.6 %copy-start.12 = (f32[4]{0:T(128)S(1)}, f32[4]{0:T(128)}, u32[]{:S(2)}) copy-start(f32[4]{0:T(128)} %param.43) | copy-start | bytes 52
  11.3 20.6 %copy-start.13 = (s32[8]{0:T(128)S(1)}, s32[8]{0:T(128)}, u32[]{:S(2)}) copy-start(s32[8]{0:T(128)} %param.42) | copy-start | bytes 100
  11.3 20.7 %copy-start.9 = (f32[8,1024]{1,0:T(8,128)S(1)}, f32[8,1024]{1,0:T(8,128)}, u32[]{:S(2)}) copy-start(f32[8,1024]{1,0:T(8,128)} %param.38) | copy-start | bytes 98308
  17.0 141.8 %collective-permute-start = (f32[2,8,3,128,128]{4,3,2,1,0:T(8,128)}, f32[2,8,3,128,128]{4,3,2,1,0:T(8,128)}, u32[]{:S(2)}, u32[]{:S(2)}) collective-permute-start(f32[2,8,3,128,128]{4,3,2,1,0:T(8,128)} %get-tuple-element.21), channel_id=1, source_target_pairs={{0,2},{2,4},{4,6},{6,8},{8,10},{10,12},{12,14},{14,16},{16,18},{18... | collective-permute-start | bytes 9437192 | tf_op jit(solution)/shard_map/ppermute | solution.py:259
  20.1 138.7 %collective-permute-start.1 = (f32[2,8,3,128,128]{4,3,2,1,0:T(8,128)S(1)}, f32[2,8,3,128,128]{4,3,2,1,0:T(8,128)}, u32[]{:S(2)}, u32[]{:S(2)}) collective-permute-start(f32[2,8,3,128,128]{4,3,2,1,0:T(8,128)S(1)} %get-tuple-element.20), channel_id=1, source_target_pairs={{2,0},{4,2},{6,4},{8,6},{10,8},{12,10},{14,12},{16,14},{18,16},{20... | collective-permute-start | bytes 9437192 | tf_op jit(solution)/shard_map/ppermute | solution.py:260
  23.9 134.9 %all-to-all-start = ((s32[16,2,1024]{2,1,0:T(2,128)}), s32[16,2,1024]{2,1,0:T(2,128)S(1)}, u32[]{:S(2)}, u32[]{:S(2)}) async-start(s32[16,2,1024]{2,1,0:T(2,128)} %broadcast_in_dim.18), calls=%async_computation | async-start | bytes 262144 | tf_op jit(solution)/shard_map/all_to_all | solution.py:264
  169.5 98.1 %all-to-all-start.1 = ((f32[2,4,128,8,128]{4,3,1,0,2:T(8,128)}), f32[2,4,128,8,128]{4,3,1,0,2:T(8,128)}, u32[]{:S(2)}, u32[]{:S(2)}) async-start(f32[2,4,128,8,128]{4,3,1,0,2:T(8,128)} %copy.119), calls=%async_computation.1 | async-start | bytes 8388608 | tf_op jit(solution)/shard_map/all_to_all | solution.py:286
  272.4 97.8 %all-to-all-start.2 = ((f32[2,4,128,8,128]{4,3,1,0,2:T(8,128)}), f32[2,4,128,8,128]{4,3,1,0,2:T(8,128)}, u32[]{:S(2)}, u32[]{:S(2)}) async-start(f32[2,4,128,8,128]{4,3,1,0,2:T(8,128)} %copy.118), calls=%async_computation.2 | async-start | bytes 8388608 | tf_op jit(solution)/shard_map/all_to_all | solution.py:286
  296.5 5.0 copy-start.7
  296.5 9.0 %slice-start = ((s8[8388608]{0:T(1024)(128)(4,1)}), s8[4194304]{0:T(1024)(128)(4,1)S(1)}, s32[]{:S(2)}) async-start(s8[8388608]{0:T(1024)(128)(4,1)} %bitcast.211), calls=%async_computation.3 | async-start | bytes 8388608
  301.5 4.2 slice-start.1
  398.4 12.5 %copy-start.3 = (f32[2,8,8,128,128]{4,3,2,1,0:T(8,128)}, f32[2,8,8,128,128]{4,3,2,1,0:T(8,128)S(1)}, u32[]{:S(2)}) copy-start(f32[2,8,8,128,128]{4,3,2,1,0:T(8,128)S(1)} %pad_maximum_fusion.1) | copy-start | bytes 25165828
  413.4 6.8 %copy-start.8 = (f32[8,128,128]{2,1,0:T(8,128)}, f32[8,128,128]{2,1,0:T(8,128)S(1)}, u32[]{:S(2)}) copy-start(f32[8,128,128]{2,1,0:T(8,128)S(1)} %reduce_sum.44) | copy-start | bytes 1572868
  413.5 8.1 %copy-start.4 = (f32[2,32,128,128]{3,2,1,0:T(8,128)S(1)}, f32[2,32,128,128]{3,2,1,0:T(8,128)}, u32[]{:S(2)}) copy-start(f32[2,32,128,128]{3,2,1,0:T(8,128)} %shard_map.333) | copy-start | bytes 12582916
  413.5 8.1 %copy-start.5 = (f32[2,32,128,128]{3,2,1,0:T(8,128)S(1)}, f32[2,32,128,128]{3,2,1,0:T(8,128)}, u32[]{:S(2)}) copy-start(f32[2,32,128,128]{3,2,1,0:T(8,128)} %shard_map.335) | copy-start | bytes 12582916
  413.5 6.8 %collective-permute-start.2 = (f32[8,128,128]{2,1,0:T(8,128)S(1)}, f32[8,128,128]{2,1,0:T(8,128)S(1)}, u32[]{:S(2)}, u32[]{:S(2)}) collective-permute-start(f32[8,128,128]{2,1,0:T(8,128)S(1)} %reduce_sum.44), channel_id=1, source_target_pairs={{0,1},{1,0},{2,3},{3,2},{4,5},{5,4},{6,7},{7,6},{8,9},{9,8},{10,11... | collective-permute-start | bytes 1572872 | tf_op jit(solution)/shard_map/ppermute | solution.py:384
  441.8 72.6 %collective-permute-start.3 = (f32[2,8,3,128,128]{4,3,2,1,0:T(8,128)}, f32[2,8,3,128,128]{4,3,2,1,0:T(8,128)}, u32[]{:S(2)}, u32[]{:S(2)}) collective-permute-start(f32[2,8,3,128,128]{4,3,2,1,0:T(8,128)} %get-tuple-element.25), channel_id=1, source_target_pairs={{0,2},{2,4},{4,6},{6,8},{8,10},{10,12},{12,14},{14,16},{16,18},{18... | collective-permute-start | bytes 9437192 | tf_op jit(solution)/shard_map/ppermute | solution.py:309
  443.7 139.4 %collective-permute-start.4 = (f32[2,8,3,128,128]{4,3,2,1,0:T(8,128)}, f32[2,8,3,128,128]{4,3,2,1,0:T(8,128)}, u32[]{:S(2)}, u32[]{:S(2)}) collective-permute-start(f32[2,8,3,128,128]{4,3,2,1,0:T(8,128)} %get-tuple-element.24), channel_id=1, source_target_pairs={{2,0},{4,2},{6,4},{8,6},{10,8},{12,10},{14,12},{16,14},{18,16},{20... | collective-permute-start | bytes 9437192 | tf_op jit(solution)/shard_map/ppermute | solution.py:310
  599.1 5.0 copy-start.6
  599.1 9.0 %slice-start.2 = ((s8[8388608]{0:T(1024)(128)(4,1)}), s8[4194304]{0:T(1024)(128)(4,1)S(1)}, s32[]{:S(2)}) async-start(s8[8388608]{0:T(1024)(128)(4,1)} %bitcast.221), calls=%async_computation.5 | async-start | bytes 8388608
  604.1 4.2 slice-start.3
  648.4 9.9 %collective-permute-start.5 = (f32[8,128,128]{2,1,0:T(8,128)S(1)}, f32[8,128,128]{2,1,0:T(8,128)S(1)}, u32[]{:S(2)}, u32[]{:S(2)}) collective-permute-start(f32[8,128,128]{2,1,0:T(8,128)S(1)} %reduce_sum.47), channel_id=1, source_target_pairs={{0,1},{1,0},{2,3},{3,2},{4,5},{5,4},{6,7},{7,6},{8,9},{9,8},{10,11... | collective-permute-start | bytes 1572872 | tf_op jit(solution)/shard_map/ppermute | solution.py:384
  658.9 15.6 %copy-start.1 = (f32[16,4]{0,1:T(4,128)S(1)}, f32[16,4]{0,1:T(4,128)}, u32[]{:S(2)}) copy-start(f32[16,4]{0,1:T(4,128)} %param.41) | copy-start | bytes 772

commit v10 on v9

--- a/solution.py
+++ b/solution.py
@@ -169,7 +169,7 @@
 
 
 def block_count(total):
-    for nb in (16, 8, 7, 6, 5, 4, 3, 2, 1):
+    for nb in (32, 16, 8, 7, 6, 5, 4, 3, 2, 1):
         if total % nb == 0:
             return nb
     return 1

time: 682 us -> 681 us (level)
  no operation moved by 1% of the time
where the time goes in v10:
time: 681 us; the launch traced here: 675 us
  waiting for transfers between devices  218 us (32%)
  other arithmetic  214 us (31%)
  Pallas kernels  104 us (15%)
  local copies, waits for them, and re-layouts  101 us (15%)
  starting transfers between devices  34.4 us (5%)
    pallas_call x8, Pallas kernels, run_transform(): pl.pallas_call(kernel, out_shape=jax.ShapeDtypeStruct(data.shape, jnp.flo...  95.7 us
    all_to_all x2, waiting for transfers between devices, body(): lax.all_to_all(piece, 'line', split_axis=2, concat_axis=3, tiled=True)  90.3 us
    ppermute x1, waiting for transfers between devices, body(): high = lax.ppermute(blended[:, :, :HALO], 'line', backward_pairs)  68.7 us
    all_to_all x1, waiting for transfers between devices, body(): lax.all_to_all(table, 'line', split_axis=0, concat_axis=2, tiled=True)[0]  37.8 us
    unnamed x50, local copies, waits for them, and re-layouts  31.8 us
    mul x2, other arithmetic, body(): latest = shifted * factor[None, None]  31.2 us
    add x2, other arithmetic, body(): blended = latest + momenta[iteration] * (latest - earlier)  30.4 us
    reduce_sum x4, other arithmetic, body(): squares = jnp.sum(shifted * shifted, axis=(0, 1))  29.6 us
  transfers between devices with their start and end apart: 9, of which 5 were waited for; matrix products, arithmetic and copies ran while one was open for 26% of the time, Pallas kernels for 9%

profile of v10, /device:TPU:21, one launch (start us, length us, event | category | flops | bytes accessed | tf_op | source)
XLA Modules:
  0.0 674.9 jit_solution(8452366508370029727)
XLA Ops:
  0.7 5.0 copy.94
  6.4 4.9 copy.93
  11.3 5.7 fusion.16
  17.0 3.1 collective-permute-start
  20.1 3.1 collective-permute-start.1
  23.9 7.6 %all-to-all-start = ((s32[16,2,1024]{2,1,0:T(2,128)}), s32[16,2,1024]{2,1,0:T(2,128)S(1)}, u32[]{:S(2)}, u32[]{:S(2)}) async-start(s32[16,2,1024]{2,1,0:T(2,128)} %broadcast_in_dim.18), calls=%async_computation | async-start | bytes 262144 | tf_op jit(solution)/shard_map/all_to_all | solution.py:264
  32.1 17.2 %fusion.12 = (f32[1,8,128,1024]{3,2,1,0:T(8,128)S(1)}, f32[1,8,128,1024]{3,2,1,0:T(8,128)S(1)}) fusion(f32[2,8,128,1024]{3,2,1,0:T(8,128)} %param.34, f32[8,1024]{1,0:T(8,128)S(1)} %copy-done.9, f32[128,1024]{1,0:T(8,128)} %param.37, f32[8]{0:T(128)S(1)} %select_reduce_fusion), kind=kLoop, calls=%fused_computation.29 | loop fusion | flops 9437184 | bytes 17334304 | tf_op jit(solution)/shard_map/mul | solution.py:274
  49.3 8.2 %copy.121 = f32[16,8,128,128]{3,2,1,0:T(8,128)} copy(f32[16,8,128,128]{3,1,2,0:T(8,128)} %bitcast.237) | data formatting | bytes 16777216
  57.5 8.1 %copy.120 = f32[16,8,128,128]{3,2,1,0:T(8,128)} copy(f32[16,8,128,128]{3,1,2,0:T(8,128)} %bitcast.230) | data formatting | bytes 16777216
  65.7 4.2 pad_maximum_fusion
  69.9 11.9 %fusion.1.x_ref = f32[2,64,128,128]{3,2,1,0:T(8,128)} fusion(f32[2,64,128,128]{3,2,1,0:T(8,128)} %bitcast.257, f32[2,64,128,128]{3,2,1,0:T(8,128)} %bitcast.239), kind=kLoop, calls=%fused_computation.2 | loop fusion | flops 6291456 | bytes 25165824 | tf_op jit(solution)/shard_map/add | solution.py:266
  81.8 26.6 %add_multiply_fusion.2 = f32[2,8,128,1024]{3,2,1,0:T(8,128)} fusion(f32[2,8,128,1024]{3,2,1,0:T(8,128)} %pad_maximum_fusion, f32[1024]{0:T(1024)S(1)} %get-tuple-element.48, f32[1024]{0:T(1024)S(1)} %get-tuple-element.49, f32[1024]{0:T(1024)S(1)} %get-tuple-element.50, f32[1024]{0:T(1024)S(1)} %get-tuple-element.51, f32[1024]{0:T(1024)S(1)} %get-tuple-element.52, ...), kind=kLoop, calls=%fused_computation.14 | loop fusion | flops 33554432 | bytes 16809984 | tf_op jit(solution)/shard_map/mul | solution.py:277
  108.6 12.3 %shard_map.329 = f32[2,64,128,128]{3,2,1,0:T(8,128)} custom-call(f32[2,64,128,128]{3,2,1,0:T(8,128)} %fusion.1.x_ref, f32[256,256]{1,0:T(8,128)} %constant.124.clone.w_ref.v_ref, f32[256,256]{1,0:T(8,128)} %constant.125.clone.v_ref.w_ref, f32[2,128,128]{2,1,0:T(8,128)} %constant.126.clone.t_ref), custom_call_target="tpu_custom_call" | custom-call | flops 2147483648 | bytes 16777216 | tf_op jit(solution)/shard_map/pallas_call | solution.py:182
  120.9 37.8 %all-to-all-done = s32[16,2,1024]{2,1,0:T(2,128)S(1)} async-done(((s32[16,2,1024]{2,1,0:T(2,128)}), s32[16,2,1024]{2,1,0:T(2,128)S(1)}, u32[]{:S(2)}, u32[]{:S(2)}) %all-to-all-start) | async-done | bytes 131104 | tf_op jit(solution)/shard_map/all_to_all | solution.py:264
  158.8 5.5 copy.122
  164.2 2.7 fusion.64
  166.9 2.6 copy.119
  169.5 5.6 all-to-all-start.1
  176.1 4.8 copy.118
  182.4 85.2 %all-to-all-done.1 = f32[2,4,128,8,128]{4,3,1,0,2:T(8,128)} async-done(((f32[2,4,128,8,128]{4,3,1,0,2:T(8,128)}), f32[2,4,128,8,128]{4,3,1,0,2:T(8,128)}, u32[]{:S(2)}, u32[]{:S(2)}) %all-to-all-start.1) | async-done | bytes 4194336 | tf_op jit(solution)/shard_map/all_to_all | solution.py:286
  267.6 4.8 copy.130
  272.4 6.8 %all-to-all-start.2 = ((f32[2,4,128,8,128]{4,3,1,0,2:T(8,128)}), f32[2,4,128,8,128]{4,3,1,0,2:T(8,128)}, u32[]{:S(2)}, u32[]{:S(2)}) async-start(f32[2,4,128,8,128]{4,3,1,0,2:T(8,128)} %copy.118), calls=%async_computation.2 | async-start | bytes 8388608 | tf_op jit(solution)/shard_map/all_to_all | solution.py:286
  280.8 6.4 pad_maximum_fusion.2
  287.2 9.3 %shard_map.330 = f32[2,48,128,128]{3,2,1,0:T(8,128)} custom-call(f32[2,48,128,128]{3,2,1,0:T(8,128)} %bitcast.261, f32[256,256]{1,0:T(8,128)} %constant.124.clone.w_ref.v_ref, f32[256,256]{1,0:T(8,128)} %constant.125.clone.v_ref.w_ref, f32[2,128,128]{2,1,0:T(8,128)} %constant.126.clone.t_ref), custom_call_target="tpu_custom_call" | custom-call | flops 1610612736 | bytes 12582912 | tf_op jit(solution)/shard_map/pallas_call | solution.py:182
  296.5 4.4 fusion.34
  301.4 4.0 subtract_dynamic-update-slice_fusion.9
  305.6 1.0 subtract_dynamic-update-slice_fusion.8
  311.2 4.4 broadcast_multiply_fusion.1.y_ref
  315.6 16.4 %shard_map.331 = f32[2,64,128,128]{3,2,1,0:T(8,128)} custom-call(f32[2,64,128,128]{3,2,1,0:T(8,128)} %broadcast_multiply_fusion.1.y_ref, f32[256,256]{1,0:T(8,128)} %constant.124.clone.w_ref.v_ref, f32[256,256]{1,0:T(8,128)} %constant.125.clone.v_ref.w_ref, f32[2,128,128]{2,1,0:T(8,128)} %constant.127.clone.t_ref), custom_call_target="tpu_custom_call" | custom-call | flops 2147483648 | bytes 16777216 | tf_op jit(solution)/shard_map/pallas_call | solution.py:182
  332.0 9.4 %reshape.228 = f32[2,8,8,16384]{3,2,1,0:T(8,128)} reshape(f32[2,64,128,128]{3,2,1,0:T(8,128)} %shard_map.331) | data formatting | bytes 16777216 | tf_op jit(solution)/shard_map/reshape | solution.py:381
  341.3 4.2 shard_map.332
  345.6 10.2 %shard_map.333 = f32[2,32,128,128]{3,2,1,0:T(8,128)} custom-call(f32[2,32,128,128]{3,2,1,0:T(8,128)} %bitcast.265, f32[256,256]{1,0:T(8,128)} %constant.124.clone.w_ref.v_ref, f32[256,256]{1,0:T(8,128)} %constant.125.clone.v_ref.w_ref, f32[2,128,128]{2,1,0:T(8,128)} %constant.127.clone.t_ref), custom_call_target="tpu_custom_call" | custom-call | flops 1073741824 | bytes 8388608 | tf_op jit(solution)/shard_map/pallas_call | solution.py:182
  355.7 4.9 concatenate.21
  360.6 4.5 constant_dynamic-update-slice_fusion.9
  365.2 5.1 all-to-all-done.2
  370.3 4.8 copy.111
  375.0 4.3 shard_map.334
  379.3 10.1 %shard_map.335 = f32[2,32,128,128]{3,2,1,0:T(8,128)} custom-call(f32[2,32,128,128]{3,2,1,0:T(8,128)} %bitcast.267, f32[256,256]{1,0:T(8,128)} %constant.124.clone.w_ref.v_ref, f32[256,256]{1,0:T(8,128)} %constant.125.clone.v_ref.w_ref, f32[2,128,128]{2,1,0:T(8,128)} %constant.127.clone.t_ref), custom_call_target="tpu_custom_call" | custom-call | flops 1073741824 | bytes 8388608 | tf_op jit(solution)/shard_map/pallas_call | solution.py:182
  389.5 4.9 concatenate.22
  394.4 4.0 pad_maximum_fusion.1
  398.5 12.5 %multiply_reduce_fusion.1 = f32[64,128,128]{2,1,0:T(8,128)} fusion(f32[2,64,128,128]{3,2,1,0:T(8,128)S(1)} %bitcast.233, f32[2,64,128,128]{3,2,1,0:T(8,128)} %fusion.1.x_ref, f32[2,64,128,128]{3,2,1,0:T(8,128)} %shard_map.331), kind=kLoop, calls=%fused_computation.11 | loop fusion | flops 7340032 | bytes 29360128 | tf_op jit(solution)/shard_map/reduce_sum | solution.py:382
  411.0 2.5 reduce_sum.44
  413.5 1.5 collective-permute-start.2
  415.0 5.2 constant_dynamic-update-slice_fusion.8
  420.3 1.3 maximum_divide_fusion
  421.6 13.6 %multiply_add_fusion = f32[2,8,8,128,128]{4,3,2,1,0:T(8,128)} fusion(f32[2,8,8,128,128]{4,3,2,1,0:T(8,128)} %bitcast.229, f32[8,128,128]{2,1,0:T(8,128)S(1)} %maximum_divide_fusion, f32[2,8,8,128,128]{4,2,3,1,0:T(8,128)} %bitcast.238, f32[2,8,8,128,128]{4,2,3,1,0:T(8,128)} %bitcast.231, f32[2,4,8,128,128]{4,3,2,1,0:T(8,128)S(1)} %bitcast.244, ...), kind=kLoop, calls=%fused_computation.10 | loop fusion | flops 20971520 | bytes 42467328 | tf_op jit(solution)/shard_map/add | solution.py:308
  435.2 6.3 fusion.63
  441.6 1.9 collective-permute-start.3
  443.5 4.3 collective-permute-start.4
  448.6 16.7 %fusion.3.x_ref = f32[2,64,128,128]{3,2,1,0:T(8,128)} fusion(f32[64,128,128]{2,1,0:T(8,128)S(1)} %bitcast.268, f32[2,64,128,128]{3,2,1,0:T(8,128)} %bitcast.234, f32[2,64,128,128]{3,2,1,0:T(8,128)} %fusion.1.x_ref, f32[2,64,128,128]{3,2,1,0:T(8,128)} %shard_map.331, f32[2,64,128,128]{3,2,1,0:T(8,128)} %bitcast.240), kind=kLoop, calls=%fused_computation.5 | loop fusion | flops 12582912 | bytes 46137344 | tf_op jit(solution)/shard_map/add | solution.py:308
  465.3 11.7 %shard_map.336 = f32[2,64,128,128]{3,2,1,0:T(8,128)} custom-call(f32[2,64,128,128]{3,2,1,0:T(8,128)} %fusion.3.x_ref, f32[256,256]{1,0:T(8,128)} %constant.124.clone.w_ref.v_ref, f32[256,256]{1,0:T(8,128)} %constant.125.clone.v_ref.w_ref, f32[2,128,128]{2,1,0:T(8,128)} %constant.126.clone.t_ref), custom_call_target="tpu_custom_call" | custom-call | flops 2147483648 | bytes 16777216 | tf_op jit(solution)/shard_map/pallas_call | solution.py:182
  477.1 15.6 %add_multiply_fusion.1 = f32[2,8,8,16384]{3,2,1,0:T(8,128)} fusion(f32[2,8,8,16384]{3,2,1,0:T(8,128)} %constant_dynamic-update-slice_fusion.8, f32[2,8,8,16384]{3,2,1,0:T(8,128)} %reshape.228, f32[2,8,8,16384]{3,2,1,0:T(8,128)} %param.35, f32[2,8,8,16384]{3,2,1,0:T(8,128)} %param.36, f32[8,16384]{1,0:T(8,128)S(1)} %bitcast.272), kind=kLoop, calls=%fused_computation.13 | loop fusion | flops 12582912 | bytes 42467328 | tf_op jit(solution)/shard_map/mul | solution.py:389
  492.7 21.5 %collective-permute-done.3 = f32[2,8,3,128,128]{4,3,2,1,0:T(8,128)} collective-permute-done((f32[2,8,3,128,128]{4,3,2,1,0:T(8,128)}, f32[2,8,3,128,128]{4,3,2,1,0:T(8,128)}, u32[]{:S(2)}, u32[]{:S(2)}) %collective-permute-start.3) | collective-permute-done | bytes 3145760 | tf_op jit(solution)/shard_map/ppermute | solution.py:309
  514.2 68.7 %collective-permute-done.4 = f32[2,8,3,128,128]{4,3,2,1,0:T(8,128)} collective-permute-done((f32[2,8,3,128,128]{4,3,2,1,0:T(8,128)}, f32[2,8,3,128,128]{4,3,2,1,0:T(8,128)}, u32[]{:S(2)}, u32[]{:S(2)}) %collective-permute-start.4) | collective-permute-done | bytes 3145760 | tf_op jit(solution)/shard_map/ppermute | solution.py:310
  582.9 6.3 pad_maximum_fusion.3
  589.2 9.7 %shard_map.337 = f32[2,48,128,128]{3,2,1,0:T(8,128)} custom-call(f32[2,48,128,128]{3,2,1,0:T(8,128)} %bitcast.260, f32[256,256]{1,0:T(8,128)} %constant.124.clone.w_ref.v_ref, f32[256,256]{1,0:T(8,128)} %constant.125.clone.v_ref.w_ref, f32[2,128,128]{2,1,0:T(8,128)} %constant.126.clone.t_ref), custom_call_target="tpu_custom_call" | custom-call | flops 1610612736 | bytes 12582912 | tf_op jit(solution)/shard_map/pallas_call | solution.py:182
  598.9 4.5 fusion.26
  603.9 4.0 subtract_dynamic-update-slice_fusion.4
  613.6 4.2 broadcast_multiply_fusion.y_ref
  617.9 16.1 %shard_map.338 = f32[2,64,128,128]{3,2,1,0:T(8,128)} custom-call(f32[2,64,128,128]{3,2,1,0:T(8,128)} %broadcast_multiply_fusion.y_ref, f32[256,256]{1,0:T(8,128)} %constant.124.clone.w_ref.v_ref, f32[256,256]{1,0:T(8,128)} %constant.125.clone.v_ref.w_ref, f32[2,128,128]{2,1,0:T(8,128)} %constant.127.clone.t_ref), custom_call_target="tpu_custom_call" | custom-call | flops 2147483648 | bytes 16777216 | tf_op jit(solution)/shard_map/pallas_call | solution.py:182
  634.0 12.1 %multiply_reduce_fusion = f32[64,128,128]{2,1,0:T(8,128)} fusion(f32[2,64,128,128]{3,2,1,0:T(8,128)} %bitcast.235, f32[2,64,128,128]{3,2,1,0:T(8,128)} %fusion.3.x_ref, f32[2,64,128,128]{3,2,1,0:T(8,128)} %shard_map.338), kind=kLoop, calls=%fused_computation.8 | loop fusion | flops 7340032 | bytes 29360128 | tf_op jit(solution)/shard_map/reduce_sum | solution.py:382
  646.2 2.5 reduce_sum.47
  649.2 9.4 %reshape.240 = f32[2,8,8,16384]{3,2,1,0:T(8,128)} reshape(f32[2,64,128,128]{3,2,1,0:T(8,128)} %shard_map.338) | data formatting | bytes 16777216 | tf_op jit(solution)/shard_map/reshape | solution.py:381
  659.1 15.6 %add_multiply_fusion = f32[2,8,8,16384]{3,2,1,0:T(8,128)} fusion(f32[2,8,8,16384]{3,2,1,0:T(8,128)} %constant_dynamic-update-slice_fusion.8, f32[2,8,8,16384]{3,2,1,0:T(8,128)} %reshape.240, f32[2,8,8,16384]{3,2,1,0:T(8,128)} %add_multiply_fusion.1, f32[2,8,8,16384]{3,2,1,0:T(8,128)} %param.35, f32[8,16384]{1,0:T(8,128)S(1)} %bitcast.273), kind=kLoop, calls=%fused_computation.9 | loop fusion | flops 12582912 | bytes 42467328 | tf_op jit(solution)/shard_map/mul | solution.py:389
  (93 shorter events, 19.6 us)
Async XLA Ops:
  0.6 30.9 %copy-start = (f32[16,4]{0,1:T(4,128)S(1)}, f32[16,4]{0,1:T(4,128)}, u32[]{:S(2)}) copy-start(f32[16,4]{0,1:T(4,128)} %param.41) | copy-start | bytes 772
  0.6 5.8 copy-start.2
  11.3 11.9 %copy-start.10 = (s32[1024]{0:T(1024)S(1)}, s32[1024]{0:T(1024)}, u32[]{:S(2)}) copy-start(s32[1024]{0:T(1024)} %param.39) | copy-start | bytes 12292
  11.3 11.9 %copy-start.11 = (s32[1024]{0:T(1024)S(1)}, s32[1024]{0:T(1024)}, u32[]{:S(2)}) copy-start(s32[1024]{0:T(1024)} %param.40) | copy-start | bytes 12292
  11.3 20.7 %copy-start.12 = (f32[4]{0:T(128)S(1)}, f32[4]{0:T(128)}, u32[]{:S(2)}) copy-start(f32[4]{0:T(128)} %param.43) | copy-start | bytes 52
  11.3 20.7 %copy-start.13 = (s32[8]{0:T(128)S(1)}, s32[8]{0:T(128)}, u32[]{:S(2)}) copy-start(s32[8]{0:T(128)} %param.42) | copy-start | bytes 100
  11.3 20.8 %copy-start.9 = (f32[8,1024]{1,0:T(8,128)S(1)}, f32[8,1024]{1,0:T(8,128)}, u32[]{:S(2)}) copy-start(f32[8,1024]{1,0:T(8,128)} %param.38) | copy-start | bytes 98308
  17.0 141.8 %collective-permute-start = (f32[2,8,3,128,128]{4,3,2,1,0:T(8,128)}, f32[2,8,3,128,128]{4,3,2,1,0:T(8,128)}, u32[]{:S(2)}, u32[]{:S(2)}) collective-permute-start(f32[2,8,3,128,128]{4,3,2,1,0:T(8,128)} %get-tuple-element.21), channel_id=1, source_target_pairs={{0,2},{2,4},{4,6},{6,8},{8,10},{10,12},{12,14},{14,16},{16,18},{18... | collective-permute-start | bytes 9437192 | tf_op jit(solution)/shard_map/ppermute | solution.py:259
  20.1 138.7 %collective-permute-start.1 = (f32[2,8,3,128,128]{4,3,2,1,0:T(8,128)S(1)}, f32[2,8,3,128,128]{4,3,2,1,0:T(8,128)}, u32[]{:S(2)}, u32[]{:S(2)}) collective-permute-start(f32[2,8,3,128,128]{4,3,2,1,0:T(8,128)S(1)} %get-tuple-element.20), channel_id=1, source_target_pairs={{2,0},{4,2},{6,4},{8,6},{10,8},{12,10},{14,12},{16,14},{18,16},{20... | collective-permute-start | bytes 9437192 | tf_op jit(solution)/shard_map/ppermute | solution.py:260
  23.9 134.9 %all-to-all-start = ((s32[16,2,1024]{2,1,0:T(2,128)}), s32[16,2,1024]{2,1,0:T(2,128)S(1)}, u32[]{:S(2)}, u32[]{:S(2)}) async-start(s32[16,2,1024]{2,1,0:T(2,128)} %broadcast_in_dim.18), calls=%async_computation | async-start | bytes 262144 | tf_op jit(solution)/shard_map/all_to_all | solution.py:264
  169.5 98.1 %all-to-all-start.1 = ((f32[2,4,128,8,128]{4,3,1,0,2:T(8,128)}), f32[2,4,128,8,128]{4,3,1,0,2:T(8,128)}, u32[]{:S(2)}, u32[]{:S(2)}) async-start(f32[2,4,128,8,128]{4,3,1,0,2:T(8,128)} %copy.119), calls=%async_computation.1 | async-start | bytes 8388608 | tf_op jit(solution)/shard_map/all_to_all | solution.py:286
  272.4 97.9 %all-to-all-start.2 = ((f32[2,4,128,8,128]{4,3,1,0,2:T(8,128)}), f32[2,4,128,8,128]{4,3,1,0,2:T(8,128)}, u32[]{:S(2)}, u32[]{:S(2)}) async-start(f32[2,4,128,8,128]{4,3,1,0,2:T(8,128)} %copy.118), calls=%async_computation.2 | async-start | bytes 8388608 | tf_op jit(solution)/shard_map/all_to_all | solution.py:286
  296.5 5.0 copy-start.7
  296.5 9.0 %slice-start = ((s8[8388608]{0:T(1024)(128)(4,1)}), s8[4194304]{0:T(1024)(128)(4,1)S(1)}, s32[]{:S(2)}) async-start(s8[8388608]{0:T(1024)(128)(4,1)} %bitcast.211), calls=%async_computation.3 | async-start | bytes 8388608
  301.4 4.2 slice-start.1
  398.5 12.5 %copy-start.3 = (f32[2,8,8,128,128]{4,3,2,1,0:T(8,128)}, f32[2,8,8,128,128]{4,3,2,1,0:T(8,128)S(1)}, u32[]{:S(2)}) copy-start(f32[2,8,8,128,128]{4,3,2,1,0:T(8,128)S(1)} %pad_maximum_fusion.1) | copy-start | bytes 25165828
  413.5 6.8 %copy-start.8 = (f32[8,128,128]{2,1,0:T(8,128)}, f32[8,128,128]{2,1,0:T(8,128)S(1)}, u32[]{:S(2)}) copy-start(f32[8,128,128]{2,1,0:T(8,128)S(1)} %reduce_sum.44) | copy-start | bytes 1572868
  413.5 8.1 %copy-start.4 = (f32[2,32,128,128]{3,2,1,0:T(8,128)S(1)}, f32[2,32,128,128]{3,2,1,0:T(8,128)}, u32[]{:S(2)}) copy-start(f32[2,32,128,128]{3,2,1,0:T(8,128)} %shard_map.333) | copy-start | bytes 12582916
  413.5 8.1 %copy-start.5 = (f32[2,32,128,128]{3,2,1,0:T(8,128)S(1)}, f32[2,32,128,128]{3,2,1,0:T(8,128)}, u32[]{:S(2)}) copy-start(f32[2,32,128,128]{3,2,1,0:T(8,128)} %shard_map.335) | copy-start | bytes 12582916
  413.5 6.8 %collective-permute-start.2 = (f32[8,128,128]{2,1,0:T(8,128)S(1)}, f32[8,128,128]{2,1,0:T(8,128)S(1)}, u32[]{:S(2)}, u32[]{:S(2)}) collective-permute-start(f32[8,128,128]{2,1,0:T(8,128)S(1)} %reduce_sum.44), channel_id=1, source_target_pairs={{0,1},{1,0},{2,3},{3,2},{4,5},{5,4},{6,7},{7,6},{8,9},{9,8},{10,11... | collective-permute-start | bytes 1572872 | tf_op jit(solution)/shard_map/ppermute | solution.py:384
  441.6 72.6 %collective-permute-start.3 = (f32[2,8,3,128,128]{4,3,2,1,0:T(8,128)}, f32[2,8,3,128,128]{4,3,2,1,0:T(8,128)}, u32[]{:S(2)}, u32[]{:S(2)}) collective-permute-start(f32[2,8,3,128,128]{4,3,2,1,0:T(8,128)} %get-tuple-element.25), channel_id=1, source_target_pairs={{0,2},{2,4},{4,6},{6,8},{8,10},{10,12},{12,14},{14,16},{16,18},{18... | collective-permute-start | bytes 9437192 | tf_op jit(solution)/shard_map/ppermute | solution.py:309
  443.5 139.4 %collective-permute-start.4 = (f32[2,8,3,128,128]{4,3,2,1,0:T(8,128)}, f32[2,8,3,128,128]{4,3,2,1,0:T(8,128)}, u32[]{:S(2)}, u32[]{:S(2)}) collective-permute-start(f32[2,8,3,128,128]{4,3,2,1,0:T(8,128)} %get-tuple-element.24), channel_id=1, source_target_pairs={{2,0},{4,2},{6,4},{8,6},{10,8},{12,10},{14,12},{16,14},{18,16},{20... | collective-permute-start | bytes 9437192 | tf_op jit(solution)/shard_map/ppermute | solution.py:310
  598.9 5.0 copy-start.6
  598.9 9.0 %slice-start.2 = ((s8[8388608]{0:T(1024)(128)(4,1)}), s8[4194304]{0:T(1024)(128)(4,1)S(1)}, s32[]{:S(2)}) async-start(s8[8388608]{0:T(1024)(128)(4,1)} %bitcast.221), calls=%async_computation.5 | async-start | bytes 8388608
  603.9 4.2 slice-start.3
  648.6 9.9 %collective-permute-start.5 = (f32[8,128,128]{2,1,0:T(8,128)S(1)}, f32[8,128,128]{2,1,0:T(8,128)S(1)}, u32[]{:S(2)}, u32[]{:S(2)}) collective-permute-start(f32[8,128,128]{2,1,0:T(8,128)S(1)} %reduce_sum.47), channel_id=1, source_target_pairs={{0,1},{1,0},{2,3},{3,2},{4,5},{5,4},{6,7},{7,6},{8,9},{9,8},{10,11... | collective-permute-start | bytes 1572872 | tf_op jit(solution)/shard_map/ppermute | solution.py:384
  659.1 15.6 %copy-start.1 = (f32[16,4]{0,1:T(4,128)S(1)}, f32[16,4]{0,1:T(4,128)}, u32[]{:S(2)}) copy-start(f32[16,4]{0,1:T(4,128)} %param.41) | copy-start | bytes 772
